TPU v7x, 1024 devices: a whole 8x8x8 slice. The times are simulated.
1024 devices in a mesh: section: 64 (over x_hi, z, core), tp: 8 (over y), mirror: 2 (over x_lo).
Axes of the slice: x: 8 (x_hi: 4, x_lo: 2; x = x_hi * 2 + x_lo), y: 8, z: 8, core: 2. Of those that a mesh axis runs over, the one named last changes fastest.
Arguments:
- hidden: bfloat16 [2, 64, 2, 128, 14336], P(None, 'section', 'mirror', None, 'tp'), may hold values from -6 to 6
- incoming: bfloat16 [2, 64, 2, 128, 4096], P(None, 'section', 'mirror', None, 'tp'), may hold values from -0.3984375 to 0.3984375
- block_mask: int32 [32, 112, 32], P(None, 'tp'), may hold values from 0 to 1, as said below
Outputs:
- block_grads: bfloat16 [64, 8, 126, 128, 128], P('section', 'tp', 'mirror')
Inputs may be any that keep to these rules, and one draw needn't show every extreme that they name: `block_mask`: for every section and every index of tp, its 14 block rows keep between 7/16 and 9/16 of their blocks, at most 252; in every section exactly 252 on some index of tp.
All inputs are finite; a program needn't handle non-finite values.
Results may differ from a plain program's by a relative error of at most 0.006.
Values may be sent and summed in bfloat16 or wider, within the bound.
No kernel may reach another device: no remote copies, remote signals or barrier semaphores. Data moves between devices by JAX's collectives and lax.ppermute only.
A program may use at most 64 MiB of HBM per device.

v0:
```python
import jax
import jax.numpy as jnp
from jax import lax
from jax.sharding import PartitionSpec as P

BLK = 128


def passed_along(block, axis, distance):
    devices = range(lax.axis_size(axis))
    route = [((i - distance) % len(devices), i) for i in devices]
    return lax.ppermute(block, axis, route)


def from_partner(value, axis, apart):
    mask = 2**apart
    pairs = [(source, source ^ mask) for source in range(lax.axis_size(axis))]
    return lax.ppermute(value, axis, pairs)


def group_of(slot_total):
    for size in range(min(slot_total, 28), 0, -1):
        return size
    return 1


def slot_table(mask_local, slot_total):
    flat = mask_local.reshape(-1)
    running = jnp.cumsum(flat)
    positions = jnp.arange(slot_total, dtype=jnp.int32)
    targets = jnp.sum((running[None, :] <= positions[:, None]).astype(jnp.int32), axis=1)
    usable = positions < running[-1]
    targets = jnp.minimum(targets, flat.shape[0] - 1)
    columns_count = mask_local.shape[1]
    return (targets // columns_count, targets % columns_count, usable)


def block_partials(hidden_rows, cotangent, block_rows, block_cols, usable, block_side):
    row_total = hidden_rows.shape[0]
    hidden_blocks = hidden_rows.reshape(row_total, -1, block_side)
    cot_blocks = cotangent.reshape(row_total, -1, block_side)
    slot_total = block_rows.shape[0]
    group_size = group_of(slot_total)

    def one_group(pieces):
        rows_piece, cols_piece, usable_piece = pieces
        left = jnp.take(hidden_blocks, rows_piece, axis=1)
        right = jnp.take(cot_blocks, cols_piece, axis=1)
        product = jnp.einsum("nkc,nkd->kcd", left, right, preferred_element_type=jnp.float32)
        product = jnp.where(usable_piece[:, None, None], product, 0.0)
        return product.astype(jnp.bfloat16)

    grouped = lax.map(
        one_group,
        (
            block_rows.reshape(-1, group_size),
            block_cols.reshape(-1, group_size),
            usable.reshape(-1, group_size),
        ),
    )
    return grouped.reshape(slot_total, block_side, block_side)


def body(hidden, incoming, block_mask):
    sections_total = lax.axis_size("section")
    half_count = sections_total // 2
    position = lax.axis_index("section")
    half_index = position // half_count
    section_index = position % half_count
    swap_bit = sections_total.bit_length() - 2
    block_side = BLK
    row_count = hidden.shape[3]
    down_part = passed_along(incoming[0, 0, 0], "section", -1)
    up_part = passed_along(incoming[1, 0, 0], "section", 1)
    arrived = jnp.stack([down_part, up_part])
    gathered = lax.all_gather(arrived, "tp", axis=2, tiled=True)
    cotangent = gathered.reshape(2 * row_count, gathered.shape[2])
    hidden_rows = hidden[:, 0, 0].reshape(2 * row_count, hidden.shape[4])
    mask_local = lax.dynamic_index_in_dim(block_mask, section_index, 0, keepdims=False)
    slot_total = mask_local.shape[0] * mask_local.shape[1] * 9 // 16
    slots_half = slot_total // 2
    block_rows, block_cols, usable = slot_table(mask_local, slot_total)
    partial_all = block_partials(hidden_rows, cotangent, block_rows, block_cols, usable, block_side)
    own_part = lax.dynamic_slice_in_dim(partial_all, half_index * slots_half, slots_half, 0)
    outgoing = lax.dynamic_slice_in_dim(partial_all, (1 - half_index) * slots_half, slots_half, 0)
    partner_part = from_partner(outgoing, "section", swap_bit)
    paired = (own_part.astype(jnp.float32) + partner_part.astype(jnp.float32)).astype(jnp.bfloat16)
    summed = lax.psum_scatter(
        paired.astype(jnp.float32).astype(jnp.bfloat16), "mirror", scatter_dimension=0, tiled=True
    )
    return summed.reshape(1, 1, -1, block_side, block_side)


def solution(mesh):
    placed = (
        P(None, "section", "mirror", None, "tp"),
        P(None, "section", "mirror", None, "tp"),
        P(None, "tp", None),
    )
    return jax.shard_map(
        body,
        mesh=mesh,
        in_specs=placed,
        out_specs=P("section", "tp", "mirror", None, None),
        check_vma=False,
    )
```

profile of v0, /device:TPU:1, one launch (start us, length us, event | category | flops | bytes accessed | tf_op | source)
XLA Modules:
  0.0 423.5 jit_solution(1043263820101527273)
XLA Ops:
  6.5 0.0 copy-start
  6.5 0.0 all-gather.2.cloned.1.call-start
  6.5 1.0 slice_bitcast_fusion.1
  7.6 16.1 %collective-permute-start = (bf16[128,512]{1,0:T(8,128)(2,1)S(1)}, bf16[128,512]{1,0:T(8,128)(2,1)S(1)}, u32[]{:S(2)}, u32[]{:S(2)}) collective-permute-start(bf16[128,512]{1,0:T(8,128)(2,1)S(1)} %get-tuple-element.82), channel_id=1, source_target_pairs={{16,0},{32,16},{48,32},{64,48},{80,64},{96,80},{112,96},{128,112},... | collective-permute-start | bytes 393224 | tf_op jit(solution)/shard_map/ppermute | solution.py:12
  23.6 1.9 collective-permute-start.1
  25.6 0.0 collective-permute-done
  25.6 6.2 %collective-permute-done.1 = bf16[128,512]{1,0:T(8,128)(2,1)S(1)} collective-permute-done((bf16[128,512]{1,0:T(8,128)(2,1)S(1)}, bf16[128,512]{1,0:T(8,128)(2,1)S(1)}, u32[]{:S(2)}, u32[]{:S(2)}) %collective-permute-start.1) | collective-permute-done | bytes 131104 | tf_op jit(solution)/shard_map/ppermute | solution.py:12
  31.8 0.7 pad_maximum_fusion
  32.5 0.0 all-gather.2.cloned.1.call-update
  32.5 0.0 reduce-scatter.2.cloned.1.call-start
  32.6 0.0 copy-done
  32.7 0.1 reshape.103
  32.8 0.3 reduce-window.9
  33.1 0.1 slice.20
  33.2 0.1 slice_reduce_fusion
  33.3 0.1 add_bitcast_fusion
  33.4 0.6 slice.22
  33.9 0.1 convert_reduce_fusion
  34.1 0.1 min.13
  34.2 1.8 reshape.124
  36.0 0.2 copy.15
  36.2 0.6 add_compare_fusion
  36.8 40.2 %all-gather.2.cloned.1.call-done = bf16[2,128,4096]{2,1,0:T(8,128)(2,1)} async-done(((bf16[2,128,512]{2,1,0:T(8,128)(2,1)}), bf16[2,128,4096]{2,1,0:T(8,128)(2,1)}) %all-gather.2.cloned.1.call-update) | async-done | bytes 2097168 | tf_op jit(solution)/shard_map/all_gather | solution.py:76
  77.1 2.1 copy.20
  79.1 0.8 copy.16
  80.0 73.2 %while.10 = (s32[]{:T(128)}, bf16[9,28,128,128]{3,2,1,0:T(8,128)(2,1)}, pred[9,28]{1,0:T(8,128)(4,1)S(1)}, s32[9,28]{1,0:T(8,128)S(1)}, bf16[256,14,128]{2,0,1:T...) while((s32[]{:T(128)}, bf16[9,28,128,128]{3,2,1,0:T(8,128)(2,1)}, ...), condition=%wide.region_4.5_spmd, body=%wide.region_3.4_spmd.sunk | while | flops 237636096 | bytes 11937169 | solution.py:53
  80.1 2.1 gather_fusion.1
  82.2 2.0 gather_fusion
  84.2 3.9 fusion.34
  88.2 2.1 gather_fusion.1
  90.3 2.0 gather_fusion
  92.3 3.9 fusion.34
  96.4 2.1 gather_fusion.1
  98.5 2.0 gather_fusion
  100.5 3.9 fusion.34
  104.5 2.1 gather_fusion.1
  106.6 2.0 gather_fusion
  108.6 3.9 fusion.34
  112.6 2.1 gather_fusion.1
  114.7 2.0 gather_fusion
  116.8 3.9 fusion.34
  120.7 2.1 gather_fusion.1
  122.8 2.0 gather_fusion
  124.9 3.9 fusion.34
  128.9 2.1 gather_fusion.1
  131.0 2.0 gather_fusion
  133.0 3.9 fusion.34
  137.0 2.1 gather_fusion.1
  139.1 2.0 gather_fusion
  141.2 3.9 fusion.34
  145.2 2.1 gather_fusion.1
  147.3 2.0 gather_fusion
  149.3 3.9 fusion.34
  153.2 4.7 %constant_dynamic-slice_fusion.2 = bf16[126,128,128]{2,1,0:T(8,128)(2,1)} fusion(bf16[252,128,128]{2,1,0:T(8,128)(2,1)} %bitcast.70, s32[]{:T(128)S(6)} %select_n.83), kind=kLoop, calls=%fused_computation.46 | loop fusion | bytes 8257540 | tf_op jit(solution)/shard_map/dynamic_slice | solution.py:85
  157.9 7.0 %collective-permute-start.2 = (bf16[126,128,128]{2,1,0:T(8,128)(2,1)}, bf16[126,128,128]{2,1,0:T(8,128)(2,1)}, u32[]{:S(2)}, u32[]{:S(2)}) collective-permute-start(bf16[126,128,128]{2,1,0:T(8,128)(2,1)} %constant_dynamic-slice_fusion.2), channel_id=1, source_target_pairs={{0,512},{16,528},{32,544},{48,560},{64,576},{80,592},{96,608},{112... | collective-permute-start | bytes 12386312 | tf_op jit(solution)/shard_map/ppermute | solution.py:18
  164.9 176.9 %collective-permute-done.2 = bf16[126,128,128]{2,1,0:T(8,128)(2,1)} collective-permute-done((bf16[126,128,128]{2,1,0:T(8,128)(2,1)}, bf16[126,128,128]{2,1,0:T(8,128)(2,1)}, u32[]{:S(2)}, u32[]{:S(2)}) %collective-permute-start.2) | collective-permute-done | bytes 4128800 | tf_op jit(solution)/shard_map/ppermute | solution.py:18
  341.8 8.0 %add_convert_fusion = bf16[126,128,128]{2,1,0:T(8,128)(2,1)} fusion(bf16[126,128,128]{2,1,0:T(8,128)(2,1)} %collective-permute-done.2, bf16[252,128,128]{2,1,0:T(8,128)(2,1)} %bitcast.71, s32[]{:T(128)S(6)} %select_n.82), kind=kLoop, calls=%fused_computation.27 | loop fusion | flops 8257536 | bytes 12386308 | tf_op jit(solution)/shard_map/convert_element_type | solution.py:87
  349.8 0.0 reduce-scatter.2.cloned.1.call-update
  349.8 66.9 %reduce-scatter.2.cloned.1.call-done = bf16[63,128,128]{2,1,0:T(8,128)(2,1)} async-done(((bf16[126,128,128]{2,1,0:T(8,128)(2,1)}), bf16[63,128,128]{2,1,0:T(8,128)(2,1)}) %reduce-scatter.2.cloned.1.call-update) | async-done | bytes 2064400 | tf_op jit(solution)/shard_map/reduce_scatter | solution.py:88
  (51 shorter events, 0.5 us)
Async XLA Ops:
  6.5 26.1 %copy-start = (s32[32,14,32]{2,0,1:T(8,128)S(1)}, s32[32,14,32]{2,0,1:T(8,128)}, u32[]{:S(2)}) copy-start(s32[32,14,32]{2,0,1:T(8,128)} %param.7) | copy-start | bytes 172036
  6.5 70.5 %all-gather.2.cloned.1.call-start = ((), (), s32[]{:S(2)}) async-start(), calls=%async_computation.1 | async-start | bytes 2359296 | tf_op jit(solution)/shard_map/all_gather | solution.py:76
  7.6 18.0 %collective-permute-start = (bf16[128,512]{1,0:T(8,128)(2,1)S(1)}, bf16[128,512]{1,0:T(8,128)(2,1)S(1)}, u32[]{:S(2)}, u32[]{:S(2)}) collective-permute-start(bf16[128,512]{1,0:T(8,128)(2,1)S(1)} %get-tuple-element.82), channel_id=1, source_target_pairs={{16,0},{32,16},{48,32},{64,48},{80,64},{96,80},{112,96},{128,112},... | collective-permute-start | bytes 393224 | tf_op jit(solution)/shard_map/ppermute | solution.py:12
  23.6 8.1 %collective-permute-start.1 = (bf16[128,512]{1,0:T(8,128)(2,1)S(1)}, bf16[128,512]{1,0:T(8,128)(2,1)S(1)}, u32[]{:S(2)}, u32[]{:S(2)}) collective-permute-start(bf16[128,512]{1,0:T(8,128)(2,1)S(1)} %get-tuple-element.83), channel_id=1, source_target_pairs={{1008,0},{0,16},{16,32},{32,48},{48,64},{64,80},{80,96},{96,112},{... | collective-permute-start | bytes 393224 | tf_op jit(solution)/shard_map/ppermute | solution.py:12
  32.5 384.2 %reduce-scatter.2.cloned.1.call-start = ((), (), s32[]{:S(2)}) async-start(), calls=%async_computation.2 | async-start | bytes 6193152 | tf_op jit(solution)/shard_map/reduce_scatter | solution.py:88
  157.9 184.0 %collective-permute-start.2 = (bf16[126,128,128]{2,1,0:T(8,128)(2,1)}, bf16[126,128,128]{2,1,0:T(8,128)(2,1)}, u32[]{:S(2)}, u32[]{:S(2)}) collective-permute-start(bf16[126,128,128]{2,1,0:T(8,128)(2,1)} %constant_dynamic-slice_fusion.2), channel_id=1, source_target_pairs={{0,512},{16,528},{32,544},{48,560},{64,576},{80,592},{96,608},{112... | collective-permute-start | bytes 12386312 | tf_op jit(solution)/shard_map/ppermute | solution.py:18
Sparse Core Ops, SparseCore 0:
  32.6 44.3 all-gather.1
  350.0 66.7 reduce-scatter.1
where the time goes:
time: 424 us
  waiting for transfers between devices  290 us (68%)
  local copies, waits for them, and re-layouts  49.1 us (12%)
  matrix products  35.1 us (8%)
  starting transfers between devices  25 us (6%)
  between operations  13.6 us (3%)
  other arithmetic  10.2 us (2%)
    ppermute x1, waiting for transfers between devices, from_partner(): return lax.ppermute(value, axis, pairs)  177 us
    reduce_scatter x1, waiting for transfers between devices, body(): lax.psum_scatter(paired.astype(jnp.float32).astype(jnp.bfloat16), 'mirror...  66.9 us
    all_gather x1, waiting for transfers between devices, body(): gathered = lax.all_gather(arrived, 'tp', axis=2, tiled=True)  40.2 us
    dot_general x9, matrix products, one_group(): jnp.einsum('nkc,nkd->kcd', left, right, preferred_element_type=jnp.float32)  35.1 us
    gather x9, local copies, waits for them, and re-layouts, one_group(): left = jnp.take(hidden_blocks, rows_piece, axis=1)  19.1 us
    gather x9, local copies, waits for them, and re-layouts, one_group(): right = jnp.take(cot_blocks, cols_piece, axis=1)  18.3 us
    ppermute x2, starting transfers between devices, passed_along(): return lax.ppermute(block, axis, route)  18 us
  transfers between devices with their start and end apart: 5, of which 4 were waited for; matrix products, arithmetic and copies ran while one was open for 1% of the time, Pallas kernels for 0%

commit v1 on v0

v1 whole, which is shorter than its diff:
```python
import jax
import jax.numpy as jnp
from jax import lax
from jax.sharding import PartitionSpec as P

BLK = 128


def passed_along(block, axis, distance):
    devices = range(lax.axis_size(axis))
    route = [((i - distance) % len(devices), i) for i in devices]
    return lax.ppermute(block, axis, route)


def from_partner(value, axis, apart):
    mask = 2**apart
    pairs = [(source, source ^ mask) for source in range(lax.axis_size(axis))]
    return lax.ppermute(value, axis, pairs)


def slot_table(mask_local, slot_total):
    flat = mask_local.reshape(-1)
    running = jnp.cumsum(flat)
    positions = jnp.arange(slot_total, dtype=jnp.int32)
    targets = jnp.sum((running[None, :] <= positions[:, None]).astype(jnp.int32), axis=1)
    usable = positions < running[-1]
    targets = jnp.minimum(targets, flat.shape[0] - 1)
    columns_count = mask_local.shape[1]
    return (targets // columns_count, targets % columns_count, usable)


def body(hidden, incoming, block_mask):
    sections_total = lax.axis_size("section")
    half_count = sections_total // 2
    position = lax.axis_index("section")
    half_index = position // half_count
    section_index = position % half_count
    swap_bit = sections_total.bit_length() - 2
    block_side = BLK
    row_count = hidden.shape[3]
    ff_local = hidden.shape[4]

    own_hidden = hidden[:, 0, 0].reshape(2 * row_count, ff_local)
    partner_hidden = from_partner(own_hidden, "section", swap_bit)
    down_part = passed_along(incoming[0, 0, 0], "section", -1)
    up_part = passed_along(incoming[1, 0, 0], "section", 1)
    own_arrived = jnp.stack([down_part, up_part])
    partner_arrived = from_partner(own_arrived, "section", swap_bit)
    own_cot = lax.all_gather(own_arrived, "tp", axis=2, tiled=True)
    partner_cot = lax.all_gather(partner_arrived, "tp", axis=2, tiled=True)
    d_total = own_cot.shape[2]
    cot = jnp.concatenate(
        [own_cot.reshape(2 * row_count, d_total), partner_cot.reshape(2 * row_count, d_total)], axis=0
    )
    hidden_rows = jnp.concatenate([own_hidden, partner_hidden], axis=0)

    ffb = ff_local // block_side
    db = d_total // block_side
    dense = jnp.einsum(
        "nic,njd->ijcd",
        hidden_rows.reshape(-1, ffb, block_side),
        cot.reshape(-1, db, block_side),
        preferred_element_type=jnp.float32,
    ).astype(jnp.bfloat16)

    mask_local = lax.dynamic_index_in_dim(block_mask, section_index, 0, keepdims=False)
    slot_total = mask_local.shape[0] * mask_local.shape[1] * 9 // 16
    slots_half = slot_total // 2
    block_rows, block_cols, usable = slot_table(mask_local, slot_total)
    rows_h = lax.dynamic_slice_in_dim(block_rows, half_index * slots_half, slots_half, 0)
    cols_h = lax.dynamic_slice_in_dim(block_cols, half_index * slots_half, slots_half, 0)
    usable_h = lax.dynamic_slice_in_dim(usable, half_index * slots_half, slots_half, 0)
    flat_index = rows_h * db + cols_h
    picked = jnp.take(dense.reshape(ffb * db, block_side, block_side), flat_index, axis=0)
    paired = jnp.where(usable_h[:, None, None], picked, jnp.zeros_like(picked))
    summed = lax.psum_scatter(paired, "mirror", scatter_dimension=0, tiled=True)
    return summed.reshape(1, 1, -1, block_side, block_side)


def solution(mesh):
    placed = (
        P(None, "section", "mirror", None, "tp"),
        P(None, "section", "mirror", None, "tp"),
        P(None, "tp", None),
    )
    return jax.shard_map(
        body,
        mesh=mesh,
        in_specs=placed,
        out_specs=P("section", "tp", "mirror", None, None),
        check_vma=False,
    )
```

time: 424 us -> 251 us (0.59)
  waiting for transfers between devices: 290 us -> 149 us
  matrix products: 35.1 us -> 12.8 us
    ppermute x1 -> x2, waiting for transfers between devices: 177 us -> 32.2 us  [from_partner(): return lax.ppermute(value, axis, pairs)]
    gather x18 -> x1, local copies, waits for them, and re-layouts: 37.4 us -> 8.16 us  [body(): jnp.take(dense.reshape(ffb * db, block_side, block_side), flat_index, axi...]
    dot_general x9 -> x1, matrix products: 35.1 us -> 12.8 us  [body(): jnp.einsum('nic,njd->ijcd', hidden_rows.reshape(-1, ffb, block_side), cot...]
    convert_element_type x0 -> x1, local copies, waits for them, and re-layouts: none -> 20.2 us  [body(): dense = jnp.einsum('nic,njd->ijcd', hidden_rows.reshape(-1, ffb, block_si...]
    concatenate x0 -> x5, local copies, waits for them, and re-layouts: none -> 8.66 us  [the longest x2 5.53 us: body(): jnp.concatenate([own_cot.reshape(2 * row_count, d_total), partner_cot.res...]
    convert_element_type x1 -> x0, other arithmetic: 7.98 us -> none  [body(): (own_part.astype(jnp.float32) + partner_part.astype(jnp.float32)).astype(...]
    all_gather x1 -> x2, waiting for transfers between devices: 40.2 us -> 48.1 us  [the longest x1 43.8 us: body(): partner_cot = lax.all_gather(partner_arrived, 'tp', axis=2, tiled=True)]
    ppermute x2, waiting for transfers between devices: 6.18 us -> 0.96 us  [passed_along(): return lax.ppermute(block, axis, route)]
  transfers between devices with their start and end apart: 5 -> 7, of which waited for: 4 -> 6; matrix products, arithmetic and copies ran while one was open for 1% -> 5% of each run, Pallas kernels for 0% -> 0%
where the time goes in v1:
time: 251 us
  waiting for transfers between devices  149 us (59%)
  local copies, waits for them, and re-layouts  46.2 us (18%)
  starting transfers between devices  23.5 us (9%)
  between operations  13.2 us (5%)
  matrix products  12.8 us (5%)
  other arithmetic  5.99 us (2%)
    reduce_scatter x1, waiting for transfers between devices, body(): summed = lax.psum_scatter(paired, 'mirror', scatter_dimension=0, tiled=True)  67.5 us
    all_gather x1, waiting for transfers between devices, body(): partner_cot = lax.all_gather(partner_arrived, 'tp', axis=2, tiled=True)  43.8 us
    ppermute x2, waiting for transfers between devices, from_partner(): return lax.ppermute(value, axis, pairs)  32.2 us
    convert_element_type x1, local copies, waits for them, and re-layouts, body(): dense = jnp.einsum('nic,njd->ijcd', hidden_rows.reshape(-1, ffb, block_si...  20.2 us
    ppermute x2, starting transfers between devices, passed_along(): return lax.ppermute(block, axis, route)  18 us
    dot_general x1, matrix products, body(): jnp.einsum('nic,njd->ijcd', hidden_rows.reshape(-1, ffb, block_side), cot...  12.8 us
    gather x1, local copies, waits for them, and re-layouts, body(): jnp.take(dense.reshape(ffb * db, block_side, block_side), flat_index, axi...  8.16 us
    concatenate x2, local copies, waits for them, and re-layouts, body(): jnp.concatenate([own_cot.reshape(2 * row_count, d_total), partner_cot.res...  5.53 us
  transfers between devices with their start and end apart: 7, of which 6 were waited for; matrix products, arithmetic and copies ran while one was open for 5% of the time, Pallas kernels for 0%

profile of v1, /device:TPU:1, one launch (start us, length us, event | category | flops | bytes accessed | tf_op | source)
XLA Modules:
  0.0 250.6 jit_solution(13795904634986436157)
XLA Ops:
  6.5 0.0 copy-start
  6.5 0.0 copy-start.1
  6.5 0.0 all-gather.3.cloned.1.call-start
  6.5 1.1 slice_bitcast_fusion.1
  7.6 6.3 %collective-permute-start.1 = (bf16[128,512]{1,0:T(8,128)(2,1)S(1)}, bf16[128,512]{1,0:T(8,128)(2,1)S(1)}, u32[]{:S(2)}, u32[]{:S(2)}) collective-permute-start(bf16[128,512]{1,0:T(8,128)(2,1)S(1)} %get-tuple-element.8), channel_id=1, source_target_pairs={{1008,0},{0,16},{16,32},{32,48},{48,64},{64,80},{80,96},{96,112},{... | collective-permute-start | bytes 393224 | tf_op jit(solution)/shard_map/ppermute | solution.py:12
  13.9 11.7 %collective-permute-start = (bf16[128,512]{1,0:T(8,128)(2,1)S(1)}, bf16[128,512]{1,0:T(8,128)(2,1)S(1)}, u32[]{:S(2)}, u32[]{:S(2)}) collective-permute-start(bf16[128,512]{1,0:T(8,128)(2,1)S(1)} %get-tuple-element.7), channel_id=1, source_target_pairs={{16,0},{32,16},{48,32},{64,48},{80,64},{96,80},{112,96},{128,112},... | collective-permute-start | bytes 393224 | tf_op jit(solution)/shard_map/ppermute | solution.py:12
  25.6 0.0 collective-permute-done.1
  25.6 1.0 collective-permute-done
  26.6 0.7 pad_maximum_fusion
  27.3 0.0 all-gather.3.cloned.1.call-update
  27.3 0.0 all-gather.5.cloned.1.call-start
  27.4 1.9 collective-permute-start.2
  29.3 9.3 %collective-permute-done.2 = bf16[2,128,512]{2,1,0:T(8,128)(2,1)S(1)} collective-permute-done((bf16[2,128,512]{2,1,0:T(8,128)(2,1)}, bf16[2,128,512]{2,1,0:T(8,128)(2,1)S(1)}, u32[]{:S(2)}, u32[]{:S(2)}) %collective-permute-start.2) | collective-permute-done | bytes 262176 | tf_op jit(solution)/shard_map/ppermute | solution.py:18
  38.6 0.0 copy-start.3
  38.6 0.7 copy-done.3
  39.3 0.0 all-gather.5.cloned.1.call-update
  39.3 0.0 reduce-scatter.2.cloned.1.call-start
  39.4 2.2 copy.25
  41.6 3.5 %collective-permute-start.3 = (bf16[256,1792]{0,1:T(8,128)(2,1)}, bf16[256,1792]{0,1:T(8,128)(2,1)S(1)}, u32[]{:S(2)}, u32[]{:S(2)}) collective-permute-start(bf16[256,1792]{0,1:T(8,128)(2,1)} %copy.25), channel_id=1, source_target_pairs={{0,512},{16,528},{32,544},{48,560},{64,576},{80,592},{96,608},{112... | collective-permute-start | bytes 2752520 | tf_op jit(solution)/shard_map/ppermute | solution.py:18
  45.1 0.0 copy-done
  45.2 0.1 reshape.42
  45.3 0.3 reduce-window.9
  45.6 0.1 slice.20
  45.7 0.1 slice_reduce_fusion
  45.8 0.0 copy-done.1
  45.8 0.7 reshape.60
  46.5 1.2 copy.17
  47.7 0.1 add_bitcast_fusion
  47.7 0.6 slice.22
  48.4 0.6 iota_compare_fusion.1
  49.0 0.1 dynamic_slice.14
  49.1 0.1 convert_reduce_fusion
  49.3 0.1 compare_and_fusion
  49.4 22.9 %collective-permute-done.3 = bf16[256,1792]{0,1:T(8,128)(2,1)S(1)} collective-permute-done((bf16[256,1792]{0,1:T(8,128)(2,1)}, bf16[256,1792]{0,1:T(8,128)(2,1)S(1)}, u32[]{:S(2)}, u32[]{:S(2)}) %collective-permute-start.3) | collective-permute-done | bytes 917536 | tf_op jit(solution)/shard_map/ppermute | solution.py:18
  72.3 1.3 copy.18
  73.5 4.3 %all-gather.3.cloned.1.call-done = bf16[2,128,4096]{2,1,0:T(8,128)(2,1)} async-done(((bf16[2,128,512]{2,1,0:T(8,128)(2,1)}), bf16[2,128,4096]{2,1,0:T(8,128)(2,1)}) %all-gather.3.cloned.1.call-update) | async-done | bytes 2097168 | tf_op jit(solution)/shard_map/all_gather | solution.py:49
  77.8 2.1 copy.26
  79.9 2.8 %copy.21 = bf16[256,32,128]{0,2,1:T(8,128)(2,1)} copy(bf16[256,32,128]{2,1,0:T(8,128)(2,1)S(1)} %bitcast.35) | data formatting | bytes 4194304 | tf_op jit(solution)/shard_map/concatenate | solution.py:52
  82.7 43.8 %all-gather.5.cloned.1.call-done = bf16[2,128,4096]{2,1,0:T(8,128)(2,1)} async-done(((bf16[2,128,512]{2,1,0:T(8,128)(2,1)}), bf16[2,128,4096]{2,1,0:T(8,128)(2,1)}) %all-gather.5.cloned.1.call-update) | async-done | bytes 2097168 | tf_op jit(solution)/shard_map/all_gather | solution.py:50
  126.5 0.0 copy-start.2
  126.5 2.1 copy.27
  128.6 2.7 %copy.22 = bf16[256,32,128]{0,2,1:T(8,128)(2,1)} copy(bf16[256,32,128]{2,1,0:T(8,128)(2,1)S(1)} %bitcast.36) | data formatting | bytes 4194304 | tf_op jit(solution)/shard_map/concatenate | solution.py:52
  131.4 0.0 copy-done.2
  131.4 12.8 %convert_bitcast_fusion = bf16[14,32,128,128]{2,3,0,1:T(8,128)(2,1)} fusion(bf16[256,32,128]{0,2,1:T(8,128)(2,1)} %copy.22, bf16[256,32,128]{0,2,1:T(8,128)(2,1)} %copy.21, bf16[256,14,128]{2,0,1:T(8,128)(2,1)S(1)} %copy-done.2, bf16[256,14,128]{2,0,1:T(8,128)(2,1)} %copy.17), kind=kOutput, calls=%fused_computation.1 | convolution fusion | flops 7535591424 | bytes 20709376 | tf_op jit(solution)/shard_map/nic,njd->ijcd/dot_general | solution.py:59
  144.2 20.2 %copy.19 = bf16[14,32,128,128]{3,2,1,0:T(8,128)(2,1)} copy(bf16[14,32,128,128]{2,3,0,1:T(8,128)(2,1)} %convert_bitcast_fusion) | data formatting | bytes 29360128 | tf_op jit(solution)/shard_map/convert_element_type | solution.py:64
  164.4 8.2 %gather_fusion = bf16[126,128,128]{2,1,0:T(8,128)(2,1)} fusion(bf16[448,128,128]{2,1,0:T(8,128)(2,1)} %bitcast.34, s32[1024]{0:T(1024)S(1)} %pad_clamp_fusion), kind=kCustom, calls=%fused_computation | custom fusion | bytes 8258040 | tf_op jit(solution)/shard_map/jit(_take)/gather | solution.py:74
  172.5 4.0 %select_select_fusion = bf16[126,128,128]{2,1,0:T(8,128)(2,1)} fusion(bf16[126,128,128]{2,1,0:T(8,128)(2,1)} %gather_fusion, pred[126]{0:T(512)(128)(4,1)S(1)} %get-tuple-element.5, pred[126]{0:T(512)(128)(4,1)S(1)} %dynamic_slice.14), kind=kLoop, calls=%fused_computation.5 | loop fusion | flops 4128768 | bytes 8257788 | tf_op jit(solution)/shard_map/jit(_where)/select_n | solution.py:75
  176.5 0.0 reduce-scatter.2.cloned.1.call-update
  176.5 67.5 %reduce-scatter.2.cloned.1.call-done = bf16[63,128,128]{2,1,0:T(8,128)(2,1)} async-done(((bf16[126,128,128]{2,1,0:T(8,128)(2,1)}), bf16[63,128,128]{2,1,0:T(8,128)(2,1)}) %reduce-scatter.2.cloned.1.call-update) | async-done | bytes 2064400 | tf_op jit(solution)/shard_map/reduce_scatter | solution.py:76
  (5 shorter events, 0.1 us)
Async XLA Ops:
  6.5 38.6 %copy-start = (s32[32,14,32]{2,0,1:T(8,128)S(1)}, s32[32,14,32]{2,0,1:T(8,128)}, u32[]{:S(2)}) copy-start(s32[32,14,32]{2,0,1:T(8,128)} %param.5) | copy-start | bytes 172036
  6.5 39.3 %copy-start.1 = (bf16[2,1,1,128,1792]{4,3,2,1,0:T(8,128)(2,1)S(1)}, bf16[2,1,1,128,1792]{4,3,2,1,0:T(8,128)(2,1)}, u32[]{:S(2)}) copy-start(bf16[2,1,1,128,1792]{4,3,2,1,0:T(8,128)(2,1)} %param.3) | copy-start | bytes 2752516
  6.5 71.3 %all-gather.3.cloned.1.call-start = ((), (), s32[]{:S(2)}) async-start(), calls=%async_computation.1 | async-start | bytes 2359296 | tf_op jit(solution)/shard_map/all_gather | solution.py:49
  7.6 18.0 %collective-permute-start.1 = (bf16[128,512]{1,0:T(8,128)(2,1)S(1)}, bf16[128,512]{1,0:T(8,128)(2,1)S(1)}, u32[]{:S(2)}, u32[]{:S(2)}) collective-permute-start(bf16[128,512]{1,0:T(8,128)(2,1)S(1)} %get-tuple-element.8), channel_id=1, source_target_pairs={{1008,0},{0,16},{16,32},{32,48},{48,64},{64,80},{80,96},{96,112},{... | collective-permute-start | bytes 393224 | tf_op jit(solution)/shard_map/ppermute | solution.py:12
  13.9 12.7 %collective-permute-start = (bf16[128,512]{1,0:T(8,128)(2,1)S(1)}, bf16[128,512]{1,0:T(8,128)(2,1)S(1)}, u32[]{:S(2)}, u32[]{:S(2)}) collective-permute-start(bf16[128,512]{1,0:T(8,128)(2,1)S(1)} %get-tuple-element.7), channel_id=1, source_target_pairs={{16,0},{32,16},{48,32},{64,48},{80,64},{96,80},{112,96},{128,112},... | collective-permute-start | bytes 393224 | tf_op jit(solution)/shard_map/ppermute | solution.py:12
  27.3 99.2 %all-gather.5.cloned.1.call-start = ((), (), s32[]{:S(2)}) async-start(), calls=%async_computation.2 | async-start | bytes 2359296 | tf_op jit(solution)/shard_map/all_gather | solution.py:50
  27.4 11.2 %collective-permute-start.2 = (bf16[2,128,512]{2,1,0:T(8,128)(2,1)}, bf16[2,128,512]{2,1,0:T(8,128)(2,1)S(1)}, u32[]{:S(2)}, u32[]{:S(2)}) collective-permute-start(bf16[2,128,512]{2,1,0:T(8,128)(2,1)} %pad_maximum_fusion), channel_id=1, source_target_pairs={{0,512},{16,528},{32,544},{48,560},{64,576},{80,592},{96,608},{112... | collective-permute-start | bytes 786440 | tf_op jit(solution)/shard_map/ppermute | solution.py:18
  38.6 0.7 copy-start.3
  39.3 204.7 %reduce-scatter.2.cloned.1.call-start = ((), (), s32[]{:S(2)}) async-start(), calls=%async_computation.3 | async-start | bytes 6193152 | tf_op jit(solution)/shard_map/reduce_scatter | solution.py:76
  41.6 30.7 %collective-permute-start.3 = (bf16[256,1792]{0,1:T(8,128)(2,1)}, bf16[256,1792]{0,1:T(8,128)(2,1)S(1)}, u32[]{:S(2)}, u32[]{:S(2)}) collective-permute-start(bf16[256,1792]{0,1:T(8,128)(2,1)} %copy.25), channel_id=1, source_target_pairs={{0,512},{16,528},{32,544},{48,560},{64,576},{80,592},{96,608},{112... | collective-permute-start | bytes 2752520 | tf_op jit(solution)/shard_map/ppermute | solution.py:18
  126.5 4.9 %copy-start.2 = (bf16[256,14,128]{2,0,1:T(8,128)(2,1)S(1)}, bf16[256,14,128]{2,0,1:T(8,128)(2,1)}, u32[]{:S(2)}) copy-start(bf16[256,14,128]{2,0,1:T(8,128)(2,1)} %copy.18) | copy-start | bytes 2752516
Sparse Core Ops, SparseCore 0:
  27.5 50.3 all-gather.2
  80.5 45.9 all-gather.4
  176.6 67.3 reduce-scatter.1

commit v2 on v1

--- a/solution.py
+++ b/solution.py
@@ -49,31 +49,48 @@
     own_cot = lax.all_gather(own_arrived, "tp", axis=2, tiled=True)
     partner_cot = lax.all_gather(partner_arrived, "tp", axis=2, tiled=True)
     d_total = own_cot.shape[2]
-    cot = jnp.concatenate(
-        [own_cot.reshape(2 * row_count, d_total), partner_cot.reshape(2 * row_count, d_total)], axis=0
-    )
-    hidden_rows = jnp.concatenate([own_hidden, partner_hidden], axis=0)
-
     ffb = ff_local // block_side
     db = d_total // block_side
-    dense = jnp.einsum(
-        "nic,njd->ijcd",
-        hidden_rows.reshape(-1, ffb, block_side),
-        cot.reshape(-1, db, block_side),
-        preferred_element_type=jnp.float32,
-    ).astype(jnp.bfloat16)
 
     mask_local = lax.dynamic_index_in_dim(block_mask, section_index, 0, keepdims=False)
     slot_total = mask_local.shape[0] * mask_local.shape[1] * 9 // 16
     slots_half = slot_total // 2
+    slots_quarter = slots_half // 2
     block_rows, block_cols, usable = slot_table(mask_local, slot_total)
-    rows_h = lax.dynamic_slice_in_dim(block_rows, half_index * slots_half, slots_half, 0)
-    cols_h = lax.dynamic_slice_in_dim(block_cols, half_index * slots_half, slots_half, 0)
-    usable_h = lax.dynamic_slice_in_dim(usable, half_index * slots_half, slots_half, 0)
-    flat_index = rows_h * db + cols_h
-    picked = jnp.take(dense.reshape(ffb * db, block_side, block_side), flat_index, axis=0)
-    paired = jnp.where(usable_h[:, None, None], picked, jnp.zeros_like(picked))
-    summed = lax.psum_scatter(paired, "mirror", scatter_dimension=0, tiled=True)
+    mirror_index = lax.axis_index("mirror")
+
+    def quarter(which):
+        start = half_index * slots_half + which * slots_quarter
+        pick = lambda table: lax.dynamic_slice_in_dim(table, start, slots_quarter, 0)
+        return pick(block_rows), pick(block_cols), pick(usable)
+
+    sent_q = quarter(1 - mirror_index)
+    kept_q = quarter(mirror_index)
+
+    def partial_of(hidden_rows, cot_rows):
+        return jnp.einsum(
+            "njd,nic->jidc",
+            cot_rows.reshape(-1, db, block_side),
+            hidden_rows.reshape(-1, ffb, block_side),
+            preferred_element_type=jnp.float32,
+        ).astype(jnp.bfloat16)
+
+    def blocks_of(dense, table):
+        rows_q, cols_q, usable_q = table
+        picked = jnp.swapaxes(dense[cols_q, rows_q], 1, 2).astype(jnp.float32)
+        return jnp.where(usable_q[:, None, None], picked, 0.0)
+
+    own_dense = partial_of(own_hidden, own_cot)
+    partner_dense = partial_of(partner_hidden, partner_cot)
+
+    def paired_of(table):
+        total = blocks_of(own_dense, table) + blocks_of(partner_dense, table)
+        return total.astype(jnp.bfloat16)
+
+    outgoing = paired_of(sent_q)
+    received = from_partner(outgoing, "mirror", 0)
+    kept = paired_of(kept_q)
+    summed = (kept.astype(jnp.float32) + received.astype(jnp.float32)).astype(jnp.bfloat16)
     return summed.reshape(1, 1, -1, block_side, block_side)
 
 

time: 251 us -> 214 us (0.85)
  the two profiles are of different devices: /device:TPU:1 before, /device:TPU:2 now
where the time goes in v2:
time: 214 us
  waiting for transfers between devices  99.1 us (46%)
  local copies, waits for them, and re-layouts  39.6 us (19%)
  starting transfers between devices  30.9 us (14%)
  matrix products  19.4 us (9%)
  between operations  13.6 us (6%)
  other arithmetic  11 us (5%)
    ppermute x3, waiting for transfers between devices, from_partner(): return lax.ppermute(value, axis, pairs)  46.2 us
    all_gather x1, waiting for transfers between devices, body(): partner_cot = lax.all_gather(partner_arrived, 'tp', axis=2, tiled=True)  31.2 us
    gather x4, local copies, waits for them, and re-layouts, blocks_of(): picked = jnp.swapaxes(dense[cols_q, rows_q], 1, 2).astype(jnp.float32)  27.4 us
    ppermute x2, starting transfers between devices, passed_along(): return lax.ppermute(block, axis, route)  21 us
    dot_general x2, matrix products, partial_of(): jnp.einsum('njd,nic->jidc', cot_rows.reshape(-1, db, block_side), hidden_...  19.4 us
    all_gather x1, waiting for transfers between devices, body(): own_cot = lax.all_gather(own_arrived, 'tp', axis=2, tiled=True)  13 us
    ppermute x3, starting transfers between devices, from_partner(): return lax.ppermute(value, axis, pairs)  9.88 us
    ppermute x2, waiting for transfers between devices, passed_along(): return lax.ppermute(block, axis, route)  8.63 us
  transfers between devices with their start and end apart: 7, of which 6 were waited for; matrix products, arithmetic and copies ran while one was open for 17% of the time, Pallas kernels for 0%

profile of v2, /device:TPU:2, one launch (start us, length us, event | category | flops | bytes accessed | tf_op | source)
XLA Modules:
  0.0 213.5 jit_solution(4069312207771680094)
XLA Ops:
  6.5 0.0 copy-start
  6.5 0.0 copy-start.1
  6.5 0.0 all-gather.3.cloned.1.call-start
  6.5 1.1 slice_bitcast_fusion.1
  7.6 19.0 %collective-permute-start = (bf16[128,512]{1,0:T(8,128)(2,1)S(1)}, bf16[128,512]{1,0:T(8,128)(2,1)S(1)}, u32[]{:S(2)}, u32[]{:S(2)}) collective-permute-start(bf16[128,512]{1,0:T(8,128)(2,1)S(1)} %get-tuple-element.5), channel_id=1, source_target_pairs={{16,0},{32,16},{48,32},{64,48},{80,64},{96,80},{112,96},{128,112},... | collective-permute-start | bytes 393224 | tf_op jit(solution)/shard_map/ppermute | solution.py:12
  26.7 1.9 collective-permute-start.1
  28.6 1.0 collective-permute-done
  29.6 7.6 %collective-permute-done.1 = bf16[128,512]{1,0:T(8,128)(2,1)S(1)} collective-permute-done((bf16[128,512]{1,0:T(8,128)(2,1)S(1)}, bf16[128,512]{1,0:T(8,128)(2,1)S(1)}, u32[]{:S(2)}, u32[]{:S(2)}) %collective-permute-start.1) | collective-permute-done | bytes 131104 | tf_op jit(solution)/shard_map/ppermute | solution.py:12
  37.2 0.7 pad_maximum_fusion
  38.0 0.0 all-gather.3.cloned.1.call-update
  38.0 0.0 all-gather.5.cloned.1.call-start
  38.0 5.3 %collective-permute-start.2 = (bf16[2,128,512]{2,1,0:T(8,128)(2,1)}, bf16[2,128,512]{2,1,0:T(8,128)(2,1)S(1)}, u32[]{:S(2)}, u32[]{:S(2)}) collective-permute-start(bf16[2,128,512]{2,1,0:T(8,128)(2,1)} %pad_maximum_fusion), channel_id=1, source_target_pairs={{0,512},{16,528},{32,544},{48,560},{64,576},{80,592},{96,608},{112... | collective-permute-start | bytes 786440 | tf_op jit(solution)/shard_map/ppermute | solution.py:18
  43.4 17.4 %collective-permute-done.2 = bf16[2,128,512]{2,1,0:T(8,128)(2,1)S(1)} collective-permute-done((bf16[2,128,512]{2,1,0:T(8,128)(2,1)}, bf16[2,128,512]{2,1,0:T(8,128)(2,1)S(1)}, u32[]{:S(2)}, u32[]{:S(2)}) %collective-permute-start.2) | collective-permute-done | bytes 262176 | tf_op jit(solution)/shard_map/ppermute | solution.py:18
  60.7 0.0 copy-start.2
  60.7 0.7 copy-done.2
  61.4 0.0 all-gather.5.cloned.1.call-update
  61.5 0.0 copy-done.1
  61.5 0.5 copy.36
  62.0 1.9 collective-permute-start.3
  64.0 0.0 copy-done
  64.0 0.1 reshape.33
  64.1 0.3 reduce-window.9
  64.4 0.1 slice.20
  64.5 0.1 slice_reduce_fusion
  64.6 0.1 add_bitcast_fusion
  64.7 0.6 slice.22
  65.3 0.1 convert_reduce_fusion
  65.5 0.6 iota_compare_fusion.1
  66.1 0.7 reshape.93
  66.8 0.1 fusion.16
  66.8 0.1 fusion.8
  66.9 13.0 %all-gather.3.cloned.1.call-done = bf16[2,128,4096]{2,1,0:T(8,128)(2,1)} async-done(((bf16[2,128,512]{2,1,0:T(8,128)(2,1)}), bf16[2,128,4096]{2,1,0:T(8,128)(2,1)}) %all-gather.3.cloned.1.call-update) | async-done | bytes 2097168 | tf_op jit(solution)/shard_map/all_gather | solution.py:49
  79.9 2.1 copy.38
  82.0 9.1 %convert_bitcast_fusion.1 = bf16[32,14,128,128]{3,2,1,0:T(8,128)(2,1)} fusion(bf16[256,32,128,1]{2,1,0,3:T(8,128)(2,1)S(1)} %bitcast.45, bf16[256,14,128,1]{2,1,0,3:T(8,128)(2,1)S(1)} %bitcast.46), kind=kOutput, calls=%fused_computation.5 | convolution fusion | flops 3765436416 | bytes 17694720 | tf_op jit(solution)/shard_map/njd,nic->jidc/dot_general | solution.py:71
  91.1 6.2 %gather_fusion.2 = bf16[63,128,128]{2,1,0:T(8,128)(2,1)S(1)} fusion(bf16[32,14,128,128]{3,2,1,0:T(8,128)(2,1)} %convert_bitcast_fusion.1, s32[63]{0:T(128)S(1)} %get-tuple-element.8), kind=kCustom, calls=%fused_computation.2 | custom fusion | bytes 4129272 | tf_op jit(solution)/shard_map/gather | solution.py:80
  97.4 31.2 %all-gather.5.cloned.1.call-done = bf16[2,128,4096]{2,1,0:T(8,128)(2,1)} async-done(((bf16[2,128,512]{2,1,0:T(8,128)(2,1)}), bf16[2,128,4096]{2,1,0:T(8,128)(2,1)}) %all-gather.5.cloned.1.call-update) | async-done | bytes 2097168 | tf_op jit(solution)/shard_map/all_gather | solution.py:50
  128.6 2.1 copy.39
  130.6 0.0 collective-permute-done.3
  130.7 10.3 %convert_bitcast_fusion = bf16[32,14,128,128]{3,2,1,0:T(8,128)(2,1)} fusion(bf16[256,14,128,1]{0,2,1,3:T(8,128)(2,1)} %bitcast.13, bf16[256,32,128,1]{2,1,0,3:T(8,128)(2,1)S(1)} %bitcast.44), kind=kOutput, calls=%fused_computation.4 | convolution fusion | flops 3765436416 | bytes 17694720 | tf_op jit(solution)/shard_map/njd,nic->jidc/dot_general | solution.py:71
  140.9 7.4 %gather_fusion.3 = bf16[63,128,128]{2,1,0:T(8,128)(2,1)} fusion(bf16[32,14,128,128]{3,2,1,0:T(8,128)(2,1)} %convert_bitcast_fusion, s32[63]{0:T(128)S(1)} %get-tuple-element.8), kind=kCustom, calls=%fused_computation.3 | custom fusion | bytes 4129272 | tf_op jit(solution)/shard_map/gather | solution.py:80
  148.4 4.0 %fusion.3 = bf16[63,128,128]{1,2,0:T(8,128)(2,1)} fusion(bf16[63,128,128]{2,1,0:T(8,128)(2,1)} %gather_fusion.3, bf16[63,128,128]{2,1,0:T(8,128)(2,1)S(1)} %gather_fusion.2, pred[63]{0:T(512)(128)(4,1)S(1)} %get-tuple-element.12), kind=kLoop, calls=%fused_computation.12 | loop fusion | flops 6193152 | bytes 6193215 | tf_op jit(solution)/shard_map/convert_element_type | solution.py:88
  152.3 2.6 %collective-permute-start.4 = (bf16[63,128,128]{1,2,0:T(8,128)(2,1)}, bf16[63,128,128]{1,2,0:T(8,128)(2,1)}, u32[]{:S(2)}, u32[]{:S(2)}) collective-permute-start(bf16[63,128,128]{1,2,0:T(8,128)(2,1)} %fusion.3), channel_id=1, source_target_pairs={{0,1},{1,0},{2,3},{3,2},{4,5},{5,4},{6,7},{7,6},{8,9},{9,8},{10,11... | collective-permute-start | bytes 6193160 | tf_op jit(solution)/shard_map/ppermute | solution.py:18
  155.0 6.3 %gather_fusion = bf16[63,128,128]{2,1,0:T(8,128)(2,1)S(1)} fusion(bf16[32,14,128,128]{3,2,1,0:T(8,128)(2,1)} %convert_bitcast_fusion.1, s32[63]{0:T(128)S(1)} %get-tuple-element.7), kind=kCustom, calls=%fused_computation | custom fusion | bytes 4129272 | tf_op jit(solution)/shard_map/gather | solution.py:80
  161.2 7.5 %gather_fusion.1 = bf16[63,128,128]{2,1,0:T(8,128)(2,1)} fusion(bf16[32,14,128,128]{3,2,1,0:T(8,128)(2,1)} %convert_bitcast_fusion, s32[63]{0:T(128)S(1)} %get-tuple-element.7), kind=kCustom, calls=%fused_computation.1 | custom fusion | bytes 4129272 | tf_op jit(solution)/shard_map/gather | solution.py:80
  168.7 28.8 %collective-permute-done.4 = bf16[63,128,128]{1,2,0:T(8,128)(2,1)} collective-permute-done((bf16[63,128,128]{1,2,0:T(8,128)(2,1)}, bf16[63,128,128]{1,2,0:T(8,128)(2,1)}, u32[]{:S(2)}, u32[]{:S(2)}) %collective-permute-start.4) | collective-permute-done | bytes 2064416 | tf_op jit(solution)/shard_map/ppermute | solution.py:18
  197.5 5.1 %fusion.4 = bf16[1,1,63,128,128]{3,4,2,1,0:T(8,128)(2,1)} fusion(bf16[63,128,128]{1,2,0:T(8,128)(2,1)} %collective-permute-done.4, bf16[63,128,128]{2,1,0:T(8,128)(2,1)} %gather_fusion.1, bf16[63,128,128]{2,1,0:T(8,128)(2,1)S(1)} %gather_fusion, pred[63]{0:T(512)(128)(4,1)S(1)} %get-tuple-element.11), kind=kLoop, calls=%fused_computation.13 | loop fusion | flops 10321920 | bytes 8257599 | tf_op jit(solution)/shard_map/reshape | solution.py:94
  202.6 4.1 %copy.21 = bf16[1,1,63,128,128]{4,3,2,1,0:T(8,128)(2,1)} copy(bf16[1,1,63,128,128]{3,4,2,1,0:T(8,128)(2,1)} %fusion.4) | data formatting | bytes 4128768 | tf_op jit(solution)/shard_map/reshape | solution.py:94
  (4 shorter events, 0.1 us)
Async XLA Ops:
  6.5 57.4 %copy-start = (s32[32,14,32]{2,0,1:T(8,128)S(1)}, s32[32,14,32]{2,0,1:T(8,128)}, u32[]{:S(2)}) copy-start(s32[32,14,32]{2,0,1:T(8,128)} %param.5) | copy-start | bytes 172036
  6.5 54.9 %copy-start.1 = (bf16[2,1,1,128,1792]{4,3,2,1,0:T(8,128)(2,1)S(1)}, bf16[2,1,1,128,1792]{4,3,2,1,0:T(8,128)(2,1)}, u32[]{:S(2)}) copy-start(bf16[2,1,1,128,1792]{4,3,2,1,0:T(8,128)(2,1)} %param.3) | copy-start | bytes 2752516
  6.5 73.4 %all-gather.3.cloned.1.call-start = ((), (), s32[]{:S(2)}) async-start(), calls=%async_computation | async-start | bytes 2359296 | tf_op jit(solution)/shard_map/all_gather | solution.py:49
  7.6 22.0 %collective-permute-start = (bf16[128,512]{1,0:T(8,128)(2,1)S(1)}, bf16[128,512]{1,0:T(8,128)(2,1)S(1)}, u32[]{:S(2)}, u32[]{:S(2)}) collective-permute-start(bf16[128,512]{1,0:T(8,128)(2,1)S(1)} %get-tuple-element.5), channel_id=1, source_target_pairs={{16,0},{32,16},{48,32},{64,48},{80,64},{96,80},{112,96},{128,112},... | collective-permute-start | bytes 393224 | tf_op jit(solution)/shard_map/ppermute | solution.py:12
  26.7 10.6 %collective-permute-start.1 = (bf16[128,512]{1,0:T(8,128)(2,1)S(1)}, bf16[128,512]{1,0:T(8,128)(2,1)S(1)}, u32[]{:S(2)}, u32[]{:S(2)}) collective-permute-start(bf16[128,512]{1,0:T(8,128)(2,1)S(1)} %get-tuple-element.6), channel_id=1, source_target_pairs={{1008,0},{0,16},{16,32},{32,48},{48,64},{64,80},{80,96},{96,112},{... | collective-permute-start | bytes 393224 | tf_op jit(solution)/shard_map/ppermute | solution.py:12
  38.0 90.6 %all-gather.5.cloned.1.call-start = ((), (), s32[]{:S(2)}) async-start(), calls=%async_computation.1 | async-start | bytes 2359296 | tf_op jit(solution)/shard_map/all_gather | solution.py:50
  38.0 22.7 %collective-permute-start.2 = (bf16[2,128,512]{2,1,0:T(8,128)(2,1)}, bf16[2,128,512]{2,1,0:T(8,128)(2,1)S(1)}, u32[]{:S(2)}, u32[]{:S(2)}) collective-permute-start(bf16[2,128,512]{2,1,0:T(8,128)(2,1)} %pad_maximum_fusion), channel_id=1, source_target_pairs={{0,512},{16,528},{32,544},{48,560},{64,576},{80,592},{96,608},{112... | collective-permute-start | bytes 786440 | tf_op jit(solution)/shard_map/ppermute | solution.py:18
  60.7 0.7 copy-start.2
  62.0 68.6 %collective-permute-start.3 = (bf16[256,1792]{0,1:T(8,128)(2,1)S(1)}, bf16[256,1792]{0,1:T(8,128)(2,1)}, u32[]{:S(2)}, u32[]{:S(2)}) collective-permute-start(bf16[256,1792]{0,1:T(8,128)(2,1)S(1)} %copy.36), channel_id=1, source_target_pairs={{0,512},{16,528},{32,544},{48,560},{64,576},{80,592},{96,608},{112... | collective-permute-start | bytes 2752520 | tf_op jit(solution)/shard_map/ppermute | solution.py:18
  152.3 45.2 %collective-permute-start.4 = (bf16[63,128,128]{1,2,0:T(8,128)(2,1)}, bf16[63,128,128]{1,2,0:T(8,128)(2,1)}, u32[]{:S(2)}, u32[]{:S(2)}) collective-permute-start(bf16[63,128,128]{1,2,0:T(8,128)(2,1)} %fusion.3), channel_id=1, source_target_pairs={{0,1},{1,0},{2,3},{3,2},{4,5},{5,4},{6,7},{7,6},{8,9},{9,8},{10,11... | collective-permute-start | bytes 6193160 | tf_op jit(solution)/shard_map/ppermute | solution.py:18
Sparse Core Ops, SparseCore 0:
  38.1 41.7 all-gather.2
  82.6 45.9 all-gather.4

commit v3 on v2

--- a/solution.py
+++ b/solution.py
@@ -46,7 +46,13 @@
     up_part = passed_along(incoming[1, 0, 0], "section", 1)
     own_arrived = jnp.stack([down_part, up_part])
     partner_arrived = from_partner(own_arrived, "section", swap_bit)
-    own_cot = lax.all_gather(own_arrived, "tp", axis=2, tiled=True)
+    own_incoming_all = lax.all_gather(incoming[:, 0, 0], "tp", axis=2, tiled=True)
+    own_cot = jnp.stack(
+        [
+            passed_along(own_incoming_all[0], "section", -1),
+            passed_along(own_incoming_all[1], "section", 1),
+        ]
+    )
     partner_cot = lax.all_gather(partner_arrived, "tp", axis=2, tiled=True)
     d_total = own_cot.shape[2]
     ffb = ff_local // block_side

time: 214 us -> 220 us (1.028)
  starting transfers between devices: 30.9 us -> 37.9 us
  waiting for transfers between devices: 99.1 us -> 94.9 us
    all_gather x1, waiting for transfers between devices: 13 us -> 1.93 us  [body(): lax.all_gather(incoming[:, 0, 0], 'tp', axis=2, tiled=True)]
    ppermute x2 -> x4, starting transfers between devices: 21 us -> 27.9 us  [passed_along(): return lax.ppermute(block, axis, route)]
    all_gather x1, waiting for transfers between devices: 31.2 us -> 37.5 us  [body(): partner_cot = lax.all_gather(partner_arrived, 'tp', axis=2, tiled=True)]
    squeeze x0 -> x1, local copies, waits for them, and re-layouts: none -> 3.1 us  [body(): own_incoming_all[0]]
    ppermute x2 -> x4, waiting for transfers between devices: 8.63 us -> 8.64 us  [passed_along(): return lax.ppermute(block, axis, route)]
  transfers between devices with their start and end apart: 7 -> 9, of which waited for: 6 -> 6; matrix products, arithmetic and copies ran while one was open for 17% -> 18% of each run, Pallas kernels for 0% -> 0%
where the time goes in v3:
time: 220 us; the launch traced here: 219 us
  waiting for transfers between devices  94.9 us (43%)
  local copies, waits for them, and re-layouts  41 us (19%)
  starting transfers between devices  37.9 us (17%)
  matrix products  19.4 us (9%)
  between operations  13.6 us (6%)
  other arithmetic  12.1 us (6%)
    ppermute x3, waiting for transfers between devices, from_partner(): return lax.ppermute(value, axis, pairs)  46 us
    all_gather x1, waiting for transfers between devices, body(): partner_cot = lax.all_gather(partner_arrived, 'tp', axis=2, tiled=True)  37.5 us
    ppermute x4, starting transfers between devices, passed_along(): return lax.ppermute(block, axis, route)  27.9 us
    gather x4, local copies, waits for them, and re-layouts, blocks_of(): picked = jnp.swapaxes(dense[cols_q, rows_q], 1, 2).astype(jnp.float32)  27.4 us
    dot_general x2, matrix products, partial_of(): jnp.einsum('njd,nic->jidc', cot_rows.reshape(-1, db, block_side), hidden_...  19.4 us
    ppermute x3, starting transfers between devices, from_partner(): return lax.ppermute(value, axis, pairs)  10 us
    ppermute x4, waiting for transfers between devices, passed_along(): return lax.ppermute(block, axis, route)  8.64 us
    reshape x1, other arithmetic, body(): return summed.reshape(1, 1, -1, block_side, block_side)  5.08 us
  transfers between devices with their start and end apart: 9, of which 6 were waited for; matrix products, arithmetic and copies ran while one was open for 18% of the time, Pallas kernels for 0%

profile of v3, /device:TPU:2, one launch (start us, length us, event | category | flops | bytes accessed | tf_op | source)
XLA Modules:
  0.0 218.9 jit_solution(18248455582295098669)
XLA Ops:
  6.5 0.0 copy-start
  6.5 0.0 copy-start.1
  6.5 0.0 all-gather.6.cloned.1.call-start
  6.5 0.7 all-gather.6.cloned.1.call-update
  7.3 0.0 all-gather.4.cloned.1.call-start
  7.3 1.0 slice_bitcast_fusion.3
  8.3 19.0 %collective-permute-start.2 = (bf16[128,512]{1,0:T(8,128)(2,1)S(1)}, bf16[128,512]{1,0:T(8,128)(2,1)S(1)}, u32[]{:S(2)}, u32[]{:S(2)}) collective-permute-start(bf16[128,512]{1,0:T(8,128)(2,1)S(1)} %get-tuple-element.7), channel_id=1, source_target_pairs={{16,0},{32,16},{48,32},{64,48},{80,64},{96,80},{112,96},{128,112},... | collective-permute-start | bytes 393224 | tf_op jit(solution)/shard_map/ppermute | solution.py:12
  27.3 1.9 collective-permute-start.3
  29.3 1.0 collective-permute-done.2
  30.3 7.6 %collective-permute-done.3 = bf16[128,512]{1,0:T(8,128)(2,1)S(1)} collective-permute-done((bf16[128,512]{1,0:T(8,128)(2,1)S(1)}, bf16[128,512]{1,0:T(8,128)(2,1)S(1)}, u32[]{:S(2)}, u32[]{:S(2)}) %collective-permute-start.3) | collective-permute-done | bytes 131104 | tf_op jit(solution)/shard_map/ppermute | solution.py:12
  37.9 5.3 %collective-permute-start.4 = (bf16[2,128,512]{2,1,0:T(8,128)(2,1)S(1)}, bf16[2,128,512]{2,1,0:T(8,128)(2,1)S(1)}, u32[]{:S(2)}, u32[]{:S(2)}) collective-permute-start(bf16[2,128,512]{2,1,0:T(8,128)(2,1)S(1)} %pad_maximum_fusion.1), channel_id=1, source_target_pairs={{0,512},{16,528},{32,544},{48,560},{64,576},{80,592},{96,608},{112... | collective-permute-start | bytes 786440 | tf_op jit(solution)/shard_map/ppermute | solution.py:18
  43.3 17.2 %collective-permute-done.4 = bf16[2,128,512]{2,1,0:T(8,128)(2,1)S(1)} collective-permute-done((bf16[2,128,512]{2,1,0:T(8,128)(2,1)S(1)}, bf16[2,128,512]{2,1,0:T(8,128)(2,1)S(1)}, u32[]{:S(2)}, u32[]{:S(2)}) %collective-permute-start.4) | collective-permute-done | bytes 262176 | tf_op jit(solution)/shard_map/ppermute | solution.py:18
  60.4 0.0 copy-start.2
  60.4 0.7 copy-done.2
  61.1 0.0 all-gather.4.cloned.1.call-update
  61.2 0.0 copy-done.1
  61.2 0.5 copy.36
  61.7 1.9 collective-permute-start.5
  63.7 0.0 copy-done
  63.7 0.1 reshape.33
  63.8 0.3 reduce-window.9
  64.1 0.1 slice.26
  64.2 0.1 slice_reduce_fusion
  64.3 0.1 add_bitcast_fusion
  64.4 0.6 slice.28
  65.0 0.6 iota_compare_fusion.1
  65.7 0.1 convert_reduce_fusion
  65.8 1.9 all-gather.6.cloned.1.call-done
  67.7 3.1 %slice_bitcast_fusion.1 = (bf16[128,4096]{1,0:T(8,128)(2,1)}, bf16[128,4096]{1,0:T(8,128)(2,1)}) fusion(bf16[2,1,1,128,4096]{4,3,2,1,0:T(8,128)(2,1)} %all-gather.6.cloned.1.call-done), kind=kLoop, calls=%fused_computation.16 | loop fusion | bytes 4194304 | tf_op jit(solution)/shard_map/squeeze | solution.py:52
  70.8 5.0 %collective-permute-start = (bf16[128,4096]{1,0:T(8,128)(2,1)}, bf16[128,4096]{1,0:T(8,128)(2,1)}, u32[]{:S(2)}, u32[]{:S(2)}) collective-permute-start(bf16[128,4096]{1,0:T(8,128)(2,1)} %get-tuple-element.5), channel_id=1, source_target_pairs={{16,0},{32,16},{48,32},{64,48},{80,64},{96,80},{112,96},{128,112},... | collective-permute-start | bytes 3145736 | tf_op jit(solution)/shard_map/ppermute | solution.py:12
  75.8 1.9 collective-permute-start.1
  77.8 0.1 fusion.16
  77.9 0.7 reshape.98
  78.6 0.1 fusion.8
  78.7 37.5 %all-gather.4.cloned.1.call-done = bf16[2,128,4096]{2,1,0:T(8,128)(2,1)} async-done(((bf16[2,128,512]{2,1,0:T(8,128)(2,1)}), bf16[2,128,4096]{2,1,0:T(8,128)(2,1)}) %all-gather.4.cloned.1.call-update) | async-done | bytes 2097168 | tf_op jit(solution)/shard_map/all_gather | solution.py:56
  116.2 2.1 copy.39
  118.3 0.0 collective-permute-done.5
  118.3 10.4 %convert_bitcast_fusion = bf16[32,14,128,128]{3,2,1,0:T(8,128)(2,1)} fusion(bf16[256,14,128,1]{0,2,1,3:T(8,128)(2,1)} %bitcast.17, bf16[256,32,128,1]{2,1,0,3:T(8,128)(2,1)S(1)} %bitcast.50), kind=kOutput, calls=%fused_computation.4 | convolution fusion | flops 3765436416 | bytes 17694720 | tf_op jit(solution)/shard_map/njd,nic->jidc/dot_general | solution.py:77
  128.6 6.2 %gather_fusion.3 = bf16[63,128,128]{2,1,0:T(8,128)(2,1)S(1)} fusion(bf16[32,14,128,128]{3,2,1,0:T(8,128)(2,1)} %convert_bitcast_fusion, s32[63]{0:T(128)S(1)} %get-tuple-element.10), kind=kCustom, calls=%fused_computation.3 | custom fusion | bytes 4129272 | tf_op jit(solution)/shard_map/gather | solution.py:86
  134.9 0.0 collective-permute-done
  134.9 0.0 collective-permute-done.1
  134.9 1.7 pad_maximum_fusion
  136.6 0.5 copy.38
  137.1 9.1 %convert_bitcast_fusion.1 = bf16[32,14,128,128]{3,2,1,0:T(8,128)(2,1)} fusion(bf16[256,32,128,1]{2,1,0,3:T(8,128)(2,1)S(1)} %bitcast.51, bf16[256,14,128,1]{2,1,0,3:T(8,128)(2,1)S(1)} %bitcast.53), kind=kOutput, calls=%fused_computation.5 | convolution fusion | flops 3765436416 | bytes 17694720 | tf_op jit(solution)/shard_map/njd,nic->jidc/dot_general | solution.py:77
  146.2 7.4 %gather_fusion.2 = bf16[63,128,128]{2,1,0:T(8,128)(2,1)} fusion(bf16[32,14,128,128]{3,2,1,0:T(8,128)(2,1)} %convert_bitcast_fusion.1, s32[63]{0:T(128)S(1)} %get-tuple-element.10), kind=kCustom, calls=%fused_computation.2 | custom fusion | bytes 4129272 | tf_op jit(solution)/shard_map/gather | solution.py:86
  153.6 4.0 %fusion.3 = bf16[63,128,128]{1,2,0:T(8,128)(2,1)} fusion(bf16[63,128,128]{2,1,0:T(8,128)(2,1)S(1)} %gather_fusion.3, bf16[63,128,128]{2,1,0:T(8,128)(2,1)} %gather_fusion.2, pred[63]{0:T(512)(128)(4,1)S(1)} %get-tuple-element.14), kind=kLoop, calls=%fused_computation.13 | loop fusion | flops 6193152 | bytes 6193215 | tf_op jit(solution)/shard_map/convert_element_type | solution.py:94
  157.6 2.8 %collective-permute-start.6 = (bf16[63,128,128]{1,2,0:T(8,128)(2,1)}, bf16[63,128,128]{1,2,0:T(8,128)(2,1)}, u32[]{:S(2)}, u32[]{:S(2)}) collective-permute-start(bf16[63,128,128]{1,2,0:T(8,128)(2,1)} %fusion.3), channel_id=1, source_target_pairs={{0,1},{1,0},{2,3},{3,2},{4,5},{5,4},{6,7},{7,6},{8,9},{9,8},{10,11... | collective-permute-start | bytes 6193160 | tf_op jit(solution)/shard_map/ppermute | solution.py:18
  160.4 6.3 %gather_fusion.1 = bf16[63,128,128]{2,1,0:T(8,128)(2,1)S(1)} fusion(bf16[32,14,128,128]{3,2,1,0:T(8,128)(2,1)} %convert_bitcast_fusion, s32[63]{0:T(128)S(1)} %get-tuple-element.9), kind=kCustom, calls=%fused_computation.1 | custom fusion | bytes 4129272 | tf_op jit(solution)/shard_map/gather | solution.py:86
  166.6 7.4 %gather_fusion = bf16[63,128,128]{2,1,0:T(8,128)(2,1)} fusion(bf16[32,14,128,128]{3,2,1,0:T(8,128)(2,1)} %convert_bitcast_fusion.1, s32[63]{0:T(128)S(1)} %get-tuple-element.9), kind=kCustom, calls=%fused_computation | custom fusion | bytes 4129272 | tf_op jit(solution)/shard_map/gather | solution.py:86
  174.1 28.9 %collective-permute-done.6 = bf16[63,128,128]{1,2,0:T(8,128)(2,1)} collective-permute-done((bf16[63,128,128]{1,2,0:T(8,128)(2,1)}, bf16[63,128,128]{1,2,0:T(8,128)(2,1)}, u32[]{:S(2)}, u32[]{:S(2)}) %collective-permute-start.6) | collective-permute-done | bytes 2064416 | tf_op jit(solution)/shard_map/ppermute | solution.py:18
  202.9 5.1 %fusion.4 = bf16[1,1,63,128,128]{3,4,2,1,0:T(8,128)(2,1)} fusion(bf16[63,128,128]{1,2,0:T(8,128)(2,1)} %collective-permute-done.6, bf16[63,128,128]{2,1,0:T(8,128)(2,1)S(1)} %gather_fusion.1, bf16[63,128,128]{2,1,0:T(8,128)(2,1)} %gather_fusion, pred[63]{0:T(512)(128)(4,1)S(1)} %get-tuple-element.13), kind=kLoop, calls=%fused_computation.14 | loop fusion | flops 10321920 | bytes 8257599 | tf_op jit(solution)/shard_map/reshape | solution.py:100
  208.0 4.1 %copy.21 = bf16[1,1,63,128,128]{4,3,2,1,0:T(8,128)(2,1)} copy(bf16[1,1,63,128,128]{3,4,2,1,0:T(8,128)(2,1)} %fusion.4) | data formatting | bytes 4128768 | tf_op jit(solution)/shard_map/reshape | solution.py:100
  (5 shorter events, 0.1 us)
Async XLA Ops:
  6.5 57.1 %copy-start = (s32[32,14,32]{2,0,1:T(8,128)S(1)}, s32[32,14,32]{2,0,1:T(8,128)}, u32[]{:S(2)}) copy-start(s32[32,14,32]{2,0,1:T(8,128)} %param.5) | copy-start | bytes 172036
  6.5 54.6 %copy-start.1 = (bf16[2,1,1,128,1792]{4,3,2,1,0:T(8,128)(2,1)S(1)}, bf16[2,1,1,128,1792]{4,3,2,1,0:T(8,128)(2,1)}, u32[]{:S(2)}) copy-start(bf16[2,1,1,128,1792]{4,3,2,1,0:T(8,128)(2,1)} %param.3) | copy-start | bytes 2752516
  6.5 61.2 %all-gather.6.cloned.1.call-start = ((), (), s32[]{:S(2)}) async-start(), calls=%async_computation.1 | async-start | bytes 2359296 | tf_op jit(solution)/shard_map/all_gather | solution.py:49
  7.3 108.9 %all-gather.4.cloned.1.call-start = ((), (), s32[]{:S(2)}) async-start(), calls=%async_computation | async-start | bytes 2359296 | tf_op jit(solution)/shard_map/all_gather | solution.py:56
  8.3 22.0 %collective-permute-start.2 = (bf16[128,512]{1,0:T(8,128)(2,1)S(1)}, bf16[128,512]{1,0:T(8,128)(2,1)S(1)}, u32[]{:S(2)}, u32[]{:S(2)}) collective-permute-start(bf16[128,512]{1,0:T(8,128)(2,1)S(1)} %get-tuple-element.7), channel_id=1, source_target_pairs={{16,0},{32,16},{48,32},{64,48},{80,64},{96,80},{112,96},{128,112},... | collective-permute-start | bytes 393224 | tf_op jit(solution)/shard_map/ppermute | solution.py:12
  27.3 10.6 %collective-permute-start.3 = (bf16[128,512]{1,0:T(8,128)(2,1)S(1)}, bf16[128,512]{1,0:T(8,128)(2,1)S(1)}, u32[]{:S(2)}, u32[]{:S(2)}) collective-permute-start(bf16[128,512]{1,0:T(8,128)(2,1)S(1)} %get-tuple-element.8), channel_id=1, source_target_pairs={{1008,0},{0,16},{16,32},{32,48},{48,64},{64,80},{80,96},{96,112},{... | collective-permute-start | bytes 393224 | tf_op jit(solution)/shard_map/ppermute | solution.py:12
  37.9 22.5 %collective-permute-start.4 = (bf16[2,128,512]{2,1,0:T(8,128)(2,1)S(1)}, bf16[2,128,512]{2,1,0:T(8,128)(2,1)S(1)}, u32[]{:S(2)}, u32[]{:S(2)}) collective-permute-start(bf16[2,128,512]{2,1,0:T(8,128)(2,1)S(1)} %pad_maximum_fusion.1), channel_id=1, source_target_pairs={{0,512},{16,528},{32,544},{48,560},{64,576},{80,592},{96,608},{112... | collective-permute-start | bytes 786440 | tf_op jit(solution)/shard_map/ppermute | solution.py:18
  60.4 0.7 copy-start.2
  61.7 56.6 %collective-permute-start.5 = (bf16[256,1792]{0,1:T(8,128)(2,1)S(1)}, bf16[256,1792]{0,1:T(8,128)(2,1)}, u32[]{:S(2)}, u32[]{:S(2)}) collective-permute-start(bf16[256,1792]{0,1:T(8,128)(2,1)S(1)} %copy.36), channel_id=1, source_target_pairs={{0,512},{16,528},{32,544},{48,560},{64,576},{80,592},{96,608},{112... | collective-permute-start | bytes 2752520 | tf_op jit(solution)/shard_map/ppermute | solution.py:18
  70.8 64.0 %collective-permute-start = (bf16[128,4096]{1,0:T(8,128)(2,1)}, bf16[128,4096]{1,0:T(8,128)(2,1)}, u32[]{:S(2)}, u32[]{:S(2)}) collective-permute-start(bf16[128,4096]{1,0:T(8,128)(2,1)} %get-tuple-element.5), channel_id=1, source_target_pairs={{16,0},{32,16},{48,32},{64,48},{80,64},{96,80},{112,96},{128,112},... | collective-permute-start | bytes 3145736 | tf_op jit(solution)/shard_map/ppermute | solution.py:12
  75.8 59.1 %collective-permute-start.1 = (bf16[128,4096]{1,0:T(8,128)(2,1)}, bf16[128,4096]{1,0:T(8,128)(2,1)}, u32[]{:S(2)}, u32[]{:S(2)}) collective-permute-start(bf16[128,4096]{1,0:T(8,128)(2,1)} %get-tuple-element.6), channel_id=1, source_target_pairs={{1008,0},{0,16},{16,32},{32,48},{48,64},{64,80},{80,96},{96,112},{... | collective-permute-start | bytes 3145736 | tf_op jit(solution)/shard_map/ppermute | solution.py:12
  157.6 45.4 %collective-permute-start.6 = (bf16[63,128,128]{1,2,0:T(8,128)(2,1)}, bf16[63,128,128]{1,2,0:T(8,128)(2,1)}, u32[]{:S(2)}, u32[]{:S(2)}) collective-permute-start(bf16[63,128,128]{1,2,0:T(8,128)(2,1)} %fusion.3), channel_id=1, source_target_pairs={{0,1},{1,0},{2,3},{3,2},{4,5},{5,4},{6,7},{7,6},{8,9},{9,8},{10,11... | collective-permute-start | bytes 6193160 | tf_op jit(solution)/shard_map/ppermute | solution.py:18
Sparse Core Ops, SparseCore 0:
  10.0 57.6 all-gather.5
  70.4 45.7 all-gather.3

commit v4 on v3

--- a/solution.py
+++ b/solution.py
@@ -83,19 +83,22 @@
 
     def blocks_of(dense, table):
         rows_q, cols_q, usable_q = table
-        picked = jnp.swapaxes(dense[cols_q, rows_q], 1, 2).astype(jnp.float32)
-        return jnp.where(usable_q[:, None, None], picked, 0.0)
+        picked = jnp.swapaxes(dense[cols_q, rows_q], 1, 2)
+        return jnp.where(usable_q[:, None, None], picked, jnp.zeros_like(picked))
 
     own_dense = partial_of(own_hidden, own_cot)
+    own_sent = blocks_of(own_dense, sent_q)
+    own_kept = blocks_of(own_dense, kept_q)
+    own_sent, own_kept, partner_cot = lax.optimization_barrier((own_sent, own_kept, partner_cot))
     partner_dense = partial_of(partner_hidden, partner_cot)
 
-    def paired_of(table):
-        total = blocks_of(own_dense, table) + blocks_of(partner_dense, table)
+    def paired_of(own_blocks, table):
+        total = own_blocks.astype(jnp.float32) + blocks_of(partner_dense, table).astype(jnp.float32)
         return total.astype(jnp.bfloat16)
 
-    outgoing = paired_of(sent_q)
+    outgoing = paired_of(own_sent, sent_q)
     received = from_partner(outgoing, "mirror", 0)
-    kept = paired_of(kept_q)
+    kept = paired_of(own_kept, kept_q)
     summed = (kept.astype(jnp.float32) + received.astype(jnp.float32)).astype(jnp.bfloat16)
     return summed.reshape(1, 1, -1, block_side, block_side)
 

time: 220 us -> 213 us (0.968)
  the two profiles are of different devices: /device:TPU:2 before, /device:TPU:4 now
where the time goes in v4:
time: 213 us; the launch traced here: 212 us
  waiting for transfers between devices  82.3 us (39%)
  local copies, waits for them, and re-layouts  44.6 us (21%)
  starting transfers between devices  36.5 us (17%)
  matrix products  19.5 us (9%)
  other arithmetic  15.8 us (7%)
  between operations  13.6 us (6%)
    ppermute x4, waiting for transfers between devices, passed_along(): return lax.ppermute(block, axis, route)  43.9 us
    gather x4, local copies, waits for them, and re-layouts, blocks_of(): picked = jnp.swapaxes(dense[cols_q, rows_q], 1, 2)  29.7 us
    ppermute x3, waiting for transfers between devices, from_partner(): return lax.ppermute(value, axis, pairs)  23.8 us
    ppermute x4, starting transfers between devices, passed_along(): return lax.ppermute(block, axis, route)  23.5 us
    dot_general x2, matrix products, partial_of(): jnp.einsum('njd,nic->jidc', cot_rows.reshape(-1, db, block_side), hidden_...  19.5 us
    all_gather x1, waiting for transfers between devices, body(): lax.all_gather(incoming[:, 0, 0], 'tp', axis=2, tiled=True)  13.8 us
    ppermute x3, starting transfers between devices, from_partner(): return lax.ppermute(value, axis, pairs)  13 us
    reshape x1, other arithmetic, body(): return summed.reshape(1, 1, -1, block_side, block_side)  5.02 us
  transfers between devices with their start and end apart: 9, of which 7 were waited for; matrix products, arithmetic and copies ran while one was open for 23% of the time, Pallas kernels for 0%

profile of v4, /device:TPU:4, one launch (start us, length us, event | category | flops | bytes accessed | tf_op | source)
XLA Modules:
  0.0 212.3 jit_solution(15822040171191524968)
XLA Ops:
  6.5 0.0 copy-start
  6.5 0.0 all-gather.6.cloned.1.call-start
  6.5 0.7 all-gather.6.cloned.1.call-update
  7.3 0.0 all-gather.4.cloned.1.call-start
  7.3 1.0 slice_bitcast_fusion.3
  8.3 16.7 %collective-permute-start.2 = (bf16[128,512]{1,0:T(8,128)(2,1)S(1)}, bf16[128,512]{1,0:T(8,128)(2,1)S(1)}, u32[]{:S(2)}, u32[]{:S(2)}) collective-permute-start(bf16[128,512]{1,0:T(8,128)(2,1)S(1)} %get-tuple-element.13), channel_id=1, source_target_pairs={{16,0},{32,16},{48,32},{64,48},{80,64},{96,80},{112,96},{128,112},... | collective-permute-start | bytes 393224 | tf_op jit(solution)/shard_map/ppermute | solution.py:12
  25.0 1.9 collective-permute-start.3
  26.9 2.0 collective-permute-done.2
  28.9 5.5 %collective-permute-done.3 = bf16[128,512]{1,0:T(8,128)(2,1)S(1)} collective-permute-done((bf16[128,512]{1,0:T(8,128)(2,1)S(1)}, bf16[128,512]{1,0:T(8,128)(2,1)S(1)}, u32[]{:S(2)}, u32[]{:S(2)}) %collective-permute-start.3) | collective-permute-done | bytes 131104 | tf_op jit(solution)/shard_map/ppermute | solution.py:12
  34.4 7.4 %collective-permute-start.4 = (bf16[2,128,512]{2,1,0:T(8,128)(2,1)S(1)}, bf16[2,128,512]{2,1,0:T(8,128)(2,1)S(1)}, u32[]{:S(2)}, u32[]{:S(2)}) collective-permute-start(bf16[2,128,512]{2,1,0:T(8,128)(2,1)S(1)} %pad_maximum_fusion.1), channel_id=1, source_target_pairs={{0,512},{16,528},{32,544},{48,560},{64,576},{80,592},{96,608},{112... | collective-permute-start | bytes 786440 | tf_op jit(solution)/shard_map/ppermute | solution.py:18
  41.8 2.2 %copy.35 = bf16[256,1792]{0,1:T(8,128)(2,1)} copy(bf16[256,1792]{1,0:T(8,128)(2,1)} %bitcast.60) | data formatting | bytes 1835008 | tf_op jit(solution)/shard_map/reshape;squeeze | solution.py:43
  44.0 2.3 %collective-permute-start.5 = (bf16[256,1792]{0,1:T(8,128)(2,1)}, bf16[256,1792]{0,1:T(8,128)(2,1)}, u32[]{:S(2)}, u32[]{:S(2)}) collective-permute-start(bf16[256,1792]{0,1:T(8,128)(2,1)} %copy.35), channel_id=1, source_target_pairs={{0,512},{16,528},{32,544},{48,560},{64,576},{80,592},{96,608},{112... | collective-permute-start | bytes 2752520 | tf_op jit(solution)/shard_map/ppermute | solution.py:18
  46.4 0.0 copy-done
  46.5 0.1 reshape.33
  46.5 6.5 %collective-permute-done.4 = bf16[2,128,512]{2,1,0:T(8,128)(2,1)S(1)} collective-permute-done((bf16[2,128,512]{2,1,0:T(8,128)(2,1)S(1)}, bf16[2,128,512]{2,1,0:T(8,128)(2,1)S(1)}, u32[]{:S(2)}, u32[]{:S(2)}) %collective-permute-start.4) | collective-permute-done | bytes 262176 | tf_op jit(solution)/shard_map/ppermute | solution.py:18
  53.0 0.0 copy-start.4
  53.1 0.7 copy-done.4
  53.7 0.0 all-gather.4.cloned.1.call-update
  53.8 0.0 copy-start.3
  53.8 13.8 %all-gather.6.cloned.1.call-done = bf16[2,1,1,128,4096]{4,3,2,1,0:T(8,128)(2,1)} async-done(((bf16[2,1,1,128,512]{4,3,2,1,0:T(8,128)(2,1)}), bf16[2,1,1,128,4096]{4,3,2,1,0:T(8,128)(2,1)}) %all-gather.6.cloned.1.call-update) | async-done | bytes 2097168 | tf_op jit(solution)/shard_map/all_gather | solution.py:49
  67.5 2.7 %slice_bitcast_fusion.1 = (bf16[128,4096]{1,0:T(8,128)(2,1)}, bf16[128,4096]{1,0:T(8,128)(2,1)S(1)}) fusion(bf16[2,1,1,128,4096]{4,3,2,1,0:T(8,128)(2,1)} %all-gather.6.cloned.1.call-done), kind=kLoop, calls=%fused_computation.18 | loop fusion | bytes 4194304 | tf_op jit(solution)/shard_map/squeeze | solution.py:52
  70.2 3.0 %collective-permute-start = (bf16[128,4096]{1,0:T(8,128)(2,1)}, bf16[128,4096]{1,0:T(8,128)(2,1)}, u32[]{:S(2)}, u32[]{:S(2)}) collective-permute-start(bf16[128,4096]{1,0:T(8,128)(2,1)} %get-tuple-element.11), channel_id=1, source_target_pairs={{16,0},{32,16},{48,32},{64,48},{80,64},{96,80},{112,96},{128,112},... | collective-permute-start | bytes 3145736 | tf_op jit(solution)/shard_map/ppermute | solution.py:12
  73.2 1.9 collective-permute-start.1
  75.2 0.0 copy-done.3
  75.2 0.7 reshape.98
  75.9 0.3 reduce-window.9
  76.2 0.1 slice.26
  76.3 0.1 slice_reduce_fusion
  76.5 0.1 add_bitcast_fusion
  76.5 0.6 slice.28
  77.1 0.6 iota_compare_fusion.1
  77.8 0.1 fusion.16
  77.8 0.1 convert_reduce_fusion
  78.0 0.1 fusion.13
  78.1 32.1 %collective-permute-done = bf16[128,4096]{1,0:T(8,128)(2,1)} collective-permute-done((bf16[128,4096]{1,0:T(8,128)(2,1)}, bf16[128,4096]{1,0:T(8,128)(2,1)}, u32[]{:S(2)}, u32[]{:S(2)}) %collective-permute-start) | collective-permute-done | bytes 1048608 | tf_op jit(solution)/shard_map/ppermute | solution.py:12
  110.1 4.4 %collective-permute-done.1 = bf16[128,4096]{1,0:T(8,128)(2,1)} collective-permute-done((bf16[128,4096]{1,0:T(8,128)(2,1)S(1)}, bf16[128,4096]{1,0:T(8,128)(2,1)}, u32[]{:S(2)}, u32[]{:S(2)}) %collective-permute-start.1) | collective-permute-done | bytes 1048608 | tf_op jit(solution)/shard_map/ppermute | solution.py:12
  114.6 1.7 pad_maximum_fusion
  116.3 0.5 copy.37
  116.8 9.1 %convert_bitcast_fusion.1 = bf16[32,14,128,128]{3,2,1,0:T(8,128)(2,1)} fusion(bf16[256,32,128,1]{2,1,0,3:T(8,128)(2,1)S(1)} %bitcast.57, bf16[256,14,128,1]{2,1,0,3:T(8,128)(2,1)S(1)} %bitcast.59), kind=kOutput, calls=%fused_computation.5 | convolution fusion | flops 3765436416 | bytes 17694720 | tf_op jit(solution)/shard_map/njd,nic->jidc/dot_general | solution.py:77
  125.9 7.5 %gather_fusion = bf16[63,128,128]{2,1,0:T(8,128)(2,1)} fusion(bf16[32,14,128,128]{3,2,1,0:T(8,128)(2,1)} %convert_bitcast_fusion.1, s32[63]{0:T(128)S(1)} %get-tuple-element.16), kind=kCustom, calls=%fused_computation | custom fusion | bytes 4129272 | tf_op jit(solution)/shard_map/gather | solution.py:86
  133.4 7.4 %gather_fusion.1 = bf16[63,128,128]{2,1,0:T(8,128)(2,1)} fusion(bf16[32,14,128,128]{3,2,1,0:T(8,128)(2,1)} %convert_bitcast_fusion.1, s32[63]{0:T(128)S(1)} %get-tuple-element.15), kind=kCustom, calls=%fused_computation.1 | custom fusion | bytes 4129272 | tf_op jit(solution)/shard_map/gather | solution.py:86
  140.8 3.9 %select_bitcast_fusion = (bf16[63,128,128]{1,2,0:T(8,128)(2,1)}, bf16[63,128,128]{1,2,0:T(8,128)(2,1)S(1)}) fusion(bf16[63,128,128]{2,1,0:T(8,128)(2,1)} %gather_fusion.1, pred[63]{0:T(512)(128)(4,1)S(1)} %get-tuple-element.19, bf16[63,128,128]{2,1,0:T(8,128)(2,1)} %gather_fusion, pred[63]{0:T(512)(128)(4,1)S(1)} %get-tuple-element.20), kind=kLoop, calls=%fused_computation.15 | loop fusion | flops 2064384 | bytes 8257662 | tf_op jit(solution)/shard_map/jit(_where)/select_n | solution.py:87
  144.7 0.0 all-gather.4.cloned.1.call-done
  144.7 2.1 copy.38
  146.7 0.0 collective-permute-done.5
  146.8 10.3 %convert_bitcast_fusion = bf16[32,14,128,128]{3,2,1,0:T(8,128)(2,1)} fusion(bf16[256,14,128,1]{0,2,1,3:T(8,128)(2,1)} %bitcast.19, bf16[256,32,128,1]{2,1,0,3:T(8,128)(2,1)S(1)} %bitcast.56), kind=kOutput, calls=%fused_computation.4 | convolution fusion | flops 3765436416 | bytes 17694720 | tf_op jit(solution)/shard_map/njd,nic->jidc/dot_general | solution.py:77
  157.1 7.4 %gather_fusion.3 = bf16[63,128,128]{2,1,0:T(8,128)(2,1)} fusion(bf16[32,14,128,128]{3,2,1,0:T(8,128)(2,1)} %convert_bitcast_fusion, s32[63]{0:T(128)S(1)} %get-tuple-element.16), kind=kCustom, calls=%fused_computation.3 | custom fusion | bytes 4129272 | tf_op jit(solution)/shard_map/gather | solution.py:86
  164.5 3.9 %fusion = bf16[63,128,128]{1,2,0:T(8,128)(2,1)} fusion(bf16[63,128,128]{1,2,0:T(8,128)(2,1)S(1)} %get-tuple-element.10, bf16[63,128,128]{2,1,0:T(8,128)(2,1)} %gather_fusion.3, pred[63]{0:T(512)(128)(4,1)S(1)} %get-tuple-element.20), kind=kLoop, calls=%fused_computation.7 | loop fusion | flops 5160960 | bytes 6193215 | tf_op jit(solution)/shard_map/convert_element_type | solution.py:97
  168.4 0.0 copy-start.2
  168.4 3.2 %collective-permute-start.6 = (bf16[63,128,128]{1,2,0:T(8,128)(2,1)}, bf16[63,128,128]{1,2,0:T(8,128)(2,1)}, u32[]{:S(2)}, u32[]{:S(2)}) collective-permute-start(bf16[63,128,128]{1,2,0:T(8,128)(2,1)} %fusion), channel_id=1, source_target_pairs={{0,1},{1,0},{2,3},{3,2},{4,5},{5,4},{6,7},{7,6},{8,9},{9,8},{10,11... | collective-permute-start | bytes 6193160 | tf_op jit(solution)/shard_map/ppermute | solution.py:18
  171.6 7.4 %gather_fusion.2 = bf16[63,128,128]{2,1,0:T(8,128)(2,1)} fusion(bf16[32,14,128,128]{3,2,1,0:T(8,128)(2,1)} %convert_bitcast_fusion, s32[63]{0:T(128)S(1)} %get-tuple-element.15), kind=kCustom, calls=%fused_computation.2 | custom fusion | bytes 4129272 | tf_op jit(solution)/shard_map/gather | solution.py:86
  179.1 17.3 %collective-permute-done.6 = bf16[63,128,128]{1,2,0:T(8,128)(2,1)} collective-permute-done((bf16[63,128,128]{1,2,0:T(8,128)(2,1)}, bf16[63,128,128]{1,2,0:T(8,128)(2,1)}, u32[]{:S(2)}, u32[]{:S(2)}) %collective-permute-start.6) | collective-permute-done | bytes 2064416 | tf_op jit(solution)/shard_map/ppermute | solution.py:18
  196.4 0.0 copy-done.2
  196.4 0.0 copy-start.1
  196.4 5.0 %fusion.4 = bf16[1,1,63,128,128]{3,4,2,1,0:T(8,128)(2,1)} fusion(bf16[63,128,128]{1,2,0:T(8,128)(2,1)} %collective-permute-done.6, bf16[63,128,128]{1,2,0:T(8,128)(2,1)S(1)} %copy-done.2, bf16[63,128,128]{2,1,0:T(8,128)(2,1)} %gather_fusion.2, pred[63]{0:T(512)(128)(4,1)S(1)} %get-tuple-element.19), kind=kLoop, calls=%fused_computation.14 | loop fusion | flops 9289728 | bytes 8257599 | tf_op jit(solution)/shard_map/reshape | solution.py:103
  201.4 4.1 %copy.21 = bf16[1,1,63,128,128]{4,3,2,1,0:T(8,128)(2,1)} copy(bf16[1,1,63,128,128]{3,4,2,1,0:T(8,128)(2,1)} %fusion.4) | data formatting | bytes 4128768 | tf_op jit(solution)/shard_map/reshape | solution.py:103
  205.5 0.0 copy-done.1
  (5 shorter events, 0.1 us)
Async XLA Ops:
  6.5 39.9 %copy-start = (s32[32,14,32]{2,0,1:T(8,128)S(1)}, s32[32,14,32]{2,0,1:T(8,128)}, u32[]{:S(2)}) copy-start(s32[32,14,32]{2,0,1:T(8,128)} %param.5) | copy-start | bytes 172036
  6.5 61.0 %all-gather.6.cloned.1.call-start = ((), (), s32[]{:S(2)}) async-start(), calls=%async_computation.1 | async-start | bytes 2359296 | tf_op jit(solution)/shard_map/all_gather | solution.py:49
  7.3 137.4 %all-gather.4.cloned.1.call-start = ((), (), s32[]{:S(2)}) async-start(), calls=%async_computation | async-start | bytes 2359296 | tf_op jit(solution)/shard_map/all_gather | solution.py:56
  8.3 20.6 %collective-permute-start.2 = (bf16[128,512]{1,0:T(8,128)(2,1)S(1)}, bf16[128,512]{1,0:T(8,128)(2,1)S(1)}, u32[]{:S(2)}, u32[]{:S(2)}) collective-permute-start(bf16[128,512]{1,0:T(8,128)(2,1)S(1)} %get-tuple-element.13), channel_id=1, source_target_pairs={{16,0},{32,16},{48,32},{64,48},{80,64},{96,80},{112,96},{128,112},... | collective-permute-start | bytes 393224 | tf_op jit(solution)/shard_map/ppermute | solution.py:12
  25.0 9.4 %collective-permute-start.3 = (bf16[128,512]{1,0:T(8,128)(2,1)S(1)}, bf16[128,512]{1,0:T(8,128)(2,1)S(1)}, u32[]{:S(2)}, u32[]{:S(2)}) collective-permute-start(bf16[128,512]{1,0:T(8,128)(2,1)S(1)} %get-tuple-element.14), channel_id=1, source_target_pairs={{1008,0},{0,16},{16,32},{32,48},{48,64},{64,80},{80,96},{96,112},{... | collective-permute-start | bytes 393224 | tf_op jit(solution)/shard_map/ppermute | solution.py:12
  34.4 18.6 %collective-permute-start.4 = (bf16[2,128,512]{2,1,0:T(8,128)(2,1)S(1)}, bf16[2,128,512]{2,1,0:T(8,128)(2,1)S(1)}, u32[]{:S(2)}, u32[]{:S(2)}) collective-permute-start(bf16[2,128,512]{2,1,0:T(8,128)(2,1)S(1)} %pad_maximum_fusion.1), channel_id=1, source_target_pairs={{0,512},{16,528},{32,544},{48,560},{64,576},{80,592},{96,608},{112... | collective-permute-start | bytes 786440 | tf_op jit(solution)/shard_map/ppermute | solution.py:18
  44.0 102.7 %collective-permute-start.5 = (bf16[256,1792]{0,1:T(8,128)(2,1)}, bf16[256,1792]{0,1:T(8,128)(2,1)}, u32[]{:S(2)}, u32[]{:S(2)}) collective-permute-start(bf16[256,1792]{0,1:T(8,128)(2,1)} %copy.35), channel_id=1, source_target_pairs={{0,512},{16,528},{32,544},{48,560},{64,576},{80,592},{96,608},{112... | collective-permute-start | bytes 2752520 | tf_op jit(solution)/shard_map/ppermute | solution.py:18
  53.0 0.7 copy-start.4
  53.8 21.5 %copy-start.3 = (bf16[2,1,1,128,1792]{4,3,2,1,0:T(8,128)(2,1)S(1)}, bf16[2,1,1,128,1792]{4,3,2,1,0:T(8,128)(2,1)}, u32[]{:S(2)}) copy-start(bf16[2,1,1,128,1792]{4,3,2,1,0:T(8,128)(2,1)} %param.3) | copy-start | bytes 2752516
  70.2 39.9 %collective-permute-start = (bf16[128,4096]{1,0:T(8,128)(2,1)}, bf16[128,4096]{1,0:T(8,128)(2,1)}, u32[]{:S(2)}, u32[]{:S(2)}) collective-permute-start(bf16[128,4096]{1,0:T(8,128)(2,1)} %get-tuple-element.11), channel_id=1, source_target_pairs={{16,0},{32,16},{48,32},{64,48},{80,64},{96,80},{112,96},{128,112},... | collective-permute-start | bytes 3145736 | tf_op jit(solution)/shard_map/ppermute | solution.py:12
  73.2 41.3 %collective-permute-start.1 = (bf16[128,4096]{1,0:T(8,128)(2,1)S(1)}, bf16[128,4096]{1,0:T(8,128)(2,1)}, u32[]{:S(2)}, u32[]{:S(2)}) collective-permute-start(bf16[128,4096]{1,0:T(8,128)(2,1)S(1)} %get-tuple-element.12), channel_id=1, source_target_pairs={{1008,0},{0,16},{16,32},{32,48},{48,64},{64,80},{80,96},{96,112},{... | collective-permute-start | bytes 3145736 | tf_op jit(solution)/shard_map/ppermute | solution.py:12
  168.4 28.0 %copy-start.2 = (bf16[63,128,128]{1,2,0:T(8,128)(2,1)S(1)}, bf16[63,128,128]{1,2,0:T(8,128)(2,1)}, u32[]{:S(2)}) copy-start(bf16[63,128,128]{1,2,0:T(8,128)(2,1)} %get-tuple-element.8) | copy-start | bytes 6193156
  168.4 28.0 %collective-permute-start.6 = (bf16[63,128,128]{1,2,0:T(8,128)(2,1)}, bf16[63,128,128]{1,2,0:T(8,128)(2,1)}, u32[]{:S(2)}, u32[]{:S(2)}) collective-permute-start(bf16[63,128,128]{1,2,0:T(8,128)(2,1)} %fusion), channel_id=1, source_target_pairs={{0,1},{1,0},{2,3},{3,2},{4,5},{5,4},{6,7},{7,6},{8,9},{9,8},{10,11... | collective-permute-start | bytes 6193160 | tf_op jit(solution)/shard_map/ppermute | solution.py:18
  196.4 9.1 %copy-start.1 = (s32[32,14,32]{2,0,1:T(8,128)S(1)}, s32[32,14,32]{2,0,1:T(8,128)}, u32[]{:S(2)}) copy-start(s32[32,14,32]{2,0,1:T(8,128)} %param.5) | copy-start | bytes 172036
Sparse Core Ops, SparseCore 0:
  10.0 57.4 all-gather.5
  70.2 46.0 all-gather.3

commit v5 on v4

--- a/solution.py
+++ b/solution.py
@@ -16,6 +16,15 @@
     mask = 2**apart
     pairs = [(source, source ^ mask) for source in range(lax.axis_size(axis))]
     return lax.ppermute(value, axis, pairs)
+
+
+def gathered_by_permutes(value, axis):
+    count = lax.axis_size(axis)
+    pieces = jnp.stack([value] + [passed_along(value, axis, shift) for shift in range(1, count)])
+    order = (lax.axis_index(axis) - jnp.arange(count, dtype=jnp.int32)) % count
+    placed = jnp.take(pieces, order, axis=0)
+    placed = jnp.moveaxis(placed, 0, -2)
+    return placed.reshape(placed.shape[:-2] + (count * value.shape[-1],))
 
 
 def slot_table(mask_local, slot_total):
@@ -46,14 +55,8 @@
     up_part = passed_along(incoming[1, 0, 0], "section", 1)
     own_arrived = jnp.stack([down_part, up_part])
     partner_arrived = from_partner(own_arrived, "section", swap_bit)
-    own_incoming_all = lax.all_gather(incoming[:, 0, 0], "tp", axis=2, tiled=True)
-    own_cot = jnp.stack(
-        [
-            passed_along(own_incoming_all[0], "section", -1),
-            passed_along(own_incoming_all[1], "section", 1),
-        ]
-    )
-    partner_cot = lax.all_gather(partner_arrived, "tp", axis=2, tiled=True)
+    own_cot = lax.all_gather(own_arrived, "tp", axis=2, tiled=True)
+    partner_cot = gathered_by_permutes(partner_arrived, "tp")
     d_total = own_cot.shape[2]
     ffb = ff_local // block_side
     db = d_total // block_side

time: 213 us -> 304 us (1.43)
  the two profiles are of different devices: /device:TPU:4 before, /device:TPU:148 now
where the time goes in v5:
time: 304 us; the launch traced here: 303 us
  waiting for transfers between devices  127 us (42%)
  local copies, waits for them, and re-layouts  74.3 us (24%)
  starting transfers between devices  52.9 us (17%)
  matrix products  17.6 us (6%)
  other arithmetic  17.1 us (6%)
  between operations  13.7 us (5%)
    ppermute x3, waiting for transfers between devices, from_partner(): return lax.ppermute(value, axis, pairs)  86.9 us
    ppermute x9, starting transfers between devices, passed_along(): return lax.ppermute(block, axis, route)  41.1 us
    ppermute x9, waiting for transfers between devices, passed_along(): return lax.ppermute(block, axis, route)  40.3 us
    gather x4, local copies, waits for them, and re-layouts, blocks_of(): picked = jnp.swapaxes(dense[cols_q, rows_q], 1, 2)  29.9 us
    reshape x2, local copies, waits for them, and re-layouts, partial_of(): cot_rows.reshape(-1, db, block_side)  21.2 us
    dot_general x2, matrix products, partial_of(): jnp.einsum('njd,nic->jidc', cot_rows.reshape(-1, db, block_side), hidden_...  17.6 us
    ppermute x3, starting transfers between devices, from_partner(): return lax.ppermute(value, axis, pairs)  11.8 us
    unnamed x18, local copies, waits for them, and re-layouts  8.09 us
  transfers between devices with their start and end apart: 13, of which 6 were waited for; matrix products, arithmetic and copies ran while one was open for 26% of the time, Pallas kernels for 0%

profile of v5, /device:TPU:148, one launch (start us, length us, event | category | flops | bytes accessed | tf_op | source)
XLA Modules:
  0.0 302.9 jit_solution(11032653112085812793)
XLA Ops:
  6.5 1.1 slice_bitcast_fusion.1
  7.6 1.9 collective-permute-start
  9.6 2.4 collective-permute-start.1
  12.0 2.2 copy.43
  14.2 5.6 %collective-permute-start.10 = (bf16[256,1792]{0,1:T(8,128)(2,1)}, bf16[256,1792]{0,1:T(8,128)(2,1)}, u32[]{:S(2)}, u32[]{:S(2)}) collective-permute-start(bf16[256,1792]{0,1:T(8,128)(2,1)} %copy.43), channel_id=1, source_target_pairs={{0,512},{16,528},{32,544},{48,560},{64,576},{80,592},{96,608},{112... | collective-permute-start | bytes 2752520 | tf_op jit(solution)/shard_map/ppermute | solution.py:18
  19.9 0.1 reshape.90
  19.9 0.0 collective-permute-done
  19.9 0.0 collective-permute-done.1
  19.9 0.7 pad_maximum_fusion
  20.7 0.0 all-gather.2.cloned.1.call-update
  20.7 0.3 reduce-window.9
  21.0 0.1 slice.20
  21.1 0.1 slice_reduce_fusion
  21.2 0.1 add_bitcast_fusion
  21.3 0.7 slice.22
  22.0 0.7 iota_compare_fusion.1
  22.7 0.1 fusion.19
  22.7 0.1 convert_reduce_fusion
  22.9 4.2 %collective-permute-start.2 = (bf16[2,128,512]{2,1,0:T(8,128)(2,1)}, bf16[2,128,512]{2,1,0:T(8,128)(2,1)S(1)}, u32[]{:S(2)}, u32[]{:S(2)}) collective-permute-start(bf16[2,128,512]{2,1,0:T(8,128)(2,1)} %pad_maximum_fusion), channel_id=1, source_target_pairs={{0,512},{16,528},{32,544},{48,560},{64,576},{80,592},{96,608},{112... | collective-permute-start | bytes 786440 | tf_op jit(solution)/shard_map/ppermute | solution.py:18
  27.1 0.1 fusion.15
  27.2 47.2 %collective-permute-done.2 = bf16[2,128,512]{2,1,0:T(8,128)(2,1)S(1)} collective-permute-done((bf16[2,128,512]{2,1,0:T(8,128)(2,1)}, bf16[2,128,512]{2,1,0:T(8,128)(2,1)S(1)}, u32[]{:S(2)}, u32[]{:S(2)}) %collective-permute-start.2) | collective-permute-done | bytes 262176 | tf_op jit(solution)/shard_map/ppermute | solution.py:18
  74.4 3.6 %collective-permute-start.3 = (bf16[2,128,512]{2,1,0:T(8,128)(2,1)S(1)}, bf16[2,128,512]{2,1,0:T(8,128)(2,1)}, u32[]{:S(2)}, u32[]{:S(2)}) collective-permute-start(bf16[2,128,512]{2,1,0:T(8,128)(2,1)S(1)} %collective-permute-done.2), channel_id=1, source_target_pairs={{14,0},{0,2},{2,4},{4,6},{6,8},{8,10},{10,12},{12,14},{15,1},{1,3}... | collective-permute-start | bytes 786440 | tf_op jit(solution)/shard_map/ppermute | solution.py:12
  78.0 0.7 reshape.159
  78.7 5.9 %collective-permute-start.4 = (bf16[2,128,512]{2,1,0:T(8,128)(2,1)S(1)}, bf16[2,128,512]{2,1,0:T(8,128)(2,1)S(1)}, u32[]{:S(2)}, u32[]{:S(2)}) collective-permute-start(bf16[2,128,512]{2,1,0:T(8,128)(2,1)S(1)} %collective-permute-done.2), channel_id=1, source_target_pairs={{12,0},{14,2},{0,4},{2,6},{4,8},{6,10},{8,12},{10,14},{13,1},{15,3... | collective-permute-start | bytes 786440 | tf_op jit(solution)/shard_map/ppermute | solution.py:12
  84.7 0.7 bitcast_dynamic-update-slice_fusion.7
  85.4 3.1 %collective-permute-start.5 = (bf16[2,128,512]{2,1,0:T(8,128)(2,1)S(1)}, bf16[2,128,512]{2,1,0:T(8,128)(2,1)S(1)}, u32[]{:S(2)}, u32[]{:S(2)}) collective-permute-start(bf16[2,128,512]{2,1,0:T(8,128)(2,1)S(1)} %collective-permute-done.2), channel_id=1, source_target_pairs={{10,0},{12,2},{14,4},{0,6},{2,8},{4,10},{6,12},{8,14},{11,1},{13,3... | collective-permute-start | bytes 786440 | tf_op jit(solution)/shard_map/ppermute | solution.py:12
  88.5 4.3 %collective-permute-start.6 = (bf16[2,128,512]{2,1,0:T(8,128)(2,1)S(1)}, bf16[2,128,512]{2,1,0:T(8,128)(2,1)S(1)}, u32[]{:S(2)}, u32[]{:S(2)}) collective-permute-start(bf16[2,128,512]{2,1,0:T(8,128)(2,1)S(1)} %collective-permute-done.2), channel_id=1, source_target_pairs={{8,0},{10,2},{12,4},{14,6},{0,8},{2,10},{4,12},{6,14},{9,1},{11,3}... | collective-permute-start | bytes 786440 | tf_op jit(solution)/shard_map/ppermute | solution.py:12
  92.8 0.0 collective-permute-done.3
  92.8 4.0 %collective-permute-start.7 = (bf16[2,128,512]{2,1,0:T(8,128)(2,1)S(1)}, bf16[2,128,512]{2,1,0:T(8,128)(2,1)S(1)}, u32[]{:S(2)}, u32[]{:S(2)}) collective-permute-start(bf16[2,128,512]{2,1,0:T(8,128)(2,1)S(1)} %collective-permute-done.2), channel_id=1, source_target_pairs={{6,0},{8,2},{10,4},{12,6},{14,8},{0,10},{2,12},{4,14},{7,1},{9,3},... | collective-permute-start | bytes 786440 | tf_op jit(solution)/shard_map/ppermute | solution.py:12
  96.8 1.7 bitcast_dynamic-update-slice_fusion.6
  98.5 5.4 %collective-permute-done.4 = bf16[2,128,512]{2,1,0:T(8,128)(2,1)S(1)} collective-permute-done((bf16[2,128,512]{2,1,0:T(8,128)(2,1)S(1)}, bf16[2,128,512]{2,1,0:T(8,128)(2,1)S(1)}, u32[]{:S(2)}, u32[]{:S(2)}) %collective-permute-start.4) | collective-permute-done | bytes 262176 | tf_op jit(solution)/shard_map/ppermute | solution.py:12
  103.9 9.0 %collective-permute-start.8 = (bf16[2,128,512]{2,1,0:T(8,128)(2,1)S(1)}, bf16[2,128,512]{2,1,0:T(8,128)(2,1)S(1)}, u32[]{:S(2)}, u32[]{:S(2)}) collective-permute-start(bf16[2,128,512]{2,1,0:T(8,128)(2,1)S(1)} %collective-permute-done.2), channel_id=1, source_target_pairs={{4,0},{6,2},{8,4},{10,6},{12,8},{14,10},{0,12},{2,14},{5,1},{7,3},... | collective-permute-start | bytes 786440 | tf_op jit(solution)/shard_map/ppermute | solution.py:12
  113.0 0.7 bitcast_dynamic-update-slice_fusion.5
  113.7 12.0 %collective-permute-done.5 = bf16[2,128,512]{2,1,0:T(8,128)(2,1)S(1)} collective-permute-done((bf16[2,128,512]{2,1,0:T(8,128)(2,1)S(1)}, bf16[2,128,512]{2,1,0:T(8,128)(2,1)S(1)}, u32[]{:S(2)}, u32[]{:S(2)}) %collective-permute-start.5) | collective-permute-done | bytes 262176 | tf_op jit(solution)/shard_map/ppermute | solution.py:12
  125.7 6.8 %collective-permute-start.9 = (bf16[2,128,512]{2,1,0:T(8,128)(2,1)S(1)}, bf16[2,128,512]{2,1,0:T(8,128)(2,1)S(1)}, u32[]{:S(2)}, u32[]{:S(2)}) collective-permute-start(bf16[2,128,512]{2,1,0:T(8,128)(2,1)S(1)} %collective-permute-done.2), channel_id=1, source_target_pairs={{2,0},{4,2},{6,4},{8,6},{10,8},{12,10},{14,12},{0,14},{3,1},{5,3},... | collective-permute-start | bytes 786440 | tf_op jit(solution)/shard_map/ppermute | solution.py:12
  132.5 0.7 bitcast_dynamic-update-slice_fusion.4
  133.2 0.0 collective-permute-done.6
  133.2 0.7 bitcast_dynamic-update-slice_fusion.3
  133.9 0.0 collective-permute-done.7
  133.9 0.7 bitcast_dynamic-update-slice_fusion.2
  134.7 14.5 %collective-permute-done.8 = bf16[2,128,512]{2,1,0:T(8,128)(2,1)S(1)} collective-permute-done((bf16[2,128,512]{2,1,0:T(8,128)(2,1)S(1)}, bf16[2,128,512]{2,1,0:T(8,128)(2,1)S(1)}, u32[]{:S(2)}, u32[]{:S(2)}) %collective-permute-start.8) | collective-permute-done | bytes 262176 | tf_op jit(solution)/shard_map/ppermute | solution.py:12
  149.1 0.7 bitcast_dynamic-update-slice_fusion.1
  149.9 8.4 %collective-permute-done.9 = bf16[2,128,512]{2,1,0:T(8,128)(2,1)S(1)} collective-permute-done((bf16[2,128,512]{2,1,0:T(8,128)(2,1)S(1)}, bf16[2,128,512]{2,1,0:T(8,128)(2,1)S(1)}, u32[]{:S(2)}, u32[]{:S(2)}) %collective-permute-start.9) | collective-permute-done | bytes 262176 | tf_op jit(solution)/shard_map/ppermute | solution.py:12
  158.3 0.7 bitcast_dynamic-update-slice_fusion
  159.0 2.3 gather_fusion.2
  161.3 1.6 select_bitcast_fusion
  162.9 3.0 %copy.25 = bf16[2,128,8,512]{1,3,2,0:T(8,128)(2,1)S(1)} copy(bf16[2,128,8,512]{3,1,0,2:T(8,128)(2,1)} %select_bitcast_fusion) | data formatting | bytes 4194304 | tf_op jit(solution)/shard_map/jit(_take)/select_n | solution.py:25
  165.9 0.0 all-gather.2.cloned.1.call-done
  165.9 2.1 copy.46
  168.0 9.1 %convert_bitcast_fusion.1 = bf16[32,14,128,128]{3,2,1,0:T(8,128)(2,1)} fusion(bf16[256,32,128,1]{2,1,0,3:T(8,128)(2,1)S(1)} %bitcast.71, bf16[256,14,128,1]{2,1,0,3:T(8,128)(2,1)S(1)} %bitcast.73), kind=kOutput, calls=%fused_computation.6 | convolution fusion | flops 3765436416 | bytes 17694720 | tf_op jit(solution)/shard_map/njd,nic->jidc/dot_general | solution.py:80
  177.1 7.4 %gather_fusion = bf16[63,128,128]{2,1,0:T(8,128)(2,1)} fusion(bf16[32,14,128,128]{3,2,1,0:T(8,128)(2,1)} %convert_bitcast_fusion.1, s32[63]{0:T(128)S(1)} %get-tuple-element.14), kind=kCustom, calls=%fused_computation | custom fusion | bytes 4129272 | tf_op jit(solution)/shard_map/gather | solution.py:89
  184.5 7.4 %gather_fusion.1 = bf16[63,128,128]{2,1,0:T(8,128)(2,1)} fusion(bf16[32,14,128,128]{3,2,1,0:T(8,128)(2,1)} %convert_bitcast_fusion.1, s32[63]{0:T(128)S(1)} %get-tuple-element.13), kind=kCustom, calls=%fused_computation.1 | custom fusion | bytes 4129272 | tf_op jit(solution)/shard_map/gather | solution.py:89
  192.0 4.5 %select_bitcast_fusion.1 = (bf16[63,128,128]{1,2,0:T(8,128)(2,1)}, bf16[63,128,128]{1,2,0:T(8,128)(2,1)}) fusion(bf16[63,128,128]{2,1,0:T(8,128)(2,1)} %gather_fusion.1, pred[63]{0:T(512)(128)(4,1)S(1)} %get-tuple-element.17, bf16[63,128,128]{2,1,0:T(8,128)(2,1)} %gather_fusion, pred[63]{0:T(512)(128)(4,1)S(1)} %get-tuple-element.18), kind=kLoop, calls=%fused_computation.16 | loop fusion | flops 2064384 | bytes 8257662 | tf_op jit(solution)/shard_map/jit(_where)/select_n | solution.py:90
  196.5 18.1 %copy.42 = bf16[2,128,4096]{1,0,2:T(2,128)(2,1)} copy(bf16[2,128,4096]{1,2,0:T(8,128)(2,1)S(1)} %bitcast.72) | data formatting | bytes 4194304 | tf_op jit(solution)/shard_map/reshape | solution.py:82
  214.6 3.2 %reshape.156 = bf16[256,32,128,1]{0,2,1,3:T(8,128)(2,1)S(1)} reshape(bf16[2,128,4096]{1,0,2:T(2,128)(2,1)} %copy.42) | data formatting | bytes 4194304 | tf_op jit(solution)/shard_map/reshape | solution.py:82
  217.7 0.0 collective-permute-done.10
  217.8 8.5 %convert_bitcast_fusion = bf16[32,14,128,128]{3,2,1,0:T(8,128)(2,1)} fusion(bf16[256,14,128,1]{0,2,1,3:T(8,128)(2,1)} %bitcast.26, bf16[256,32,128,1]{0,2,1,3:T(8,128)(2,1)S(1)} %reshape.156), kind=kOutput, calls=%fused_computation.5 | convolution fusion | flops 3765436416 | bytes 17694720 | tf_op jit(solution)/shard_map/njd,nic->jidc/dot_general | solution.py:80
  226.2 7.6 %gather_fusion.4 = bf16[63,128,128]{2,1,0:T(8,128)(2,1)} fusion(bf16[32,14,128,128]{3,2,1,0:T(8,128)(2,1)} %convert_bitcast_fusion, s32[63]{0:T(128)S(1)} %get-tuple-element.14), kind=kCustom, calls=%fused_computation.4 | custom fusion | bytes 4129272 | tf_op jit(solution)/shard_map/gather | solution.py:89
  233.8 3.9 %fusion = bf16[63,128,128]{1,2,0:T(8,128)(2,1)} fusion(bf16[63,128,128]{1,2,0:T(8,128)(2,1)S(1)} %copy-done.2, bf16[63,128,128]{2,1,0:T(8,128)(2,1)} %gather_fusion.4, pred[63]{0:T(512)(128)(4,1)S(1)} %get-tuple-element.18), kind=kLoop, calls=%fused_computation.8 | loop fusion | flops 5160960 | bytes 6193215 | tf_op jit(solution)/shard_map/convert_element_type | solution.py:100
  237.7 2.0 collective-permute-start.11
  239.7 7.5 %gather_fusion.3 = bf16[63,128,128]{2,1,0:T(8,128)(2,1)} fusion(bf16[32,14,128,128]{3,2,1,0:T(8,128)(2,1)} %convert_bitcast_fusion, s32[63]{0:T(128)S(1)} %get-tuple-element.13), kind=kCustom, calls=%fused_computation.3 | custom fusion | bytes 4129272 | tf_op jit(solution)/shard_map/gather | solution.py:89
  247.2 39.7 %collective-permute-done.11 = bf16[63,128,128]{1,2,0:T(8,128)(2,1)} collective-permute-done((bf16[63,128,128]{1,2,0:T(8,128)(2,1)}, bf16[63,128,128]{1,2,0:T(8,128)(2,1)}, u32[]{:S(2)}, u32[]{:S(2)}) %collective-permute-start.11) | collective-permute-done | bytes 2064416 | tf_op jit(solution)/shard_map/ppermute | solution.py:18
  286.9 5.0 %fusion.4 = bf16[1,1,63,128,128]{3,4,2,1,0:T(8,128)(2,1)} fusion(bf16[63,128,128]{1,2,0:T(8,128)(2,1)} %collective-permute-done.11, bf16[63,128,128]{1,2,0:T(8,128)(2,1)S(1)} %copy-done.3, bf16[63,128,128]{2,1,0:T(8,128)(2,1)} %gather_fusion.3, pred[63]{0:T(512)(128)(4,1)S(1)} %get-tuple-element.17), kind=kLoop, calls=%fused_computation.15 | loop fusion | flops 9289728 | bytes 8257599 | tf_op jit(solution)/shard_map/reshape | solution.py:106
  292.0 4.1 %copy.30 = bf16[1,1,63,128,128]{4,3,2,1,0:T(8,128)(2,1)} copy(bf16[1,1,63,128,128]{3,4,2,1,0:T(8,128)(2,1)} %fusion.4) | data formatting | bytes 4128768 | tf_op jit(solution)/shard_map/reshape | solution.py:106
  (18 shorter events, 0.1 us)
Async XLA Ops:
  6.5 13.3 %copy-start = (s32[32,14,32]{2,0,1:T(8,128)S(1)}, s32[32,14,32]{2,0,1:T(8,128)}, u32[]{:S(2)}) copy-start(s32[32,14,32]{2,0,1:T(8,128)} %param.5) | copy-start | bytes 172036
  6.5 71.5 %copy-start.4 = (bf16[2,1,1,128,1792]{4,3,2,1,0:T(8,128)(2,1)S(1)}, bf16[2,1,1,128,1792]{4,3,2,1,0:T(8,128)(2,1)}, u32[]{:S(2)}) copy-start(bf16[2,1,1,128,1792]{4,3,2,1,0:T(8,128)(2,1)} %param.3) | copy-start | bytes 2752516
  6.5 159.4 %all-gather.2.cloned.1.call-start = ((), (), s32[]{:S(2)}) async-start(), calls=%async_computation | async-start | bytes 2359296 | tf_op jit(solution)/shard_map/all_gather | solution.py:58
  7.6 12.3 %collective-permute-start = (bf16[128,512]{1,0:T(8,128)(2,1)S(1)}, bf16[128,512]{1,0:T(8,128)(2,1)S(1)}, u32[]{:S(2)}, u32[]{:S(2)}) collective-permute-start(bf16[128,512]{1,0:T(8,128)(2,1)S(1)} %get-tuple-element.11), channel_id=1, source_target_pairs={{16,0},{32,16},{48,32},{64,48},{80,64},{96,80},{112,96},{128,112},... | collective-permute-start | bytes 393224 | tf_op jit(solution)/shard_map/ppermute | solution.py:12
  9.6 10.4 %collective-permute-start.1 = (bf16[128,512]{1,0:T(8,128)(2,1)S(1)}, bf16[128,512]{1,0:T(8,128)(2,1)S(1)}, u32[]{:S(2)}, u32[]{:S(2)}) collective-permute-start(bf16[128,512]{1,0:T(8,128)(2,1)S(1)} %get-tuple-element.12), channel_id=1, source_target_pairs={{1008,0},{0,16},{16,32},{32,48},{48,64},{64,80},{80,96},{96,112},{... | collective-permute-start | bytes 393224 | tf_op jit(solution)/shard_map/ppermute | solution.py:12
  14.2 203.6 %collective-permute-start.10 = (bf16[256,1792]{0,1:T(8,128)(2,1)}, bf16[256,1792]{0,1:T(8,128)(2,1)}, u32[]{:S(2)}, u32[]{:S(2)}) collective-permute-start(bf16[256,1792]{0,1:T(8,128)(2,1)} %copy.43), channel_id=1, source_target_pairs={{0,512},{16,528},{32,544},{48,560},{64,576},{80,592},{96,608},{112... | collective-permute-start | bytes 2752520 | tf_op jit(solution)/shard_map/ppermute | solution.py:18
  22.9 51.5 %collective-permute-start.2 = (bf16[2,128,512]{2,1,0:T(8,128)(2,1)}, bf16[2,128,512]{2,1,0:T(8,128)(2,1)S(1)}, u32[]{:S(2)}, u32[]{:S(2)}) collective-permute-start(bf16[2,128,512]{2,1,0:T(8,128)(2,1)} %pad_maximum_fusion), channel_id=1, source_target_pairs={{0,512},{16,528},{32,544},{48,560},{64,576},{80,592},{96,608},{112... | collective-permute-start | bytes 786440 | tf_op jit(solution)/shard_map/ppermute | solution.py:18
  74.4 18.4 %collective-permute-start.3 = (bf16[2,128,512]{2,1,0:T(8,128)(2,1)S(1)}, bf16[2,128,512]{2,1,0:T(8,128)(2,1)}, u32[]{:S(2)}, u32[]{:S(2)}) collective-permute-start(bf16[2,128,512]{2,1,0:T(8,128)(2,1)S(1)} %collective-permute-done.2), channel_id=1, source_target_pairs={{14,0},{0,2},{2,4},{4,6},{6,8},{8,10},{10,12},{12,14},{15,1},{1,3}... | collective-permute-start | bytes 786440 | tf_op jit(solution)/shard_map/ppermute | solution.py:12
  78.7 25.2 %collective-permute-start.4 = (bf16[2,128,512]{2,1,0:T(8,128)(2,1)S(1)}, bf16[2,128,512]{2,1,0:T(8,128)(2,1)S(1)}, u32[]{:S(2)}, u32[]{:S(2)}) collective-permute-start(bf16[2,128,512]{2,1,0:T(8,128)(2,1)S(1)} %collective-permute-done.2), channel_id=1, source_target_pairs={{12,0},{14,2},{0,4},{2,6},{4,8},{6,10},{8,12},{10,14},{13,1},{15,3... | collective-permute-start | bytes 786440 | tf_op jit(solution)/shard_map/ppermute | solution.py:12
  85.4 40.3 %collective-permute-start.5 = (bf16[2,128,512]{2,1,0:T(8,128)(2,1)S(1)}, bf16[2,128,512]{2,1,0:T(8,128)(2,1)S(1)}, u32[]{:S(2)}, u32[]{:S(2)}) collective-permute-start(bf16[2,128,512]{2,1,0:T(8,128)(2,1)S(1)} %collective-permute-done.2), channel_id=1, source_target_pairs={{10,0},{12,2},{14,4},{0,6},{2,8},{4,10},{6,12},{8,14},{11,1},{13,3... | collective-permute-start | bytes 786440 | tf_op jit(solution)/shard_map/ppermute | solution.py:12
  88.5 44.7 %collective-permute-start.6 = (bf16[2,128,512]{2,1,0:T(8,128)(2,1)S(1)}, bf16[2,128,512]{2,1,0:T(8,128)(2,1)S(1)}, u32[]{:S(2)}, u32[]{:S(2)}) collective-permute-start(bf16[2,128,512]{2,1,0:T(8,128)(2,1)S(1)} %collective-permute-done.2), channel_id=1, source_target_pairs={{8,0},{10,2},{12,4},{14,6},{0,8},{2,10},{4,12},{6,14},{9,1},{11,3}... | collective-permute-start | bytes 786440 | tf_op jit(solution)/shard_map/ppermute | solution.py:12
  92.8 41.1 %collective-permute-start.7 = (bf16[2,128,512]{2,1,0:T(8,128)(2,1)S(1)}, bf16[2,128,512]{2,1,0:T(8,128)(2,1)S(1)}, u32[]{:S(2)}, u32[]{:S(2)}) collective-permute-start(bf16[2,128,512]{2,1,0:T(8,128)(2,1)S(1)} %collective-permute-done.2), channel_id=1, source_target_pairs={{6,0},{8,2},{10,4},{12,6},{14,8},{0,10},{2,12},{4,14},{7,1},{9,3},... | collective-permute-start | bytes 786440 | tf_op jit(solution)/shard_map/ppermute | solution.py:12
  103.9 45.2 %collective-permute-start.8 = (bf16[2,128,512]{2,1,0:T(8,128)(2,1)S(1)}, bf16[2,128,512]{2,1,0:T(8,128)(2,1)S(1)}, u32[]{:S(2)}, u32[]{:S(2)}) collective-permute-start(bf16[2,128,512]{2,1,0:T(8,128)(2,1)S(1)} %collective-permute-done.2), channel_id=1, source_target_pairs={{4,0},{6,2},{8,4},{10,6},{12,8},{14,10},{0,12},{2,14},{5,1},{7,3},... | collective-permute-start | bytes 786440 | tf_op jit(solution)/shard_map/ppermute | solution.py:12
  125.7 32.6 %collective-permute-start.9 = (bf16[2,128,512]{2,1,0:T(8,128)(2,1)S(1)}, bf16[2,128,512]{2,1,0:T(8,128)(2,1)S(1)}, u32[]{:S(2)}, u32[]{:S(2)}) collective-permute-start(bf16[2,128,512]{2,1,0:T(8,128)(2,1)S(1)} %collective-permute-done.2), channel_id=1, source_target_pairs={{2,0},{4,2},{6,4},{8,6},{10,8},{12,10},{14,12},{0,14},{3,1},{5,3},... | collective-permute-start | bytes 786440 | tf_op jit(solution)/shard_map/ppermute | solution.py:12
  226.2 7.6 %copy-start.2 = (bf16[63,128,128]{1,2,0:T(8,128)(2,1)S(1)}, bf16[63,128,128]{1,2,0:T(8,128)(2,1)}, u32[]{:S(2)}) copy-start(bf16[63,128,128]{1,2,0:T(8,128)(2,1)} %get-tuple-element.10) | copy-start | bytes 6193156
  237.7 49.3 %copy-start.3 = (bf16[63,128,128]{1,2,0:T(8,128)(2,1)S(1)}, bf16[63,128,128]{1,2,0:T(8,128)(2,1)}, u32[]{:S(2)}) copy-start(bf16[63,128,128]{1,2,0:T(8,128)(2,1)} %get-tuple-element.8) | copy-start | bytes 6193156
  237.7 49.2 %collective-permute-start.11 = (bf16[63,128,128]{1,2,0:T(8,128)(2,1)}, bf16[63,128,128]{1,2,0:T(8,128)(2,1)}, u32[]{:S(2)}, u32[]{:S(2)}) collective-permute-start(bf16[63,128,128]{1,2,0:T(8,128)(2,1)} %fusion), channel_id=1, source_target_pairs={{0,1},{1,0},{2,3},{3,2},{4,5},{5,4},{6,7},{7,6},{8,9},{9,8},{10,11... | collective-permute-start | bytes 6193160 | tf_op jit(solution)/shard_map/ppermute | solution.py:18
  286.9 9.1 %copy-start.1 = (s32[32,14,32]{2,0,1:T(8,128)S(1)}, s32[32,14,32]{2,0,1:T(8,128)}, u32[]{:S(2)}) copy-start(s32[32,14,32]{2,0,1:T(8,128)} %param.5) | copy-start | bytes 172036
Sparse Core Ops, SparseCore 0:
  20.8 137.9 all-gather.1

commit v6 on v5

--- a/solution.py
+++ b/solution.py
@@ -16,15 +16,6 @@
     mask = 2**apart
     pairs = [(source, source ^ mask) for source in range(lax.axis_size(axis))]
     return lax.ppermute(value, axis, pairs)
-
-
-def gathered_by_permutes(value, axis):
-    count = lax.axis_size(axis)
-    pieces = jnp.stack([value] + [passed_along(value, axis, shift) for shift in range(1, count)])
-    order = (lax.axis_index(axis) - jnp.arange(count, dtype=jnp.int32)) % count
-    placed = jnp.take(pieces, order, axis=0)
-    placed = jnp.moveaxis(placed, 0, -2)
-    return placed.reshape(placed.shape[:-2] + (count * value.shape[-1],))
 
 
 def slot_table(mask_local, slot_total):
@@ -56,7 +47,9 @@
     own_arrived = jnp.stack([down_part, up_part])
     partner_arrived = from_partner(own_arrived, "section", swap_bit)
     own_cot = lax.all_gather(own_arrived, "tp", axis=2, tiled=True)
-    partner_cot = gathered_by_permutes(partner_arrived, "tp")
+    partner_down = lax.all_gather(partner_arrived[0], "tp", axis=1, tiled=True)
+    partner_up = from_partner(own_cot[1], "section", swap_bit)
+    partner_cot = jnp.stack([partner_down, partner_up])
     d_total = own_cot.shape[2]
     ffb = ff_local // block_side
     db = d_total // block_side

time: 304 us -> 230 us (0.76)
  the two profiles are of different devices: /device:TPU:148 before, /device:TPU:1 now
where the time goes in v6:
time: 230 us; the launch traced here: 229 us
  waiting for transfers between devices  102 us (44%)
  local copies, waits for them, and re-layouts  42.3 us (18%)
  starting transfers between devices  34.9 us (15%)
  matrix products  19.5 us (8%)
  other arithmetic  16.5 us (7%)
  between operations  13.6 us (6%)
    ppermute x4, waiting for transfers between devices, from_partner(): return lax.ppermute(value, axis, pairs)  91 us
    gather x4, local copies, waits for them, and re-layouts, blocks_of(): picked = jnp.swapaxes(dense[cols_q, rows_q], 1, 2)  29.8 us
    dot_general x2, matrix products, partial_of(): jnp.einsum('njd,nic->jidc', cot_rows.reshape(-1, db, block_side), hidden_...  19.5 us
    ppermute x2, starting transfers between devices, passed_along(): return lax.ppermute(block, axis, route)  18 us
    ppermute x4, starting transfers between devices, from_partner(): return lax.ppermute(value, axis, pairs)  16.9 us
    ppermute x2, waiting for transfers between devices, passed_along(): return lax.ppermute(block, axis, route)  6.18 us
    all_gather x1, waiting for transfers between devices, body(): partner_down = lax.all_gather(partner_arrived[0], 'tp', axis=1, tiled=True)  5.11 us
    reshape x1, other arithmetic, body(): return summed.reshape(1, 1, -1, block_side, block_side)  4.98 us
  transfers between devices with their start and end apart: 8, of which 5 were waited for; matrix products, arithmetic and copies ran while one was open for 20% of the time, Pallas kernels for 0%

profile of v6, /device:TPU:1, one launch (start us, length us, event | category | flops | bytes accessed | tf_op | source)
XLA Modules:
  0.0 229.2 jit_solution(12040676200778659937)
XLA Ops:
  6.5 0.0 copy-start
  6.5 0.0 copy-start.3
  6.5 0.0 all-gather.4.cloned.1.call-start
  6.5 1.1 slice_bitcast_fusion.2
  7.6 16.1 %collective-permute-start = (bf16[128,512]{1,0:T(8,128)(2,1)S(1)}, bf16[128,512]{1,0:T(8,128)(2,1)S(1)}, u32[]{:S(2)}, u32[]{:S(2)}) collective-permute-start(bf16[128,512]{1,0:T(8,128)(2,1)S(1)} %get-tuple-element.11), channel_id=1, source_target_pairs={{16,0},{32,16},{48,32},{64,48},{80,64},{96,80},{112,96},{128,112},... | collective-permute-start | bytes 393224 | tf_op jit(solution)/shard_map/ppermute | solution.py:12
  23.7 1.9 collective-permute-start.1
  25.6 0.0 collective-permute-done
  25.6 6.2 %collective-permute-done.1 = bf16[128,512]{1,0:T(8,128)(2,1)S(1)} collective-permute-done((bf16[128,512]{1,0:T(8,128)(2,1)S(1)}, bf16[128,512]{1,0:T(8,128)(2,1)S(1)}, u32[]{:S(2)}, u32[]{:S(2)}) %collective-permute-start.1) | collective-permute-done | bytes 131104 | tf_op jit(solution)/shard_map/ppermute | solution.py:12
  31.8 0.7 pad_maximum_fusion.1
  32.5 0.0 copy-start.4
  32.5 0.0 all-gather.4.cloned.1.call-update
  32.6 0.0 all-gather.6.cloned.1.call-start
  32.6 2.2 copy.35
  34.8 3.9 %collective-permute-start.4 = (bf16[256,1792]{0,1:T(8,128)(2,1)}, bf16[256,1792]{0,1:T(8,128)(2,1)}, u32[]{:S(2)}, u32[]{:S(2)}) collective-permute-start(bf16[256,1792]{0,1:T(8,128)(2,1)} %copy.35), channel_id=1, source_target_pairs={{0,512},{16,528},{32,544},{48,560},{64,576},{80,592},{96,608},{112... | collective-permute-start | bytes 2752520 | tf_op jit(solution)/shard_map/ppermute | solution.py:18
  38.7 0.0 copy-done
  38.8 0.1 reshape.33
  38.8 0.3 reduce-window.9
  39.2 0.1 slice.26
  39.3 0.1 slice_reduce_fusion
  39.4 0.1 add_bitcast_fusion
  39.5 0.7 slice.28
  40.1 0.1 convert_reduce_fusion
  40.3 0.0 copy-done.4
  40.3 5.3 %collective-permute-start.2 = (bf16[2,128,512]{2,1,0:T(8,128)(2,1)S(1)}, bf16[2,128,512]{2,1,0:T(8,128)(2,1)S(1)}, u32[]{:S(2)}, u32[]{:S(2)}) collective-permute-start(bf16[2,128,512]{2,1,0:T(8,128)(2,1)S(1)} %copy-done.4), channel_id=1, source_target_pairs={{0,512},{16,528},{32,544},{48,560},{64,576},{80,592},{96,608},{112... | collective-permute-start | bytes 786440 | tf_op jit(solution)/shard_map/ppermute | solution.py:18
  45.6 0.7 iota_compare_fusion.1
  46.3 0.0 copy-done.3
  46.3 0.7 reshape.95
  47.0 0.1 fusion.16
  47.1 0.1 fusion.13
  47.2 43.2 %collective-permute-done.2 = bf16[2,128,512]{2,1,0:T(8,128)(2,1)S(1)} collective-permute-done((bf16[2,128,512]{2,1,0:T(8,128)(2,1)S(1)}, bf16[2,128,512]{2,1,0:T(8,128)(2,1)S(1)}, u32[]{:S(2)}, u32[]{:S(2)}) %collective-permute-start.2) | collective-permute-done | bytes 262176 | tf_op jit(solution)/shard_map/ppermute | solution.py:18
  90.4 0.7 slice.42
  91.1 0.0 all-gather.6.cloned.1.call-update
  91.1 0.0 all-gather.4.cloned.1.call-done
  91.1 0.0 copy-start.2
  91.1 2.2 copy.37
  93.4 0.0 copy-done.2
  93.4 0.1 slice_bitcast_fusion
  93.5 4.8 %collective-permute-start.3 = (bf16[128,4096]{1,0:T(8,128)(2,1)S(1)}, bf16[128,4096]{1,0:T(8,128)(2,1)}, u32[]{:S(2)}, u32[]{:S(2)}) collective-permute-start(bf16[128,4096]{1,0:T(8,128)(2,1)S(1)} %slice_bitcast_fusion), channel_id=1, source_target_pairs={{0,512},{16,528},{32,544},{48,560},{64,576},{80,592},{96,608},{112... | collective-permute-start | bytes 3145736 | tf_op jit(solution)/shard_map/ppermute | solution.py:18
  98.3 9.1 %convert_bitcast_fusion.1 = bf16[32,14,128,128]{3,2,1,0:T(8,128)(2,1)} fusion(bf16[256,32,128,1]{2,1,0,3:T(8,128)(2,1)S(1)} %bitcast.54, bf16[256,14,128,1]{2,1,0,3:T(8,128)(2,1)S(1)} %bitcast.57), kind=kOutput, calls=%fused_computation.5 | convolution fusion | flops 3765436416 | bytes 17694720 | tf_op jit(solution)/shard_map/njd,nic->jidc/dot_general | solution.py:73
  107.4 7.5 %gather_fusion = bf16[63,128,128]{2,1,0:T(8,128)(2,1)} fusion(bf16[32,14,128,128]{3,2,1,0:T(8,128)(2,1)} %convert_bitcast_fusion.1, s32[63]{0:T(128)S(1)} %get-tuple-element.14), kind=kCustom, calls=%fused_computation | custom fusion | bytes 4129272 | tf_op jit(solution)/shard_map/gather | solution.py:82
  114.9 7.5 %gather_fusion.1 = bf16[63,128,128]{2,1,0:T(8,128)(2,1)} fusion(bf16[32,14,128,128]{3,2,1,0:T(8,128)(2,1)} %convert_bitcast_fusion.1, s32[63]{0:T(128)S(1)} %get-tuple-element.13), kind=kCustom, calls=%fused_computation.1 | custom fusion | bytes 4129272 | tf_op jit(solution)/shard_map/gather | solution.py:82
  122.4 3.9 %select_bitcast_fusion = (bf16[63,128,128]{1,2,0:T(8,128)(2,1)}, bf16[63,128,128]{1,2,0:T(8,128)(2,1)S(1)}) fusion(bf16[63,128,128]{2,1,0:T(8,128)(2,1)} %gather_fusion.1, pred[63]{0:T(512)(128)(4,1)S(1)} %get-tuple-element.17, bf16[63,128,128]{2,1,0:T(8,128)(2,1)} %gather_fusion, pred[63]{0:T(512)(128)(4,1)S(1)} %get-tuple-element.18), kind=kLoop, calls=%fused_computation.15 | loop fusion | flops 2064384 | bytes 8257662 | tf_op jit(solution)/shard_map/jit(_where)/select_n | solution.py:83
  126.2 5.1 %all-gather.6.cloned.1.call-done = bf16[1,128,4096]{2,1,0:T(8,128)(2,1)} async-done(((bf16[1,128,512]{2,1,0:T(8,128)(2,1)}), bf16[1,128,4096]{2,1,0:T(8,128)(2,1)}) %all-gather.6.cloned.1.call-update) | async-done | bytes 1048592 | tf_op jit(solution)/shard_map/all_gather | solution.py:50
  131.3 9.7 %collective-permute-done.3 = bf16[128,4096]{1,0:T(8,128)(2,1)} collective-permute-done((bf16[128,4096]{1,0:T(8,128)(2,1)S(1)}, bf16[128,4096]{1,0:T(8,128)(2,1)}, u32[]{:S(2)}, u32[]{:S(2)}) %collective-permute-start.3) | collective-permute-done | bytes 1048608 | tf_op jit(solution)/shard_map/ppermute | solution.py:18
  141.1 1.7 pad_maximum_fusion
  142.8 0.5 copy.38
  143.3 0.0 collective-permute-done.4
  143.3 10.3 %convert_bitcast_fusion = bf16[32,14,128,128]{3,2,1,0:T(8,128)(2,1)} fusion(bf16[256,14,128,1]{0,2,1,3:T(8,128)(2,1)} %bitcast.17, bf16[256,32,128,1]{2,1,0,3:T(8,128)(2,1)S(1)} %bitcast.53), kind=kOutput, calls=%fused_computation.4 | convolution fusion | flops 3765436416 | bytes 17694720 | tf_op jit(solution)/shard_map/njd,nic->jidc/dot_general | solution.py:73
  153.7 7.4 %gather_fusion.3 = bf16[63,128,128]{2,1,0:T(8,128)(2,1)} fusion(bf16[32,14,128,128]{3,2,1,0:T(8,128)(2,1)} %convert_bitcast_fusion, s32[63]{0:T(128)S(1)} %get-tuple-element.14), kind=kCustom, calls=%fused_computation.3 | custom fusion | bytes 4129272 | tf_op jit(solution)/shard_map/gather | solution.py:82
  161.1 3.9 %fusion = bf16[63,128,128]{1,2,0:T(8,128)(2,1)} fusion(bf16[63,128,128]{1,2,0:T(8,128)(2,1)S(1)} %get-tuple-element.10, bf16[63,128,128]{2,1,0:T(8,128)(2,1)} %gather_fusion.3, pred[63]{0:T(512)(128)(4,1)S(1)} %get-tuple-element.18), kind=kLoop, calls=%fused_computation.7 | loop fusion | flops 5160960 | bytes 6193215 | tf_op jit(solution)/shard_map/convert_element_type | solution.py:93
  165.0 0.0 copy-start.1
  165.0 2.9 %collective-permute-start.5 = (bf16[63,128,128]{1,2,0:T(8,128)(2,1)}, bf16[63,128,128]{1,2,0:T(8,128)(2,1)}, u32[]{:S(2)}, u32[]{:S(2)}) collective-permute-start(bf16[63,128,128]{1,2,0:T(8,128)(2,1)} %fusion), channel_id=1, source_target_pairs={{0,1},{1,0},{2,3},{3,2},{4,5},{5,4},{6,7},{7,6},{8,9},{9,8},{10,11... | collective-permute-start | bytes 6193160 | tf_op jit(solution)/shard_map/ppermute | solution.py:18
  167.8 7.4 %gather_fusion.2 = bf16[63,128,128]{2,1,0:T(8,128)(2,1)} fusion(bf16[32,14,128,128]{3,2,1,0:T(8,128)(2,1)} %convert_bitcast_fusion, s32[63]{0:T(128)S(1)} %get-tuple-element.13), kind=kCustom, calls=%fused_computation.2 | custom fusion | bytes 4129272 | tf_op jit(solution)/shard_map/gather | solution.py:82
  175.3 38.0 %collective-permute-done.5 = bf16[63,128,128]{1,2,0:T(8,128)(2,1)} collective-permute-done((bf16[63,128,128]{1,2,0:T(8,128)(2,1)}, bf16[63,128,128]{1,2,0:T(8,128)(2,1)}, u32[]{:S(2)}, u32[]{:S(2)}) %collective-permute-start.5) | collective-permute-done | bytes 2064416 | tf_op jit(solution)/shard_map/ppermute | solution.py:18
  213.3 0.0 copy-done.1
  213.3 5.0 %fusion.4 = bf16[1,1,63,128,128]{3,4,2,1,0:T(8,128)(2,1)} fusion(bf16[63,128,128]{1,2,0:T(8,128)(2,1)} %collective-permute-done.5, bf16[63,128,128]{1,2,0:T(8,128)(2,1)S(1)} %copy-done.1, bf16[63,128,128]{2,1,0:T(8,128)(2,1)} %gather_fusion.2, pred[63]{0:T(512)(128)(4,1)S(1)} %get-tuple-element.17), kind=kLoop, calls=%fused_computation.14 | loop fusion | flops 9289728 | bytes 8257599 | tf_op jit(solution)/shard_map/reshape | solution.py:99
  218.3 4.1 %copy.21 = bf16[1,1,63,128,128]{4,3,2,1,0:T(8,128)(2,1)} copy(bf16[1,1,63,128,128]{3,4,2,1,0:T(8,128)(2,1)} %fusion.4) | data formatting | bytes 4128768 | tf_op jit(solution)/shard_map/reshape | solution.py:99
  (4 shorter events, 0.1 us)
Async XLA Ops:
  6.5 32.2 %copy-start = (s32[32,14,32]{2,0,1:T(8,128)S(1)}, s32[32,14,32]{2,0,1:T(8,128)}, u32[]{:S(2)}) copy-start(s32[32,14,32]{2,0,1:T(8,128)} %param.5) | copy-start | bytes 172036
  6.5 39.8 %copy-start.3 = (bf16[2,1,1,128,1792]{4,3,2,1,0:T(8,128)(2,1)S(1)}, bf16[2,1,1,128,1792]{4,3,2,1,0:T(8,128)(2,1)}, u32[]{:S(2)}) copy-start(bf16[2,1,1,128,1792]{4,3,2,1,0:T(8,128)(2,1)} %param.3) | copy-start | bytes 2752516
  6.5 84.6 %all-gather.4.cloned.1.call-start = ((), (), s32[]{:S(2)}) async-start(), calls=%async_computation | async-start | bytes 2359296 | tf_op jit(solution)/shard_map/all_gather | solution.py:49
  7.6 18.0 %collective-permute-start = (bf16[128,512]{1,0:T(8,128)(2,1)S(1)}, bf16[128,512]{1,0:T(8,128)(2,1)S(1)}, u32[]{:S(2)}, u32[]{:S(2)}) collective-permute-start(bf16[128,512]{1,0:T(8,128)(2,1)S(1)} %get-tuple-element.11), channel_id=1, source_target_pairs={{16,0},{32,16},{48,32},{64,48},{80,64},{96,80},{112,96},{128,112},... | collective-permute-start | bytes 393224 | tf_op jit(solution)/shard_map/ppermute | solution.py:12
  23.7 8.1 %collective-permute-start.1 = (bf16[128,512]{1,0:T(8,128)(2,1)S(1)}, bf16[128,512]{1,0:T(8,128)(2,1)S(1)}, u32[]{:S(2)}, u32[]{:S(2)}) collective-permute-start(bf16[128,512]{1,0:T(8,128)(2,1)S(1)} %get-tuple-element.12), channel_id=1, source_target_pairs={{1008,0},{0,16},{16,32},{32,48},{48,64},{64,80},{80,96},{96,112},{... | collective-permute-start | bytes 393224 | tf_op jit(solution)/shard_map/ppermute | solution.py:12
  32.5 7.7 %copy-start.4 = (bf16[2,128,512]{2,1,0:T(8,128)(2,1)S(1)}, bf16[2,128,512]{2,1,0:T(8,128)(2,1)}, u32[]{:S(2)}) copy-start(bf16[2,128,512]{2,1,0:T(8,128)(2,1)} %pad_maximum_fusion.1) | copy-start | bytes 786436
  32.6 98.8 %all-gather.6.cloned.1.call-start = ((), (), s32[]{:S(2)}) async-start(), calls=%async_computation.1 | async-start | bytes 1179648 | tf_op jit(solution)/shard_map/all_gather | solution.py:50
  34.8 108.5 %collective-permute-start.4 = (bf16[256,1792]{0,1:T(8,128)(2,1)}, bf16[256,1792]{0,1:T(8,128)(2,1)}, u32[]{:S(2)}, u32[]{:S(2)}) collective-permute-start(bf16[256,1792]{0,1:T(8,128)(2,1)} %copy.35), channel_id=1, source_target_pairs={{0,512},{16,528},{32,544},{48,560},{64,576},{80,592},{96,608},{112... | collective-permute-start | bytes 2752520 | tf_op jit(solution)/shard_map/ppermute | solution.py:18
  40.3 50.1 %collective-permute-start.2 = (bf16[2,128,512]{2,1,0:T(8,128)(2,1)S(1)}, bf16[2,128,512]{2,1,0:T(8,128)(2,1)S(1)}, u32[]{:S(2)}, u32[]{:S(2)}) collective-permute-start(bf16[2,128,512]{2,1,0:T(8,128)(2,1)S(1)} %copy-done.4), channel_id=1, source_target_pairs={{0,512},{16,528},{32,544},{48,560},{64,576},{80,592},{96,608},{112... | collective-permute-start | bytes 786440 | tf_op jit(solution)/shard_map/ppermute | solution.py:18
  91.1 2.2 copy-start.2
  93.5 47.6 %collective-permute-start.3 = (bf16[128,4096]{1,0:T(8,128)(2,1)S(1)}, bf16[128,4096]{1,0:T(8,128)(2,1)}, u32[]{:S(2)}, u32[]{:S(2)}) collective-permute-start(bf16[128,4096]{1,0:T(8,128)(2,1)S(1)} %slice_bitcast_fusion), channel_id=1, source_target_pairs={{0,512},{16,528},{32,544},{48,560},{64,576},{80,592},{96,608},{112... | collective-permute-start | bytes 3145736 | tf_op jit(solution)/shard_map/ppermute | solution.py:18
  165.0 48.4 %copy-start.1 = (bf16[63,128,128]{1,2,0:T(8,128)(2,1)S(1)}, bf16[63,128,128]{1,2,0:T(8,128)(2,1)}, u32[]{:S(2)}) copy-start(bf16[63,128,128]{1,2,0:T(8,128)(2,1)} %get-tuple-element.8) | copy-start | bytes 6193156
  165.0 48.4 %collective-permute-start.5 = (bf16[63,128,128]{1,2,0:T(8,128)(2,1)}, bf16[63,128,128]{1,2,0:T(8,128)(2,1)}, u32[]{:S(2)}, u32[]{:S(2)}) collective-permute-start(bf16[63,128,128]{1,2,0:T(8,128)(2,1)} %fusion), channel_id=1, source_target_pairs={{0,1},{1,0},{2,3},{3,2},{4,5},{5,4},{6,7},{7,6},{8,9},{9,8},{10,11... | collective-permute-start | bytes 6193160 | tf_op jit(solution)/shard_map/ppermute | solution.py:18
Sparse Core Ops, SparseCore 0:
  32.7 44.3 all-gather.3
  91.2 40.0 all-gather.5

commit v7 on v6

--- a/solution.py
+++ b/solution.py
@@ -41,16 +41,17 @@
     ff_local = hidden.shape[4]
 
     own_hidden = hidden[:, 0, 0].reshape(2 * row_count, ff_local)
+    arrived_all = jnp.stack(
+        [
+            passed_along(incoming[0, 0, 0], "section", -1),
+            passed_along(incoming[1, 0, 0], "section", 1),
+            passed_along(incoming[0, 0, 0], "section", -(half_count + 1)),
+            passed_along(incoming[1, 0, 0], "section", half_count + 1),
+        ]
+    )
     partner_hidden = from_partner(own_hidden, "section", swap_bit)
-    down_part = passed_along(incoming[0, 0, 0], "section", -1)
-    up_part = passed_along(incoming[1, 0, 0], "section", 1)
-    own_arrived = jnp.stack([down_part, up_part])
-    partner_arrived = from_partner(own_arrived, "section", swap_bit)
-    own_cot = lax.all_gather(own_arrived, "tp", axis=2, tiled=True)
-    partner_down = lax.all_gather(partner_arrived[0], "tp", axis=1, tiled=True)
-    partner_up = from_partner(own_cot[1], "section", swap_bit)
-    partner_cot = jnp.stack([partner_down, partner_up])
-    d_total = own_cot.shape[2]
+    cot_all = lax.all_gather(arrived_all, "tp", axis=2, tiled=True)
+    d_total = cot_all.shape[2]
     ffb = ff_local // block_side
     db = d_total // block_side
 
@@ -82,10 +83,10 @@
         picked = jnp.swapaxes(dense[cols_q, rows_q], 1, 2)
         return jnp.where(usable_q[:, None, None], picked, jnp.zeros_like(picked))
 
-    own_dense = partial_of(own_hidden, own_cot)
+    own_dense = partial_of(own_hidden, cot_all[:2])
     own_sent = blocks_of(own_dense, sent_q)
     own_kept = blocks_of(own_dense, kept_q)
-    own_sent, own_kept, partner_cot = lax.optimization_barrier((own_sent, own_kept, partner_cot))
+    own_sent, own_kept, partner_cot = lax.optimization_barrier((own_sent, own_kept, cot_all[2:]))
     partner_dense = partial_of(partner_hidden, partner_cot)
 
     def paired_of(own_blocks, table):

time: 230 us -> 223 us (0.970)
  waiting for transfers between devices: 102 us -> 96.6 us
    ppermute x4 -> x2, waiting for transfers between devices: 91 us -> 37.4 us  [from_partner(): return lax.ppermute(value, axis, pairs)]
    all_gather x2 -> x1, waiting for transfers between devices: 5.13 us -> 45.5 us  [body(): cot_all = lax.all_gather(arrived_all, 'tp', axis=2, tiled=True)]
    ppermute x2 -> x4, starting transfers between devices: 18 us -> 29 us  [passed_along(): return lax.ppermute(block, axis, route)]
    ppermute x4 -> x2, starting transfers between devices: 16.9 us -> 6.97 us  [from_partner(): return lax.ppermute(value, axis, pairs)]
    ppermute x2 -> x4, waiting for transfers between devices: 6.18 us -> 13.7 us  [passed_along(): return lax.ppermute(block, axis, route)]
  transfers between devices with their start and end apart: 8 -> 7, of which waited for: 5 -> 4; matrix products, arithmetic and copies ran while one was open for 20% -> 20% of each run, Pallas kernels for 0% -> 0%
where the time goes in v7:
time: 223 us
  waiting for transfers between devices  96.6 us (43%)
  local copies, waits for them, and re-layouts  41.6 us (19%)
  starting transfers between devices  36 us (16%)
  matrix products  19.5 us (9%)
  other arithmetic  15.6 us (7%)
  between operations  13.6 us (6%)
    all_gather x1, waiting for transfers between devices, body(): cot_all = lax.all_gather(arrived_all, 'tp', axis=2, tiled=True)  45.5 us
    ppermute x2, waiting for transfers between devices, from_partner(): return lax.ppermute(value, axis, pairs)  37.4 us
    gather x4, local copies, waits for them, and re-layouts, blocks_of(): picked = jnp.swapaxes(dense[cols_q, rows_q], 1, 2)  29.8 us
    ppermute x4, starting transfers between devices, passed_along(): return lax.ppermute(block, axis, route)  29 us
    dot_general x2, matrix products, partial_of(): jnp.einsum('njd,nic->jidc', cot_rows.reshape(-1, db, block_side), hidden_...  19.5 us
    ppermute x4, waiting for transfers between devices, passed_along(): return lax.ppermute(block, axis, route)  13.7 us
    ppermute x2, starting transfers between devices, from_partner(): return lax.ppermute(value, axis, pairs)  6.97 us
    reshape x1, other arithmetic, body(): return summed.reshape(1, 1, -1, block_side, block_side)  5.02 us
  transfers between devices with their start and end apart: 7, of which 4 were waited for; matrix products, arithmetic and copies ran while one was open for 20% of the time, Pallas kernels for 0%

profile of v7, /device:TPU:1, one launch (start us, length us, event | category | flops | bytes accessed | tf_op | source)
XLA Modules:
  0.0 222.8 jit_solution(12950847716404715636)
XLA Ops:
  6.5 0.0 copy-start
  6.5 0.0 copy-start.4
  6.5 0.0 all-gather.2.cloned.1.call-start
  6.5 1.1 slice_bitcast_fusion.1
  7.6 16.1 %collective-permute-start = (bf16[128,512]{1,0:T(8,128)(2,1)S(1)}, bf16[128,512]{1,0:T(8,128)(2,1)S(1)}, u32[]{:S(2)}, u32[]{:S(2)}) collective-permute-start(bf16[128,512]{1,0:T(8,128)(2,1)S(1)} %get-tuple-element.13), channel_id=1, source_target_pairs={{16,0},{32,16},{48,32},{64,48},{80,64},{96,80},{112,96},{128,112},... | collective-permute-start | bytes 393224 | tf_op jit(solution)/shard_map/ppermute | solution.py:12
  23.7 1.9 collective-permute-start.1
  25.6 9.1 %collective-permute-start.2 = (bf16[128,512]{1,0:T(8,128)(2,1)S(1)}, bf16[128,512]{1,0:T(8,128)(2,1)S(1)}, u32[]{:S(2)}, u32[]{:S(2)}) collective-permute-start(bf16[128,512]{1,0:T(8,128)(2,1)S(1)} %get-tuple-element.13), channel_id=1, source_target_pairs={{528,0},{544,16},{560,32},{576,48},{592,64},{608,80},{624,96},{640... | collective-permute-start | bytes 393224 | tf_op jit(solution)/shard_map/ppermute | solution.py:12
  34.8 1.9 collective-permute-start.3
  36.7 0.0 collective-permute-done
  36.7 0.0 collective-permute-done.1
  36.7 3.4 %collective-permute-done.2 = bf16[128,512]{1,0:T(8,128)(2,1)S(1)} collective-permute-done((bf16[128,512]{1,0:T(8,128)(2,1)S(1)}, bf16[128,512]{1,0:T(8,128)(2,1)S(1)}, u32[]{:S(2)}, u32[]{:S(2)}) %collective-permute-start.2) | collective-permute-done | bytes 131104 | tf_op jit(solution)/shard_map/ppermute | solution.py:12
  40.1 10.4 %collective-permute-done.3 = bf16[128,512]{1,0:T(8,128)(2,1)S(1)} collective-permute-done((bf16[128,512]{1,0:T(8,128)(2,1)S(1)}, bf16[128,512]{1,0:T(8,128)(2,1)S(1)}, u32[]{:S(2)}, u32[]{:S(2)}) %collective-permute-start.3) | collective-permute-done | bytes 131104 | tf_op jit(solution)/shard_map/ppermute | solution.py:12
  50.4 0.9 pad_maximum_fusion
  51.3 0.0 all-gather.2.cloned.1.call-update
  51.3 0.0 copy-done.4
  51.3 1.3 copy.35
  52.6 3.8 %collective-permute-start.4 = (bf16[256,1792]{0,1:T(8,128)(2,1)}, bf16[256,1792]{0,1:T(8,128)(2,1)}, u32[]{:S(2)}, u32[]{:S(2)}) collective-permute-start(bf16[256,1792]{0,1:T(8,128)(2,1)} %copy.35), channel_id=1, source_target_pairs={{0,512},{16,528},{32,544},{48,560},{64,576},{80,592},{96,608},{112... | collective-permute-start | bytes 2752520 | tf_op jit(solution)/shard_map/ppermute | solution.py:18
  56.4 0.7 reshape.93
  57.1 0.0 copy-done
  57.2 0.1 reshape.33
  57.3 0.3 reduce-window.9
  57.6 0.1 slice.28
  57.7 0.1 slice_reduce_fusion
  57.8 0.1 add_bitcast_fusion
  57.9 0.6 slice.30
  58.5 0.6 iota_compare_fusion.1
  59.1 0.1 fusion.17
  59.2 0.1 convert_reduce_fusion
  59.4 0.1 fusion.13
  59.4 45.5 %all-gather.2.cloned.1.call-done = bf16[4,128,4096]{2,1,0:T(8,128)(2,1)} async-done(((bf16[4,128,512]{2,1,0:T(8,128)(2,1)}), bf16[4,128,4096]{2,1,0:T(8,128)(2,1)}) %all-gather.2.cloned.1.call-update) | async-done | bytes 4194320 | tf_op jit(solution)/shard_map/all_gather | solution.py:53
  104.9 2.6 %fusion.16 = (bf16[2,128,4096]{2,1,0:T(8,128)(2,1)S(1)}, bf16[2,128,4096]{2,1,0:T(8,128)(2,1)S(1)}) fusion(bf16[4,128,4096]{2,1,0:T(8,128)(2,1)} %all-gather.2.cloned.1.call-done), kind=kLoop, calls=%fused_computation.48 | loop fusion | bytes 8388608 | tf_op jit(solution)/shard_map/slice | solution.py:89
  107.5 0.5 copy.37
  108.0 9.1 %convert_bitcast_fusion.1 = bf16[32,14,128,128]{3,2,1,0:T(8,128)(2,1)} fusion(bf16[256,32,128,1]{2,1,0,3:T(8,128)(2,1)S(1)} %bitcast.53, bf16[256,14,128,1]{2,1,0,3:T(8,128)(2,1)S(1)} %bitcast.56), kind=kOutput, calls=%fused_computation.5 | convolution fusion | flops 3765436416 | bytes 17694720 | tf_op jit(solution)/shard_map/njd,nic->jidc/dot_general | solution.py:74
  117.1 7.4 %gather_fusion = bf16[63,128,128]{2,1,0:T(8,128)(2,1)} fusion(bf16[32,14,128,128]{3,2,1,0:T(8,128)(2,1)} %convert_bitcast_fusion.1, s32[63]{0:T(128)S(1)} %get-tuple-element.16), kind=kCustom, calls=%fused_computation | custom fusion | bytes 4129272 | tf_op jit(solution)/shard_map/gather | solution.py:83
  124.5 7.4 %gather_fusion.1 = bf16[63,128,128]{2,1,0:T(8,128)(2,1)} fusion(bf16[32,14,128,128]{3,2,1,0:T(8,128)(2,1)} %convert_bitcast_fusion.1, s32[63]{0:T(128)S(1)} %get-tuple-element.15), kind=kCustom, calls=%fused_computation.1 | custom fusion | bytes 4129272 | tf_op jit(solution)/shard_map/gather | solution.py:83
  132.0 4.5 %select_bitcast_fusion = (bf16[63,128,128]{1,2,0:T(8,128)(2,1)}, bf16[63,128,128]{1,2,0:T(8,128)(2,1)}) fusion(bf16[63,128,128]{2,1,0:T(8,128)(2,1)} %gather_fusion.1, pred[63]{0:T(512)(128)(4,1)S(1)} %get-tuple-element.19, bf16[63,128,128]{2,1,0:T(8,128)(2,1)} %gather_fusion, pred[63]{0:T(512)(128)(4,1)S(1)} %get-tuple-element.20), kind=kLoop, calls=%fused_computation.14 | loop fusion | flops 2064384 | bytes 8257662 | tf_op jit(solution)/shard_map/jit(_where)/select_n | solution.py:84
  136.5 0.5 copy.38
  137.0 0.0 collective-permute-done.4
  137.0 10.3 %convert_bitcast_fusion = bf16[32,14,128,128]{3,2,1,0:T(8,128)(2,1)} fusion(bf16[256,14,128,1]{0,2,1,3:T(8,128)(2,1)} %bitcast.17, bf16[256,32,128,1]{2,1,0,3:T(8,128)(2,1)S(1)} %bitcast.52), kind=kOutput, calls=%fused_computation.4 | convolution fusion | flops 3765436416 | bytes 17694720 | tf_op jit(solution)/shard_map/njd,nic->jidc/dot_general | solution.py:74
  147.3 0.0 copy-start.2
  147.3 7.6 %gather_fusion.3 = bf16[63,128,128]{2,1,0:T(8,128)(2,1)} fusion(bf16[32,14,128,128]{3,2,1,0:T(8,128)(2,1)} %convert_bitcast_fusion, s32[63]{0:T(128)S(1)} %get-tuple-element.16), kind=kCustom, calls=%fused_computation.3 | custom fusion | bytes 4129272 | tf_op jit(solution)/shard_map/gather | solution.py:83
  154.9 0.0 copy-done.2
  154.9 3.9 %fusion = bf16[63,128,128]{1,2,0:T(8,128)(2,1)} fusion(bf16[63,128,128]{1,2,0:T(8,128)(2,1)S(1)} %copy-done.2, bf16[63,128,128]{2,1,0:T(8,128)(2,1)} %gather_fusion.3, pred[63]{0:T(512)(128)(4,1)S(1)} %get-tuple-element.20), kind=kLoop, calls=%fused_computation.7 | loop fusion | flops 5160960 | bytes 6193215 | tf_op jit(solution)/shard_map/convert_element_type | solution.py:94
  158.8 0.0 copy-start.3
  158.8 3.2 %collective-permute-start.5 = (bf16[63,128,128]{1,2,0:T(8,128)(2,1)}, bf16[63,128,128]{1,2,0:T(8,128)(2,1)}, u32[]{:S(2)}, u32[]{:S(2)}) collective-permute-start(bf16[63,128,128]{1,2,0:T(8,128)(2,1)} %fusion), channel_id=1, source_target_pairs={{0,1},{1,0},{2,3},{3,2},{4,5},{5,4},{6,7},{7,6},{8,9},{9,8},{10,11... | collective-permute-start | bytes 6193160 | tf_op jit(solution)/shard_map/ppermute | solution.py:18
  162.0 7.5 %gather_fusion.2 = bf16[63,128,128]{2,1,0:T(8,128)(2,1)} fusion(bf16[32,14,128,128]{3,2,1,0:T(8,128)(2,1)} %convert_bitcast_fusion, s32[63]{0:T(128)S(1)} %get-tuple-element.15), kind=kCustom, calls=%fused_computation.2 | custom fusion | bytes 4129272 | tf_op jit(solution)/shard_map/gather | solution.py:83
  169.4 37.4 %collective-permute-done.5 = bf16[63,128,128]{1,2,0:T(8,128)(2,1)} collective-permute-done((bf16[63,128,128]{1,2,0:T(8,128)(2,1)}, bf16[63,128,128]{1,2,0:T(8,128)(2,1)}, u32[]{:S(2)}, u32[]{:S(2)}) %collective-permute-start.5) | collective-permute-done | bytes 2064416 | tf_op jit(solution)/shard_map/ppermute | solution.py:18
  206.9 0.0 copy-done.3
  206.9 0.0 copy-start.1
  206.9 5.0 %fusion.4 = bf16[1,1,63,128,128]{3,4,2,1,0:T(8,128)(2,1)} fusion(bf16[63,128,128]{1,2,0:T(8,128)(2,1)} %collective-permute-done.5, bf16[63,128,128]{1,2,0:T(8,128)(2,1)S(1)} %copy-done.3, bf16[63,128,128]{2,1,0:T(8,128)(2,1)} %gather_fusion.2, pred[63]{0:T(512)(128)(4,1)S(1)} %get-tuple-element.19), kind=kLoop, calls=%fused_computation.13 | loop fusion | flops 9289728 | bytes 8257599 | tf_op jit(solution)/shard_map/reshape | solution.py:100
  211.9 4.1 %copy.21 = bf16[1,1,63,128,128]{4,3,2,1,0:T(8,128)(2,1)} copy(bf16[1,1,63,128,128]{3,4,2,1,0:T(8,128)(2,1)} %fusion.4) | data formatting | bytes 4128768 | tf_op jit(solution)/shard_map/reshape | solution.py:100
  216.0 0.0 copy-done.1
  (4 shorter events, 0.1 us)
Async XLA Ops:
  6.5 50.6 %copy-start = (s32[32,14,32]{2,0,1:T(8,128)S(1)}, s32[32,14,32]{2,0,1:T(8,128)}, u32[]{:S(2)}) copy-start(s32[32,14,32]{2,0,1:T(8,128)} %param.5) | copy-start | bytes 172036
  6.5 44.8 %copy-start.4 = (bf16[2,1,1,128,1792]{4,3,2,1,0:T(8,128)(2,1)S(1)}, bf16[2,1,1,128,1792]{4,3,2,1,0:T(8,128)(2,1)}, u32[]{:S(2)}) copy-start(bf16[2,1,1,128,1792]{4,3,2,1,0:T(8,128)(2,1)} %param.3) | copy-start | bytes 2752516
  6.5 98.4 %all-gather.2.cloned.1.call-start = ((), (), s32[]{:S(2)}) async-start(), calls=%async_computation | async-start | bytes 4718592 | tf_op jit(solution)/shard_map/all_gather | solution.py:53
  7.6 29.1 %collective-permute-start = (bf16[128,512]{1,0:T(8,128)(2,1)S(1)}, bf16[128,512]{1,0:T(8,128)(2,1)S(1)}, u32[]{:S(2)}, u32[]{:S(2)}) collective-permute-start(bf16[128,512]{1,0:T(8,128)(2,1)S(1)} %get-tuple-element.13), channel_id=1, source_target_pairs={{16,0},{32,16},{48,32},{64,48},{80,64},{96,80},{112,96},{128,112},... | collective-permute-start | bytes 393224 | tf_op jit(solution)/shard_map/ppermute | solution.py:12
  23.7 13.0 %collective-permute-start.1 = (bf16[128,512]{1,0:T(8,128)(2,1)S(1)}, bf16[128,512]{1,0:T(8,128)(2,1)S(1)}, u32[]{:S(2)}, u32[]{:S(2)}) collective-permute-start(bf16[128,512]{1,0:T(8,128)(2,1)S(1)} %get-tuple-element.14), channel_id=1, source_target_pairs={{1008,0},{0,16},{16,32},{32,48},{48,64},{64,80},{80,96},{96,112},{... | collective-permute-start | bytes 393224 | tf_op jit(solution)/shard_map/ppermute | solution.py:12
  25.6 14.5 %collective-permute-start.2 = (bf16[128,512]{1,0:T(8,128)(2,1)S(1)}, bf16[128,512]{1,0:T(8,128)(2,1)S(1)}, u32[]{:S(2)}, u32[]{:S(2)}) collective-permute-start(bf16[128,512]{1,0:T(8,128)(2,1)S(1)} %get-tuple-element.13), channel_id=1, source_target_pairs={{528,0},{544,16},{560,32},{576,48},{592,64},{608,80},{624,96},{640... | collective-permute-start | bytes 393224 | tf_op jit(solution)/shard_map/ppermute | solution.py:12
  34.8 15.7 %collective-permute-start.3 = (bf16[128,512]{1,0:T(8,128)(2,1)S(1)}, bf16[128,512]{1,0:T(8,128)(2,1)S(1)}, u32[]{:S(2)}, u32[]{:S(2)}) collective-permute-start(bf16[128,512]{1,0:T(8,128)(2,1)S(1)} %get-tuple-element.14), channel_id=1, source_target_pairs={{496,0},{512,16},{528,32},{544,48},{560,64},{576,80},{592,96},{608... | collective-permute-start | bytes 393224 | tf_op jit(solution)/shard_map/ppermute | solution.py:12
  52.6 84.4 %collective-permute-start.4 = (bf16[256,1792]{0,1:T(8,128)(2,1)}, bf16[256,1792]{0,1:T(8,128)(2,1)}, u32[]{:S(2)}, u32[]{:S(2)}) collective-permute-start(bf16[256,1792]{0,1:T(8,128)(2,1)} %copy.35), channel_id=1, source_target_pairs={{0,512},{16,528},{32,544},{48,560},{64,576},{80,592},{96,608},{112... | collective-permute-start | bytes 2752520 | tf_op jit(solution)/shard_map/ppermute | solution.py:18
  147.3 7.6 %copy-start.2 = (bf16[63,128,128]{1,2,0:T(8,128)(2,1)S(1)}, bf16[63,128,128]{1,2,0:T(8,128)(2,1)}, u32[]{:S(2)}) copy-start(bf16[63,128,128]{1,2,0:T(8,128)(2,1)} %get-tuple-element.10) | copy-start | bytes 6193156
  158.8 48.1 %copy-start.3 = (bf16[63,128,128]{1,2,0:T(8,128)(2,1)S(1)}, bf16[63,128,128]{1,2,0:T(8,128)(2,1)}, u32[]{:S(2)}) copy-start(bf16[63,128,128]{1,2,0:T(8,128)(2,1)} %get-tuple-element.8) | copy-start | bytes 6193156
  158.8 48.1 %collective-permute-start.5 = (bf16[63,128,128]{1,2,0:T(8,128)(2,1)}, bf16[63,128,128]{1,2,0:T(8,128)(2,1)}, u32[]{:S(2)}, u32[]{:S(2)}) collective-permute-start(bf16[63,128,128]{1,2,0:T(8,128)(2,1)} %fusion), channel_id=1, source_target_pairs={{0,1},{1,0},{2,3},{3,2},{4,5},{5,4},{6,7},{7,6},{8,9},{9,8},{10,11... | collective-permute-start | bytes 6193160 | tf_op jit(solution)/shard_map/ppermute | solution.py:18
  206.9 9.1 %copy-start.1 = (s32[32,14,32]{2,0,1:T(8,128)S(1)}, s32[32,14,32]{2,0,1:T(8,128)}, u32[]{:S(2)}) copy-start(s32[32,14,32]{2,0,1:T(8,128)} %param.5) | copy-start | bytes 172036
Sparse Core Ops, SparseCore 0:
  51.4 53.4 all-gather.1

commit v8 on v7

--- a/solution.py
+++ b/solution.py
@@ -86,8 +86,7 @@
     own_dense = partial_of(own_hidden, cot_all[:2])
     own_sent = blocks_of(own_dense, sent_q)
     own_kept = blocks_of(own_dense, kept_q)
-    own_sent, own_kept, partner_cot = lax.optimization_barrier((own_sent, own_kept, cot_all[2:]))
-    partner_dense = partial_of(partner_hidden, partner_cot)
+    partner_dense = partial_of(partner_hidden, cot_all[2:])
 
     def paired_of(own_blocks, table):
         total = own_blocks.astype(jnp.float32) + blocks_of(partner_dense, table).astype(jnp.float32)

time: 223 us -> 208 us (0.933)
  waiting for transfers between devices: 96.6 us -> 87.7 us
  other arithmetic: 15.6 us -> 11.1 us
    ppermute x4, waiting for transfers between devices: 13.7 us -> 5.59 us  [passed_along(): return lax.ppermute(block, axis, route)]
    ppermute x2, waiting for transfers between devices: 37.4 us -> 31 us  [from_partner(): return lax.ppermute(value, axis, pairs)]
    all_gather x1, waiting for transfers between devices: 45.5 us -> 51 us  [body(): cot_all = lax.all_gather(arrived_all, 'tp', axis=2, tiled=True)]
    select_n x1 -> x0, other arithmetic: 4.54 us -> none  [blocks_of(): return jnp.where(usable_q[:, None, None], picked, jnp.zeros_like(picked))]
  transfers between devices with their start and end apart: 7 -> 7, of which waited for: 4 -> 3; matrix products, arithmetic and copies ran while one was open for 20% -> 18% of each run, Pallas kernels for 0% -> 0%
where the time goes in v8:
time: 208 us
  waiting for transfers between devices  87.7 us (42%)
  local copies, waits for them, and re-layouts  40.5 us (19%)
  starting transfers between devices  35.5 us (17%)
  matrix products  19.4 us (9%)
  between operations  13.6 us (7%)
  other arithmetic  11.1 us (5%)
    all_gather x1, waiting for transfers between devices, body(): cot_all = lax.all_gather(arrived_all, 'tp', axis=2, tiled=True)  51 us
    ppermute x2, waiting for transfers between devices, from_partner(): return lax.ppermute(value, axis, pairs)  31 us
    gather x4, local copies, waits for them, and re-layouts, blocks_of(): picked = jnp.swapaxes(dense[cols_q, rows_q], 1, 2)  28.7 us
    ppermute x4, starting transfers between devices, passed_along(): return lax.ppermute(block, axis, route)  28.5 us
    dot_general x2, matrix products, partial_of(): jnp.einsum('njd,nic->jidc', cot_rows.reshape(-1, db, block_side), hidden_...  19.4 us
    ppermute x2, starting transfers between devices, from_partner(): return lax.ppermute(value, axis, pairs)  6.96 us
    ppermute x4, waiting for transfers between devices, passed_along(): return lax.ppermute(block, axis, route)  5.59 us
    reshape x1, other arithmetic, body(): return summed.reshape(1, 1, -1, block_side, block_side)  5.08 us
  transfers between devices with their start and end apart: 7, of which 3 were waited for; matrix products, arithmetic and copies ran while one was open for 18% of the time, Pallas kernels for 0%

profile of v8, /device:TPU:1, one launch (start us, length us, event | category | flops | bytes accessed | tf_op | source)
XLA Modules:
  0.0 207.8 jit_solution(11151493206111933952)
XLA Ops:
  6.5 0.0 copy-start
  6.5 0.0 copy-start.2
  6.5 0.0 all-gather.2.cloned.1.call-start
  6.5 1.1 slice_bitcast_fusion.1
  7.6 8.5 %collective-permute-start.2 = (bf16[128,512]{1,0:T(8,128)(2,1)S(1)}, bf16[128,512]{1,0:T(8,128)(2,1)S(1)}, u32[]{:S(2)}, u32[]{:S(2)}) collective-permute-start(bf16[128,512]{1,0:T(8,128)(2,1)S(1)} %get-tuple-element.7), channel_id=1, source_target_pairs={{528,0},{544,16},{560,32},{576,48},{592,64},{608,80},{624,96},{640... | collective-permute-start | bytes 393224 | tf_op jit(solution)/shard_map/ppermute | solution.py:12
  16.1 13.5 %collective-permute-start = (bf16[128,512]{1,0:T(8,128)(2,1)S(1)}, bf16[128,512]{1,0:T(8,128)(2,1)S(1)}, u32[]{:S(2)}, u32[]{:S(2)}) collective-permute-start(bf16[128,512]{1,0:T(8,128)(2,1)S(1)} %get-tuple-element.7), channel_id=1, source_target_pairs={{16,0},{32,16},{48,32},{64,48},{80,64},{96,80},{112,96},{128,112},... | collective-permute-start | bytes 393224 | tf_op jit(solution)/shard_map/ppermute | solution.py:12
  29.7 4.6 %collective-permute-start.3 = (bf16[128,512]{1,0:T(8,128)(2,1)S(1)}, bf16[128,512]{1,0:T(8,128)(2,1)S(1)}, u32[]{:S(2)}, u32[]{:S(2)}) collective-permute-start(bf16[128,512]{1,0:T(8,128)(2,1)S(1)} %get-tuple-element.8), channel_id=1, source_target_pairs={{496,0},{512,16},{528,32},{544,48},{560,64},{576,80},{592,96},{608... | collective-permute-start | bytes 393224 | tf_op jit(solution)/shard_map/ppermute | solution.py:12
  34.2 1.9 collective-permute-start.1
  36.2 0.0 collective-permute-done.2
  36.2 0.0 collective-permute-done
  36.2 5.6 %collective-permute-done.3 = bf16[128,512]{1,0:T(8,128)(2,1)S(1)} collective-permute-done((bf16[128,512]{1,0:T(8,128)(2,1)S(1)}, bf16[128,512]{1,0:T(8,128)(2,1)S(1)}, u32[]{:S(2)}, u32[]{:S(2)}) %collective-permute-start.3) | collective-permute-done | bytes 131104 | tf_op jit(solution)/shard_map/ppermute | solution.py:12
  41.8 0.0 collective-permute-done.1
  41.8 0.9 pad_maximum_fusion
  42.6 0.0 all-gather.2.cloned.1.call-update
  42.7 0.0 copy-done.2
  42.7 1.3 copy.36
  44.0 3.7 %collective-permute-start.4 = (bf16[256,1792]{0,1:T(8,128)(2,1)}, bf16[256,1792]{0,1:T(8,128)(2,1)}, u32[]{:S(2)}, u32[]{:S(2)}) collective-permute-start(bf16[256,1792]{0,1:T(8,128)(2,1)} %copy.36), channel_id=1, source_target_pairs={{0,512},{16,528},{32,544},{48,560},{64,576},{80,592},{96,608},{112... | collective-permute-start | bytes 2752520 | tf_op jit(solution)/shard_map/ppermute | solution.py:18
  47.7 0.7 reshape.93
  48.4 0.0 copy-done
  48.5 0.1 reshape.33
  48.6 0.3 reduce-window.9
  48.9 0.1 slice.28
  49.0 0.1 slice_reduce_fusion
  49.1 0.1 add_bitcast_fusion
  49.2 0.6 slice.30
  49.8 0.6 iota_compare_fusion.1
  50.3 0.1 fusion.17
  50.4 0.1 convert_reduce_fusion
  50.6 0.1 fusion.8
  50.7 51.0 %all-gather.2.cloned.1.call-done = bf16[4,128,4096]{2,1,0:T(8,128)(2,1)} async-done(((bf16[4,128,512]{2,1,0:T(8,128)(2,1)}), bf16[4,128,4096]{2,1,0:T(8,128)(2,1)}) %all-gather.2.cloned.1.call-update) | async-done | bytes 4194320 | tf_op jit(solution)/shard_map/all_gather | solution.py:53
  101.7 2.7 %fusion.16 = (bf16[2,128,4096]{2,1,0:T(8,128)(2,1)S(1)}, bf16[2,128,4096]{2,1,0:T(8,128)(2,1)S(1)}) fusion(bf16[4,128,4096]{2,1,0:T(8,128)(2,1)} %all-gather.2.cloned.1.call-done), kind=kLoop, calls=%fused_computation.46 | loop fusion | bytes 8388608 | tf_op jit(solution)/shard_map/slice | solution.py:86
  104.4 0.5 copy.38
  104.9 0.5 copy.39
  105.4 9.1 %convert_bitcast_fusion.1 = bf16[32,14,128,128]{3,2,1,0:T(8,128)(2,1)} fusion(bf16[256,32,128,1]{2,1,0,3:T(8,128)(2,1)S(1)} %bitcast.47, bf16[256,14,128,1]{2,1,0,3:T(8,128)(2,1)S(1)} %bitcast.50), kind=kOutput, calls=%fused_computation.5 | convolution fusion | flops 3765436416 | bytes 17694720 | tf_op jit(solution)/shard_map/njd,nic->jidc/dot_general | solution.py:74
  114.5 7.5 %gather_fusion.2 = bf16[63,128,128]{2,1,0:T(8,128)(2,1)} fusion(bf16[32,14,128,128]{3,2,1,0:T(8,128)(2,1)} %convert_bitcast_fusion.1, s32[63]{0:T(128)S(1)} %get-tuple-element.10), kind=kCustom, calls=%fused_computation.2 | custom fusion | bytes 4129272 | tf_op jit(solution)/shard_map/gather | solution.py:83
  121.9 0.0 collective-permute-done.4
  121.9 10.3 %convert_bitcast_fusion = bf16[32,14,128,128]{3,2,1,0:T(8,128)(2,1)} fusion(bf16[256,14,128,1]{0,2,1,3:T(8,128)(2,1)} %bitcast.15, bf16[256,32,128,1]{2,1,0,3:T(8,128)(2,1)S(1)} %bitcast.46), kind=kOutput, calls=%fused_computation.4 | convolution fusion | flops 3765436416 | bytes 17694720 | tf_op jit(solution)/shard_map/njd,nic->jidc/dot_general | solution.py:74
  132.2 0.0 copy-start.1
  132.2 7.6 %gather_fusion.3 = bf16[63,128,128]{2,1,0:T(8,128)(2,1)} fusion(bf16[32,14,128,128]{3,2,1,0:T(8,128)(2,1)} %convert_bitcast_fusion, s32[63]{0:T(128)S(1)} %get-tuple-element.10), kind=kCustom, calls=%fused_computation.3 | custom fusion | bytes 4129272 | tf_op jit(solution)/shard_map/gather | solution.py:83
  139.8 0.0 copy-done.1
  139.8 4.0 %fusion.3 = bf16[63,128,128]{1,2,0:T(8,128)(2,1)} fusion(bf16[63,128,128]{2,1,0:T(8,128)(2,1)} %gather_fusion.3, bf16[63,128,128]{2,1,0:T(8,128)(2,1)S(1)} %copy-done.1, pred[63]{0:T(512)(128)(4,1)S(1)} %get-tuple-element.14), kind=kLoop, calls=%fused_computation.12 | loop fusion | flops 6193152 | bytes 6193215 | tf_op jit(solution)/shard_map/convert_element_type | solution.py:93
  143.8 3.2 %collective-permute-start.5 = (bf16[63,128,128]{1,2,0:T(8,128)(2,1)}, bf16[63,128,128]{1,2,0:T(8,128)(2,1)}, u32[]{:S(2)}, u32[]{:S(2)}) collective-permute-start(bf16[63,128,128]{1,2,0:T(8,128)(2,1)} %fusion.3), channel_id=1, source_target_pairs={{0,1},{1,0},{2,3},{3,2},{4,5},{5,4},{6,7},{7,6},{8,9},{9,8},{10,11... | collective-permute-start | bytes 6193160 | tf_op jit(solution)/shard_map/ppermute | solution.py:18
  147.0 6.3 %gather_fusion = bf16[63,128,128]{2,1,0:T(8,128)(2,1)S(1)} fusion(bf16[32,14,128,128]{3,2,1,0:T(8,128)(2,1)} %convert_bitcast_fusion.1, s32[63]{0:T(128)S(1)} %get-tuple-element.9), kind=kCustom, calls=%fused_computation | custom fusion | bytes 4129272 | tf_op jit(solution)/shard_map/gather | solution.py:83
  153.3 7.4 %gather_fusion.1 = bf16[63,128,128]{2,1,0:T(8,128)(2,1)} fusion(bf16[32,14,128,128]{3,2,1,0:T(8,128)(2,1)} %convert_bitcast_fusion, s32[63]{0:T(128)S(1)} %get-tuple-element.9), kind=kCustom, calls=%fused_computation.1 | custom fusion | bytes 4129272 | tf_op jit(solution)/shard_map/gather | solution.py:83
  160.7 31.0 %collective-permute-done.5 = bf16[63,128,128]{1,2,0:T(8,128)(2,1)} collective-permute-done((bf16[63,128,128]{1,2,0:T(8,128)(2,1)}, bf16[63,128,128]{1,2,0:T(8,128)(2,1)}, u32[]{:S(2)}, u32[]{:S(2)}) %collective-permute-start.5) | collective-permute-done | bytes 2064416 | tf_op jit(solution)/shard_map/ppermute | solution.py:18
  191.8 5.1 %fusion.4 = bf16[1,1,63,128,128]{3,4,2,1,0:T(8,128)(2,1)} fusion(bf16[63,128,128]{1,2,0:T(8,128)(2,1)} %collective-permute-done.5, bf16[63,128,128]{2,1,0:T(8,128)(2,1)} %gather_fusion.1, bf16[63,128,128]{2,1,0:T(8,128)(2,1)S(1)} %gather_fusion, pred[63]{0:T(512)(128)(4,1)S(1)} %get-tuple-element.13), kind=kLoop, calls=%fused_computation.13 | loop fusion | flops 10321920 | bytes 8257599 | tf_op jit(solution)/shard_map/reshape | solution.py:99
  196.9 4.1 %copy.21 = bf16[1,1,63,128,128]{4,3,2,1,0:T(8,128)(2,1)} copy(bf16[1,1,63,128,128]{3,4,2,1,0:T(8,128)(2,1)} %fusion.4) | data formatting | bytes 4128768 | tf_op jit(solution)/shard_map/reshape | solution.py:99
  (4 shorter events, 0.1 us)
Async XLA Ops:
  6.5 41.9 %copy-start = (s32[32,14,32]{2,0,1:T(8,128)S(1)}, s32[32,14,32]{2,0,1:T(8,128)}, u32[]{:S(2)}) copy-start(s32[32,14,32]{2,0,1:T(8,128)} %param.5) | copy-start | bytes 172036
  6.5 36.1 %copy-start.2 = (bf16[2,1,1,128,1792]{4,3,2,1,0:T(8,128)(2,1)S(1)}, bf16[2,1,1,128,1792]{4,3,2,1,0:T(8,128)(2,1)}, u32[]{:S(2)}) copy-start(bf16[2,1,1,128,1792]{4,3,2,1,0:T(8,128)(2,1)} %param.3) | copy-start | bytes 2752516
  6.5 95.1 %all-gather.2.cloned.1.call-start = ((), (), s32[]{:S(2)}) async-start(), calls=%async_computation | async-start | bytes 4718592 | tf_op jit(solution)/shard_map/all_gather | solution.py:53
  7.6 28.6 %collective-permute-start.2 = (bf16[128,512]{1,0:T(8,128)(2,1)S(1)}, bf16[128,512]{1,0:T(8,128)(2,1)S(1)}, u32[]{:S(2)}, u32[]{:S(2)}) collective-permute-start(bf16[128,512]{1,0:T(8,128)(2,1)S(1)} %get-tuple-element.7), channel_id=1, source_target_pairs={{528,0},{544,16},{560,32},{576,48},{592,64},{608,80},{624,96},{640... | collective-permute-start | bytes 393224 | tf_op jit(solution)/shard_map/ppermute | solution.py:12
  16.1 20.1 %collective-permute-start = (bf16[128,512]{1,0:T(8,128)(2,1)S(1)}, bf16[128,512]{1,0:T(8,128)(2,1)S(1)}, u32[]{:S(2)}, u32[]{:S(2)}) collective-permute-start(bf16[128,512]{1,0:T(8,128)(2,1)S(1)} %get-tuple-element.7), channel_id=1, source_target_pairs={{16,0},{32,16},{48,32},{64,48},{80,64},{96,80},{112,96},{128,112},... | collective-permute-start | bytes 393224 | tf_op jit(solution)/shard_map/ppermute | solution.py:12
  29.7 12.1 %collective-permute-start.3 = (bf16[128,512]{1,0:T(8,128)(2,1)S(1)}, bf16[128,512]{1,0:T(8,128)(2,1)S(1)}, u32[]{:S(2)}, u32[]{:S(2)}) collective-permute-start(bf16[128,512]{1,0:T(8,128)(2,1)S(1)} %get-tuple-element.8), channel_id=1, source_target_pairs={{496,0},{512,16},{528,32},{544,48},{560,64},{576,80},{592,96},{608... | collective-permute-start | bytes 393224 | tf_op jit(solution)/shard_map/ppermute | solution.py:12
  34.2 7.5 %collective-permute-start.1 = (bf16[128,512]{1,0:T(8,128)(2,1)S(1)}, bf16[128,512]{1,0:T(8,128)(2,1)S(1)}, u32[]{:S(2)}, u32[]{:S(2)}) collective-permute-start(bf16[128,512]{1,0:T(8,128)(2,1)S(1)} %get-tuple-element.8), channel_id=1, source_target_pairs={{1008,0},{0,16},{16,32},{32,48},{48,64},{64,80},{80,96},{96,112},{... | collective-permute-start | bytes 393224 | tf_op jit(solution)/shard_map/ppermute | solution.py:12
  44.0 77.9 %collective-permute-start.4 = (bf16[256,1792]{0,1:T(8,128)(2,1)}, bf16[256,1792]{0,1:T(8,128)(2,1)}, u32[]{:S(2)}, u32[]{:S(2)}) collective-permute-start(bf16[256,1792]{0,1:T(8,128)(2,1)} %copy.36), channel_id=1, source_target_pairs={{0,512},{16,528},{32,544},{48,560},{64,576},{80,592},{96,608},{112... | collective-permute-start | bytes 2752520 | tf_op jit(solution)/shard_map/ppermute | solution.py:18
  132.2 7.6 %copy-start.1 = (bf16[63,128,128]{2,1,0:T(8,128)(2,1)S(1)}, bf16[63,128,128]{2,1,0:T(8,128)(2,1)}, u32[]{:S(2)}) copy-start(bf16[63,128,128]{2,1,0:T(8,128)(2,1)} %gather_fusion.2) | copy-start | bytes 6193156
  143.8 48.0 %collective-permute-start.5 = (bf16[63,128,128]{1,2,0:T(8,128)(2,1)}, bf16[63,128,128]{1,2,0:T(8,128)(2,1)}, u32[]{:S(2)}, u32[]{:S(2)}) collective-permute-start(bf16[63,128,128]{1,2,0:T(8,128)(2,1)} %fusion.3), channel_id=1, source_target_pairs={{0,1},{1,0},{2,3},{3,2},{4,5},{5,4},{6,7},{7,6},{8,9},{9,8},{10,11... | collective-permute-start | bytes 6193160 | tf_op jit(solution)/shard_map/ppermute | solution.py:18
Sparse Core Ops, SparseCore 0:
  42.8 58.8 all-gather.1

commit v9 on v8

--- a/solution.py
+++ b/solution.py
@@ -84,17 +84,20 @@
         return jnp.where(usable_q[:, None, None], picked, jnp.zeros_like(picked))
 
     own_dense = partial_of(own_hidden, cot_all[:2])
-    own_sent = blocks_of(own_dense, sent_q)
     own_kept = blocks_of(own_dense, kept_q)
     partner_dense = partial_of(partner_hidden, cot_all[2:])
 
-    def paired_of(own_blocks, table):
-        total = own_blocks.astype(jnp.float32) + blocks_of(partner_dense, table).astype(jnp.float32)
+    def paired_of(table):
+        total = blocks_of(own_dense, table).astype(jnp.float32) + blocks_of(partner_dense, table).astype(jnp.float32)
         return total.astype(jnp.bfloat16)
 
-    outgoing = paired_of(own_sent, sent_q)
-    received = from_partner(outgoing, "mirror", 0)
-    kept = paired_of(own_kept, kept_q)
+    split = (slots_quarter + 1) // 2
+    first_out = paired_of(tuple(part[:split] for part in sent_q))
+    first_out, second_table = lax.optimization_barrier((first_out, tuple(part[split:] for part in sent_q)))
+    first_back = from_partner(first_out, "mirror", 0)
+    second_back = from_partner(paired_of(second_table), "mirror", 0)
+    received = jnp.concatenate([first_back, second_back])
+    kept = (own_kept.astype(jnp.float32) + blocks_of(partner_dense, kept_q).astype(jnp.float32)).astype(jnp.bfloat16)
     summed = (kept.astype(jnp.float32) + received.astype(jnp.float32)).astype(jnp.bfloat16)
     return summed.reshape(1, 1, -1, block_side, block_side)
 

time: 208 us -> 218 us (1.048)
  local copies, waits for them, and re-layouts: 40.5 us -> 49.6 us
  starting transfers between devices: 35.5 us -> 38.3 us
    gather x4 -> x6, local copies, waits for them, and re-layouts: 28.7 us -> 37.5 us  [blocks_of(): picked = jnp.swapaxes(dense[cols_q, rows_q], 1, 2)]
    ppermute x4, waiting for transfers between devices: 5.59 us -> 13.7 us  [passed_along(): return lax.ppermute(block, axis, route)]
    all_gather x1, waiting for transfers between devices: 51 us -> 45.2 us  [body(): cot_all = lax.all_gather(arrived_all, 'tp', axis=2, tiled=True)]
    ppermute x2 -> x3, waiting for transfers between devices: 31 us -> 27.2 us  [from_partner(): return lax.ppermute(value, axis, pairs)]
    ppermute x2 -> x3, starting transfers between devices: 6.96 us -> 9.21 us  [from_partner(): return lax.ppermute(value, axis, pairs)]
  transfers between devices with their start and end apart: 7 -> 8, of which waited for: 3 -> 4; matrix products, arithmetic and copies ran while one was open for 18% -> 18% of each run, Pallas kernels for 0% -> 0%
where the time goes in v9:
time: 218 us; the launch traced here: 217 us
  waiting for transfers between devices  86.2 us (40%)
  local copies, waits for them, and re-layouts  49.6 us (23%)
  starting transfers between devices  38.3 us (18%)
  matrix products  19.4 us (9%)
  between operations  13.6 us (6%)
  other arithmetic  10.2 us (5%)
    all_gather x1, waiting for transfers between devices, body(): cot_all = lax.all_gather(arrived_all, 'tp', axis=2, tiled=True)  45.2 us
    gather x6, local copies, waits for them, and re-layouts, blocks_of(): picked = jnp.swapaxes(dense[cols_q, rows_q], 1, 2)  37.5 us
    ppermute x4, starting transfers between devices, passed_along(): return lax.ppermute(block, axis, route)  29 us
    ppermute x3, waiting for transfers between devices, from_partner(): return lax.ppermute(value, axis, pairs)  27.2 us
    dot_general x2, matrix products, partial_of(): jnp.einsum('njd,nic->jidc', cot_rows.reshape(-1, db, block_side), hidden_...  19.4 us
    ppermute x4, waiting for transfers between devices, passed_along(): return lax.ppermute(block, axis, route)  13.7 us
    ppermute x3, starting transfers between devices, from_partner(): return lax.ppermute(value, axis, pairs)  9.21 us
    reshape x1, other arithmetic, body(): return summed.reshape(1, 1, -1, block_side, block_side)  5.1 us
  transfers between devices with their start and end apart: 8, of which 4 were waited for; matrix products, arithmetic and copies ran while one was open for 18% of the time, Pallas kernels for 0%

profile of v9, /device:TPU:1, one launch (start us, length us, event | category | flops | bytes accessed | tf_op | source)
XLA Modules:
  0.0 217.3 jit_solution(11312074654100364808)
XLA Ops:
  6.5 0.0 copy-start
  6.5 0.0 copy-start.1
  6.5 0.0 all-gather.2.cloned.1.call-start
  6.5 1.1 slice_bitcast_fusion.1
  7.6 16.1 %collective-permute-start = (bf16[128,512]{1,0:T(8,128)(2,1)S(1)}, bf16[128,512]{1,0:T(8,128)(2,1)S(1)}, u32[]{:S(2)}, u32[]{:S(2)}) collective-permute-start(bf16[128,512]{1,0:T(8,128)(2,1)S(1)} %get-tuple-element.15), channel_id=1, source_target_pairs={{16,0},{32,16},{48,32},{64,48},{80,64},{96,80},{112,96},{128,112},... | collective-permute-start | bytes 393224 | tf_op jit(solution)/shard_map/ppermute | solution.py:12
  23.7 1.9 collective-permute-start.1
  25.6 9.1 %collective-permute-start.2 = (bf16[128,512]{1,0:T(8,128)(2,1)S(1)}, bf16[128,512]{1,0:T(8,128)(2,1)S(1)}, u32[]{:S(2)}, u32[]{:S(2)}) collective-permute-start(bf16[128,512]{1,0:T(8,128)(2,1)S(1)} %get-tuple-element.15), channel_id=1, source_target_pairs={{528,0},{544,16},{560,32},{576,48},{592,64},{608,80},{624,96},{640... | collective-permute-start | bytes 393224 | tf_op jit(solution)/shard_map/ppermute | solution.py:12
  34.8 1.9 collective-permute-start.3
  36.7 0.0 collective-permute-done
  36.7 0.0 collective-permute-done.1
  36.7 3.4 %collective-permute-done.2 = bf16[128,512]{1,0:T(8,128)(2,1)S(1)} collective-permute-done((bf16[128,512]{1,0:T(8,128)(2,1)S(1)}, bf16[128,512]{1,0:T(8,128)(2,1)S(1)}, u32[]{:S(2)}, u32[]{:S(2)}) %collective-permute-start.2) | collective-permute-done | bytes 131104 | tf_op jit(solution)/shard_map/ppermute | solution.py:12
  40.1 10.4 %collective-permute-done.3 = bf16[128,512]{1,0:T(8,128)(2,1)S(1)} collective-permute-done((bf16[128,512]{1,0:T(8,128)(2,1)S(1)}, bf16[128,512]{1,0:T(8,128)(2,1)S(1)}, u32[]{:S(2)}, u32[]{:S(2)}) %collective-permute-start.3) | collective-permute-done | bytes 131104 | tf_op jit(solution)/shard_map/ppermute | solution.py:12
  50.4 0.9 pad_maximum_fusion
  51.3 0.0 all-gather.2.cloned.1.call-update
  51.3 0.0 copy-done.1
  51.3 1.3 copy.36
  52.6 3.8 %collective-permute-start.4 = (bf16[256,1792]{0,1:T(8,128)(2,1)}, bf16[256,1792]{0,1:T(8,128)(2,1)}, u32[]{:S(2)}, u32[]{:S(2)}) collective-permute-start(bf16[256,1792]{0,1:T(8,128)(2,1)} %copy.36), channel_id=1, source_target_pairs={{0,512},{16,528},{32,544},{48,560},{64,576},{80,592},{96,608},{112... | collective-permute-start | bytes 2752520 | tf_op jit(solution)/shard_map/ppermute | solution.py:18
  56.4 0.7 reshape.118
  57.1 0.0 copy-done
  57.2 0.1 reshape.34
  57.3 0.3 reduce-window.9
  57.6 0.1 slice.46
  57.7 0.1 slice_reduce_fusion
  57.8 0.1 add_bitcast_fusion
  57.9 0.6 slice.48
  58.5 0.1 convert_reduce_fusion
  58.7 0.1 fusion.9
  58.8 0.1 slice.57
  58.8 0.1 slice.58
  58.9 0.6 iota_compare_fusion.1
  59.5 0.1 fusion.23
  59.6 0.1 slice.59
  59.7 45.2 %all-gather.2.cloned.1.call-done = bf16[4,128,4096]{2,1,0:T(8,128)(2,1)} async-done(((bf16[4,128,512]{2,1,0:T(8,128)(2,1)}), bf16[4,128,4096]{2,1,0:T(8,128)(2,1)}) %all-gather.2.cloned.1.call-update) | async-done | bytes 4194320 | tf_op jit(solution)/shard_map/all_gather | solution.py:53
  105.0 2.7 %fusion.22 = (bf16[2,128,4096]{2,1,0:T(8,128)(2,1)S(1)}, bf16[2,128,4096]{2,1,0:T(8,128)(2,1)S(1)}) fusion(bf16[4,128,4096]{2,1,0:T(8,128)(2,1)} %all-gather.2.cloned.1.call-done), kind=kLoop, calls=%fused_computation.57 | loop fusion | bytes 8388608 | tf_op jit(solution)/shard_map/slice | solution.py:86
  107.7 0.5 copy.38
  108.2 0.5 copy.39
  108.7 9.1 %convert_bitcast_fusion.1 = bf16[32,14,128,128]{3,2,1,0:T(8,128)(2,1)} fusion(bf16[256,32,128,1]{2,1,0,3:T(8,128)(2,1)S(1)} %bitcast.50, bf16[256,14,128,1]{2,1,0,3:T(8,128)(2,1)S(1)} %bitcast.53), kind=kOutput, calls=%fused_computation.7 | convolution fusion | flops 3765436416 | bytes 17694720 | tf_op jit(solution)/shard_map/njd,nic->jidc/dot_general | solution.py:74
  117.8 5.9 %gather_fusion.2 = bf16[32,128,128]{2,1,0:T(8,128)(2,1)S(1)} fusion(bf16[32,14,128,128]{3,2,1,0:T(8,128)(2,1)} %convert_bitcast_fusion.1, s32[32]{0:T(128)S(1)} %fusion.14), kind=kCustom, calls=%fused_computation.2 | custom fusion | bytes 2097408 | tf_op jit(solution)/shard_map/gather | solution.py:83
  123.7 0.0 collective-permute-done.4
  123.7 10.3 %convert_bitcast_fusion = bf16[32,14,128,128]{3,2,1,0:T(8,128)(2,1)} fusion(bf16[256,14,128,1]{0,2,1,3:T(8,128)(2,1)} %bitcast.15, bf16[256,32,128,1]{2,1,0,3:T(8,128)(2,1)S(1)} %bitcast.49), kind=kOutput, calls=%fused_computation.6 | convolution fusion | flops 3765436416 | bytes 17694720 | tf_op jit(solution)/shard_map/njd,nic->jidc/dot_general | solution.py:74
  134.0 5.9 %gather_fusion.3 = bf16[32,128,128]{2,1,0:T(8,128)(2,1)S(1)} fusion(bf16[32,14,128,128]{3,2,1,0:T(8,128)(2,1)} %convert_bitcast_fusion, s32[32]{0:T(128)S(1)} %fusion.14), kind=kCustom, calls=%fused_computation.3 | custom fusion | bytes 2097408 | tf_op jit(solution)/shard_map/gather | solution.py:83
  140.0 1.5 fusion.4
  141.5 0.0 copy-start.2
  141.5 6.1 %gather_fusion.4 = bf16[31,128,128]{2,1,0:T(8,128)(2,1)S(1)} fusion(bf16[32,14,128,128]{3,2,1,0:T(8,128)(2,1)} %convert_bitcast_fusion.1, s32[31]{0:T(128)S(1)} %fusion.19), kind=kCustom, calls=%fused_computation.4 | custom fusion | bytes 2031864 | tf_op jit(solution)/shard_map/gather | solution.py:83
  147.5 6.0 %gather_fusion.5 = bf16[31,128,128]{2,1,0:T(8,128)(2,1)S(1)} fusion(bf16[32,14,128,128]{3,2,1,0:T(8,128)(2,1)} %convert_bitcast_fusion, s32[31]{0:T(128)S(1)} %fusion.19), kind=kCustom, calls=%fused_computation.5 | custom fusion | bytes 2031864 | tf_op jit(solution)/shard_map/gather | solution.py:83
  153.5 0.0 copy-done.2
  153.5 3.1 %collective-permute-start.5 = (bf16[32,128,128]{1,2,0:T(8,128)(2,1)S(1)}, bf16[32,128,128]{1,2,0:T(8,128)(2,1)}, u32[]{:S(2)}, u32[]{:S(2)}) collective-permute-start(bf16[32,128,128]{1,2,0:T(8,128)(2,1)S(1)} %copy-done.2), channel_id=1, source_target_pairs={{0,1},{1,0},{2,3},{3,2},{4,5},{5,4},{6,7},{7,6},{8,9},{9,8},{10,11... | collective-permute-start | bytes 3145736 | tf_op jit(solution)/shard_map/ppermute | solution.py:18
  156.6 1.5 fusion.5
  158.1 2.4 %collective-permute-start.6 = (bf16[31,128,128]{1,2,0:T(8,128)(2,1)}, bf16[31,128,128]{1,2,0:T(8,128)(2,1)}, u32[]{:S(2)}, u32[]{:S(2)}) collective-permute-start(bf16[31,128,128]{1,2,0:T(8,128)(2,1)} %fusion.5), channel_id=1, source_target_pairs={{0,1},{1,0},{2,3},{3,2},{4,5},{5,4},{6,7},{7,6},{8,9},{9,8},{10,11... | collective-permute-start | bytes 3047432 | tf_op jit(solution)/shard_map/ppermute | solution.py:18
  160.5 6.3 %gather_fusion.1 = bf16[63,128,128]{2,1,0:T(8,128)(2,1)S(1)} fusion(bf16[32,14,128,128]{3,2,1,0:T(8,128)(2,1)} %convert_bitcast_fusion, s32[63]{0:T(128)S(1)} %get-tuple-element.17), kind=kCustom, calls=%fused_computation.1 | custom fusion | bytes 4129272 | tf_op jit(solution)/shard_map/gather | solution.py:83
  166.7 7.4 %gather_fusion = bf16[63,128,128]{2,1,0:T(8,128)(2,1)} fusion(bf16[32,14,128,128]{3,2,1,0:T(8,128)(2,1)} %convert_bitcast_fusion.1, s32[63]{0:T(128)S(1)} %get-tuple-element.17), kind=kCustom, calls=%fused_computation | custom fusion | bytes 4129272 | tf_op jit(solution)/shard_map/gather | solution.py:83
  174.1 27.2 %collective-permute-done.6 = bf16[31,128,128]{1,2,0:T(8,128)(2,1)} collective-permute-done((bf16[31,128,128]{1,2,0:T(8,128)(2,1)}, bf16[31,128,128]{1,2,0:T(8,128)(2,1)}, u32[]{:S(2)}, u32[]{:S(2)}) %collective-permute-start.6) | collective-permute-done | bytes 1015840 | tf_op jit(solution)/shard_map/ppermute | solution.py:18
  201.3 0.0 collective-permute-done.5
  201.3 5.1 %fusion.3 = bf16[1,1,63,128,128]{3,4,2,1,0:T(8,128)(2,1)} fusion(bf16[31,128,128]{1,2,0:T(8,128)(2,1)} %collective-permute-done.6, bf16[32,128,128]{1,2,0:T(8,128)(2,1)} %collective-permute-done.5, bf16[63,128,128]{2,1,0:T(8,128)(2,1)S(1)} %gather_fusion.1, bf16[63,128,128]{2,1,0:T(8,128)(2,1)} %gather_fusion, pred[63]{0:T(512)(128)(4,1)S(1)} %get-tuple-element.22), kind=kLoop, calls=%fused_computation.14 | loop fusion | flops 11354112 | bytes 8257599 | tf_op jit(solution)/shard_map/reshape | solution.py:102
  206.4 4.1 %copy.21 = bf16[1,1,63,128,128]{4,3,2,1,0:T(8,128)(2,1)} copy(bf16[1,1,63,128,128]{3,4,2,1,0:T(8,128)(2,1)} %fusion.3) | data formatting | bytes 4128768 | tf_op jit(solution)/shard_map/reshape | solution.py:102
  (6 shorter events, 0.1 us)
Async XLA Ops:
  6.5 50.6 %copy-start = (s32[32,14,32]{2,0,1:T(8,128)S(1)}, s32[32,14,32]{2,0,1:T(8,128)}, u32[]{:S(2)}) copy-start(s32[32,14,32]{2,0,1:T(8,128)} %param.5) | copy-start | bytes 172036
  6.5 44.8 %copy-start.1 = (bf16[2,1,1,128,1792]{4,3,2,1,0:T(8,128)(2,1)S(1)}, bf16[2,1,1,128,1792]{4,3,2,1,0:T(8,128)(2,1)}, u32[]{:S(2)}) copy-start(bf16[2,1,1,128,1792]{4,3,2,1,0:T(8,128)(2,1)} %param.3) | copy-start | bytes 2752516
  6.5 98.4 %all-gather.2.cloned.1.call-start = ((), (), s32[]{:S(2)}) async-start(), calls=%async_computation | async-start | bytes 4718592 | tf_op jit(solution)/shard_map/all_gather | solution.py:53
  7.6 29.1 %collective-permute-start = (bf16[128,512]{1,0:T(8,128)(2,1)S(1)}, bf16[128,512]{1,0:T(8,128)(2,1)S(1)}, u32[]{:S(2)}, u32[]{:S(2)}) collective-permute-start(bf16[128,512]{1,0:T(8,128)(2,1)S(1)} %get-tuple-element.15), channel_id=1, source_target_pairs={{16,0},{32,16},{48,32},{64,48},{80,64},{96,80},{112,96},{128,112},... | collective-permute-start | bytes 393224 | tf_op jit(solution)/shard_map/ppermute | solution.py:12
  23.7 13.0 %collective-permute-start.1 = (bf16[128,512]{1,0:T(8,128)(2,1)S(1)}, bf16[128,512]{1,0:T(8,128)(2,1)S(1)}, u32[]{:S(2)}, u32[]{:S(2)}) collective-permute-start(bf16[128,512]{1,0:T(8,128)(2,1)S(1)} %get-tuple-element.16), channel_id=1, source_target_pairs={{1008,0},{0,16},{16,32},{32,48},{48,64},{64,80},{80,96},{96,112},{... | collective-permute-start | bytes 393224 | tf_op jit(solution)/shard_map/ppermute | solution.py:12
  25.6 14.5 %collective-permute-start.2 = (bf16[128,512]{1,0:T(8,128)(2,1)S(1)}, bf16[128,512]{1,0:T(8,128)(2,1)S(1)}, u32[]{:S(2)}, u32[]{:S(2)}) collective-permute-start(bf16[128,512]{1,0:T(8,128)(2,1)S(1)} %get-tuple-element.15), channel_id=1, source_target_pairs={{528,0},{544,16},{560,32},{576,48},{592,64},{608,80},{624,96},{640... | collective-permute-start | bytes 393224 | tf_op jit(solution)/shard_map/ppermute | solution.py:12
  34.8 15.7 %collective-permute-start.3 = (bf16[128,512]{1,0:T(8,128)(2,1)S(1)}, bf16[128,512]{1,0:T(8,128)(2,1)S(1)}, u32[]{:S(2)}, u32[]{:S(2)}) collective-permute-start(bf16[128,512]{1,0:T(8,128)(2,1)S(1)} %get-tuple-element.16), channel_id=1, source_target_pairs={{496,0},{512,16},{528,32},{544,48},{560,64},{576,80},{592,96},{608... | collective-permute-start | bytes 393224 | tf_op jit(solution)/shard_map/ppermute | solution.py:12
  52.6 71.1 %collective-permute-start.4 = (bf16[256,1792]{0,1:T(8,128)(2,1)}, bf16[256,1792]{0,1:T(8,128)(2,1)}, u32[]{:S(2)}, u32[]{:S(2)}) collective-permute-start(bf16[256,1792]{0,1:T(8,128)(2,1)} %copy.36), channel_id=1, source_target_pairs={{0,512},{16,528},{32,544},{48,560},{64,576},{80,592},{96,608},{112... | collective-permute-start | bytes 2752520 | tf_op jit(solution)/shard_map/ppermute | solution.py:18
  141.5 12.0 %copy-start.2 = (bf16[32,128,128]{1,2,0:T(8,128)(2,1)S(1)}, bf16[32,128,128]{1,2,0:T(8,128)(2,1)}, u32[]{:S(2)}) copy-start(bf16[32,128,128]{1,2,0:T(8,128)(2,1)} %fusion.4) | copy-start | bytes 3145732
  153.5 47.8 %collective-permute-start.5 = (bf16[32,128,128]{1,2,0:T(8,128)(2,1)S(1)}, bf16[32,128,128]{1,2,0:T(8,128)(2,1)}, u32[]{:S(2)}, u32[]{:S(2)}) collective-permute-start(bf16[32,128,128]{1,2,0:T(8,128)(2,1)S(1)} %copy-done.2), channel_id=1, source_target_pairs={{0,1},{1,0},{2,3},{3,2},{4,5},{5,4},{6,7},{7,6},{8,9},{9,8},{10,11... | collective-permute-start | bytes 3145736 | tf_op jit(solution)/shard_map/ppermute | solution.py:18
  158.1 43.2 %collective-permute-start.6 = (bf16[31,128,128]{1,2,0:T(8,128)(2,1)}, bf16[31,128,128]{1,2,0:T(8,128)(2,1)}, u32[]{:S(2)}, u32[]{:S(2)}) collective-permute-start(bf16[31,128,128]{1,2,0:T(8,128)(2,1)} %fusion.5), channel_id=1, source_target_pairs={{0,1},{1,0},{2,3},{3,2},{4,5},{5,4},{6,7},{7,6},{8,9},{9,8},{10,11... | collective-permute-start | bytes 3047432 | tf_op jit(solution)/shard_map/ppermute | solution.py:18
Sparse Core Ops, SparseCore 0:
  51.4 53.4 all-gather.1

commit v10 on v8

--- a/solution.py
+++ b/solution.py
@@ -83,18 +83,9 @@
         picked = jnp.swapaxes(dense[cols_q, rows_q], 1, 2)
         return jnp.where(usable_q[:, None, None], picked, jnp.zeros_like(picked))
 
-    own_dense = partial_of(own_hidden, cot_all[:2])
-    own_sent = blocks_of(own_dense, sent_q)
-    own_kept = blocks_of(own_dense, kept_q)
-    partner_dense = partial_of(partner_hidden, cot_all[2:])
-
-    def paired_of(own_blocks, table):
-        total = own_blocks.astype(jnp.float32) + blocks_of(partner_dense, table).astype(jnp.float32)
-        return total.astype(jnp.bfloat16)
-
-    outgoing = paired_of(own_sent, sent_q)
-    received = from_partner(outgoing, "mirror", 0)
-    kept = paired_of(own_kept, kept_q)
+    dense = partial_of(jnp.concatenate([own_hidden, partner_hidden]), cot_all)
+    received = from_partner(blocks_of(dense, sent_q), "mirror", 0)
+    kept = blocks_of(dense, kept_q)
     summed = (kept.astype(jnp.float32) + received.astype(jnp.float32)).astype(jnp.bfloat16)
     return summed.reshape(1, 1, -1, block_side, block_side)
 

time: 208 us -> 192 us (0.923)
  local copies, waits for them, and re-layouts: 40.5 us -> 21 us
  waiting for transfers between devices: 87.7 us -> 100 us
  matrix products: 19.4 us -> 13.2 us
  other arithmetic: 11.1 us -> 7.62 us
    gather x4 -> x2, local copies, waits for them, and re-layouts: 28.7 us -> 12.5 us  [blocks_of(): picked = jnp.swapaxes(dense[cols_q, rows_q], 1, 2)]
    all_gather x1, waiting for transfers between devices: 51 us -> 60.7 us  [body(): cot_all = lax.all_gather(arrived_all, 'tp', axis=2, tiled=True)]
    ppermute x2, waiting for transfers between devices: 31 us -> 38.6 us  [from_partner(): return lax.ppermute(value, axis, pairs)]
    dot_general x2 -> x1, matrix products: 19.4 us -> 13.2 us  [partial_of(): jnp.einsum('njd,nic->jidc', cot_rows.reshape(-1, db, block_side), hidden_...]
    ppermute x4, waiting for transfers between devices: 5.59 us -> 0.94 us  [passed_along(): return lax.ppermute(block, axis, route)]
    reshape x2 -> x1, local copies, waits for them, and re-layouts: 4.07 us -> 0.01 us  [the longest x1 4.06 us: body(): return summed.reshape(1, 1, -1, block_side, block_side)]
    convert_element_type x1 -> x0, other arithmetic: 3.97 us -> none  [paired_of(): return total.astype(jnp.bfloat16)]
    slice x2 -> x1, local copies, waits for them, and re-layouts: 2.78 us -> 0.07 us  [the longest x1 2.71 us: body(): own_dense = partial_of(own_hidden, cot_all[:2])]
  transfers between devices with their start and end apart: 7 -> 7, of which waited for: 3 -> 3; matrix products, arithmetic and copies ran while one was open for 18% -> 8% of each run, Pallas kernels for 0% -> 0%
where the time goes in v10:
time: 192 us; the launch traced here: 191 us
  waiting for transfers between devices  100 us (52%)
  starting transfers between devices  35.5 us (18%)
  local copies, waits for them, and re-layouts  21 us (11%)
  between operations  13.6 us (7%)
  matrix products  13.2 us (7%)
  other arithmetic  7.62 us (4%)
    all_gather x1, waiting for transfers between devices, body(): cot_all = lax.all_gather(arrived_all, 'tp', axis=2, tiled=True)  60.7 us
    ppermute x2, waiting for transfers between devices, from_partner(): return lax.ppermute(value, axis, pairs)  38.6 us
    ppermute x4, starting transfers between devices, passed_along(): return lax.ppermute(block, axis, route)  26.6 us
    dot_general x1, matrix products, partial_of(): jnp.einsum('njd,nic->jidc', cot_rows.reshape(-1, db, block_side), hidden_...  13.2 us
    gather x2, local copies, waits for them, and re-layouts, blocks_of(): picked = jnp.swapaxes(dense[cols_q, rows_q], 1, 2)  12.5 us
    ppermute x2, starting transfers between devices, from_partner(): return lax.ppermute(value, axis, pairs)  8.91 us
    reshape x1, other arithmetic, body(): return summed.reshape(1, 1, -1, block_side, block_side)  3.92 us
  transfers between devices with their start and end apart: 7, of which 3 were waited for; matrix products, arithmetic and copies ran while one was open for 8% of the time, Pallas kernels for 0%

profile of v10, /device:TPU:1, one launch (start us, length us, event | category | flops | bytes accessed | tf_op | source)
XLA Modules:
  0.0 191.2 jit_solution(5522661037765055658)
XLA Ops:
  6.5 0.0 copy-start
  6.5 0.0 copy-start.1
  6.5 0.0 all-gather.2.cloned.1.call-start
  6.5 1.1 slice_bitcast_fusion.1
  7.6 11.2 %collective-permute-start.4 = (bf16[128,512]{1,0:T(8,128)(2,1)S(1)}, bf16[128,512]{1,0:T(8,128)(2,1)S(1)}, u32[]{:S(2)}, u32[]{:S(2)}) collective-permute-start(bf16[128,512]{1,0:T(8,128)(2,1)S(1)} %get-tuple-element.6), channel_id=1, source_target_pairs={{496,0},{512,16},{528,32},{544,48},{560,64},{576,80},{592,96},{608... | collective-permute-start | bytes 393224 | tf_op jit(solution)/shard_map/ppermute | solution.py:12
  18.9 1.9 %collective-permute-start.3 = (bf16[128,512]{1,0:T(8,128)(2,1)S(1)}, bf16[128,512]{1,0:T(8,128)(2,1)S(1)}, u32[]{:S(2)}, u32[]{:S(2)}) collective-permute-start(bf16[128,512]{1,0:T(8,128)(2,1)S(1)} %get-tuple-element.5), channel_id=1, source_target_pairs={{528,0},{544,16},{560,32},{576,48},{592,64},{608,80},{624,96},{640... | collective-permute-start | bytes 393224 | tf_op jit(solution)/shard_map/ppermute | solution.py:12
  20.8 3.5 %collective-permute-start.2 = (bf16[128,512]{1,0:T(8,128)(2,1)S(1)}, bf16[128,512]{1,0:T(8,128)(2,1)S(1)}, u32[]{:S(2)}, u32[]{:S(2)}) collective-permute-start(bf16[128,512]{1,0:T(8,128)(2,1)S(1)} %get-tuple-element.6), channel_id=1, source_target_pairs={{1008,0},{0,16},{16,32},{32,48},{48,64},{64,80},{80,96},{96,112},{... | collective-permute-start | bytes 393224 | tf_op jit(solution)/shard_map/ppermute | solution.py:12
  24.3 9.9 %collective-permute-start.1 = (bf16[128,512]{1,0:T(8,128)(2,1)S(1)}, bf16[128,512]{1,0:T(8,128)(2,1)S(1)}, u32[]{:S(2)}, u32[]{:S(2)}) collective-permute-start(bf16[128,512]{1,0:T(8,128)(2,1)S(1)} %get-tuple-element.5), channel_id=1, source_target_pairs={{16,0},{32,16},{48,32},{64,48},{80,64},{96,80},{112,96},{128,112},... | collective-permute-start | bytes 393224 | tf_op jit(solution)/shard_map/ppermute | solution.py:12
  34.2 0.0 collective-permute-done.4
  34.2 0.0 collective-permute-done.3
  34.2 0.0 collective-permute-done.2
  34.2 0.9 collective-permute-done.1
  35.2 0.9 pad_maximum_fusion
  36.0 0.0 all-gather.2.cloned.1.call-update
  36.1 0.0 copy-done.1
  36.1 0.5 copy.10
  36.6 5.8 %collective-permute-start = (bf16[256,1792]{0,1:T(8,128)(2,1)S(1)}, bf16[256,1792]{0,1:T(8,128)(2,1)}, u32[]{:S(2)}, u32[]{:S(2)}) collective-permute-start(bf16[256,1792]{0,1:T(8,128)(2,1)S(1)} %copy.10), channel_id=1, source_target_pairs={{0,512},{16,528},{32,544},{48,560},{64,576},{80,592},{96,608},{112... | collective-permute-start | bytes 2752520 | tf_op jit(solution)/shard_map/ppermute | solution.py:18
  42.5 0.0 copy-done
  42.5 0.1 reshape.31
  42.6 0.3 reduce-window.9
  42.9 0.1 slice.22
  43.0 0.1 slice_reduce_fusion
  43.1 0.7 reshape.74
  43.9 1.6 copy.13
  45.5 0.1 add_bitcast_fusion
  45.6 0.6 slice.24
  46.2 0.7 iota_compare_fusion.1
  46.9 0.1 fusion.17
  47.0 0.1 convert_reduce_fusion
  47.1 0.1 fusion.8
  47.2 60.7 %all-gather.2.cloned.1.call-done = bf16[4,128,4096]{2,1,0:T(8,128)(2,1)} async-done(((bf16[4,128,512]{2,1,0:T(8,128)(2,1)}), bf16[4,128,4096]{2,1,0:T(8,128)(2,1)}) %all-gather.2.cloned.1.call-update) | async-done | bytes 4194320 | tf_op jit(solution)/shard_map/all_gather | solution.py:53
  108.0 0.0 copy-start.2
  108.0 3.5 %copy.14 = bf16[64,8,32,128]{3,2,1,0:T(8,128)(2,1)S(1)} copy(bf16[64,8,32,128]{3,1,2,0:T(8,128)(2,1)} %bitcast.41) | data formatting | bytes 8388608
  111.5 0.0 collective-permute-done
  111.5 0.0 copy-done.2
  111.5 13.2 %convert_bitcast_fusion = bf16[32,14,128,128]{2,3,0,1:T(8,128)(2,1)} fusion(bf16[512,32,128]{2,1,0:T(8,128)(2,1)S(1)} %bitcast.42, bf16[256,14,128]{0,2,1:T(8,128)(2,1)} %bitcast.4, bf16[256,14,128]{0,2,1:T(8,128)(2,1)S(1)} %copy-done.2), kind=kOutput, calls=%fused_computation.2 | convolution fusion | flops 7527202816 | bytes 20709376 | tf_op jit(solution)/shard_map/njd,nic->jidc/dot_general | solution.py:74
  124.7 6.2 %gather_fusion.1 = bf16[63,128,128]{1,2,0:T(8,128)(2,1)S(1)} fusion(bf16[32,14,128,128]{2,3,0,1:T(8,128)(2,1)} %convert_bitcast_fusion, s32[63]{0:T(128)S(1)} %get-tuple-element.8), kind=kCustom, calls=%fused_computation.1 | custom fusion | bytes 4129272 | tf_op jit(solution)/shard_map/gather | solution.py:83
  131.0 1.5 select_bitcast_fusion
  132.5 3.1 %collective-permute-start.5 = (bf16[63,128,128]{2,1,0:T(8,128)(2,1)}, bf16[63,128,128]{2,1,0:T(8,128)(2,1)}, u32[]{:S(2)}, u32[]{:S(2)}) collective-permute-start(bf16[63,128,128]{2,1,0:T(8,128)(2,1)} %select_bitcast_fusion), channel_id=1, source_target_pairs={{0,1},{1,0},{2,3},{3,2},{4,5},{5,4},{6,7},{7,6},{8,9},{9,8},{10,11... | collective-permute-start | bytes 6193160 | tf_op jit(solution)/shard_map/ppermute | solution.py:18
  135.6 6.3 %gather_fusion = bf16[63,128,128]{1,2,0:T(8,128)(2,1)S(1)} fusion(bf16[32,14,128,128]{2,3,0,1:T(8,128)(2,1)} %convert_bitcast_fusion, s32[63]{0:T(128)S(1)} %get-tuple-element.7), kind=kCustom, calls=%fused_computation | custom fusion | bytes 4129272 | tf_op jit(solution)/shard_map/gather | solution.py:83
  141.8 38.6 %collective-permute-done.5 = bf16[63,128,128]{2,1,0:T(8,128)(2,1)} collective-permute-done((bf16[63,128,128]{2,1,0:T(8,128)(2,1)}, bf16[63,128,128]{2,1,0:T(8,128)(2,1)}, u32[]{:S(2)}, u32[]{:S(2)}) %collective-permute-start.5) | collective-permute-done | bytes 2064416 | tf_op jit(solution)/shard_map/ppermute | solution.py:18
  180.5 3.9 %fusion.3 = bf16[1,1,63,128,128]{4,3,2,1,0:T(8,128)(2,1)} fusion(bf16[63,128,128]{2,1,0:T(8,128)(2,1)} %collective-permute-done.5, bf16[63,128,128]{1,2,0:T(8,128)(2,1)S(1)} %gather_fusion, pred[63]{0:T(512)(128)(4,1)S(1)} %get-tuple-element.11), kind=kLoop, calls=%fused_computation.7 | loop fusion | flops 5160960 | bytes 6193215 | tf_op jit(solution)/shard_map/reshape | solution.py:90
  (4 shorter events, 0.1 us)
Async XLA Ops:
  6.5 35.9 %copy-start = (s32[32,14,32]{2,0,1:T(8,128)S(1)}, s32[32,14,32]{2,0,1:T(8,128)}, u32[]{:S(2)}) copy-start(s32[32,14,32]{2,0,1:T(8,128)} %param.5) | copy-start | bytes 172036
  6.5 29.5 %copy-start.1 = (bf16[2,1,1,128,1792]{4,3,2,1,0:T(8,128)(2,1)S(1)}, bf16[2,1,1,128,1792]{4,3,2,1,0:T(8,128)(2,1)}, u32[]{:S(2)}) copy-start(bf16[2,1,1,128,1792]{4,3,2,1,0:T(8,128)(2,1)} %param.3) | copy-start | bytes 2752516
  6.5 101.4 %all-gather.2.cloned.1.call-start = ((), (), s32[]{:S(2)}) async-start(), calls=%async_computation | async-start | bytes 4718592 | tf_op jit(solution)/shard_map/all_gather | solution.py:53
  7.6 26.6 %collective-permute-start.4 = (bf16[128,512]{1,0:T(8,128)(2,1)S(1)}, bf16[128,512]{1,0:T(8,128)(2,1)S(1)}, u32[]{:S(2)}, u32[]{:S(2)}) collective-permute-start(bf16[128,512]{1,0:T(8,128)(2,1)S(1)} %get-tuple-element.6), channel_id=1, source_target_pairs={{496,0},{512,16},{528,32},{544,48},{560,64},{576,80},{592,96},{608... | collective-permute-start | bytes 393224 | tf_op jit(solution)/shard_map/ppermute | solution.py:12
  18.9 15.4 %collective-permute-start.3 = (bf16[128,512]{1,0:T(8,128)(2,1)S(1)}, bf16[128,512]{1,0:T(8,128)(2,1)S(1)}, u32[]{:S(2)}, u32[]{:S(2)}) collective-permute-start(bf16[128,512]{1,0:T(8,128)(2,1)S(1)} %get-tuple-element.5), channel_id=1, source_target_pairs={{528,0},{544,16},{560,32},{576,48},{592,64},{608,80},{624,96},{640... | collective-permute-start | bytes 393224 | tf_op jit(solution)/shard_map/ppermute | solution.py:12
  20.8 13.5 %collective-permute-start.2 = (bf16[128,512]{1,0:T(8,128)(2,1)S(1)}, bf16[128,512]{1,0:T(8,128)(2,1)S(1)}, u32[]{:S(2)}, u32[]{:S(2)}) collective-permute-start(bf16[128,512]{1,0:T(8,128)(2,1)S(1)} %get-tuple-element.6), channel_id=1, source_target_pairs={{1008,0},{0,16},{16,32},{32,48},{48,64},{64,80},{80,96},{96,112},{... | collective-permute-start | bytes 393224 | tf_op jit(solution)/shard_map/ppermute | solution.py:12
  24.3 10.9 %collective-permute-start.1 = (bf16[128,512]{1,0:T(8,128)(2,1)S(1)}, bf16[128,512]{1,0:T(8,128)(2,1)S(1)}, u32[]{:S(2)}, u32[]{:S(2)}) collective-permute-start(bf16[128,512]{1,0:T(8,128)(2,1)S(1)} %get-tuple-element.5), channel_id=1, source_target_pairs={{16,0},{32,16},{48,32},{64,48},{80,64},{96,80},{112,96},{128,112},... | collective-permute-start | bytes 393224 | tf_op jit(solution)/shard_map/ppermute | solution.py:12
  36.6 74.9 %collective-permute-start = (bf16[256,1792]{0,1:T(8,128)(2,1)S(1)}, bf16[256,1792]{0,1:T(8,128)(2,1)}, u32[]{:S(2)}, u32[]{:S(2)}) collective-permute-start(bf16[256,1792]{0,1:T(8,128)(2,1)S(1)} %copy.10), channel_id=1, source_target_pairs={{0,512},{16,528},{32,544},{48,560},{64,576},{80,592},{96,608},{112... | collective-permute-start | bytes 2752520 | tf_op jit(solution)/shard_map/ppermute | solution.py:18
  108.0 3.5 %copy-start.2 = (bf16[256,14,128]{0,2,1:T(8,128)(2,1)S(1)}, bf16[256,14,128]{0,2,1:T(8,128)(2,1)}, u32[]{:S(2)}) copy-start(bf16[256,14,128]{0,2,1:T(8,128)(2,1)} %copy.13) | copy-start | bytes 2752516
  132.5 48.0 %collective-permute-start.5 = (bf16[63,128,128]{2,1,0:T(8,128)(2,1)}, bf16[63,128,128]{2,1,0:T(8,128)(2,1)}, u32[]{:S(2)}, u32[]{:S(2)}) collective-permute-start(bf16[63,128,128]{2,1,0:T(8,128)(2,1)} %select_bitcast_fusion), channel_id=1, source_target_pairs={{0,1},{1,0},{2,3},{3,2},{4,5},{5,4},{6,7},{7,6},{8,9},{9,8},{10,11... | collective-permute-start | bytes 6193160 | tf_op jit(solution)/shard_map/ppermute | solution.py:18
Sparse Core Ops, SparseCore 0:
  36.2 71.7 all-gather.1
